TPU v7x, 512 devices: a whole 4x8x8 slice. The times are simulated.
512 devices in a mesh: pipe: 8 (over z), space: 64 (over x, y, core).
Axes of the slice: x: 4, y: 8, z: 8, core: 2. Of those that a mesh axis runs over, the one named last changes fastest.
Arguments:
- activations: bfloat16 [8, 2, 96, 256, 512], P('pipe', None, None, 'space'), may hold values from -6 to 6
- cotangent: bfloat16 [8, 2, 96, 256, 512], P('pipe', None, None, 'space'), may hold values from -6 to 6
- kept_modes: int32 [8, 2], P('pipe'), may hold values from 32 to 128, as said below
- weight_in: float32 [8, 2, 2, 96, 96], P('pipe'), may hold values from -0.4375 to 0.4375
- bias_in: float32 [8, 2, 2, 96], P('pipe'), may hold values from -4 to 4
- weight_out: float32 [8, 2, 2, 96, 96], P('pipe'), may hold values from -0.4375 to 0.4375
Outputs:
- grad_input: bfloat16 [8, 2, 96, 256, 512], P('pipe', None, None, 'space')
- grad_weight_in: float32 [8, 2, 2, 96, 96], P('pipe')
- grad_bias_in: float32 [8, 2, 2, 96], P('pipe')
- grad_weight_out: float32 [8, 2, 2, 96, 96], P('pipe')
- grad_bias_out: float32 [8, 2, 2, 96], P('pipe')
Inputs may be any that keep to these rules, and one draw needn't show every extreme that they name: `kept_modes`: column 0 is a layer's kept longitude wavenumbers, from 64 to 128, with exactly 128 in some layer; column 1 is the kept latitude wavenumbers of each sign, from 32 to 64, with exactly 64 in some layer.
All inputs are finite; a program needn't handle non-finite values.
Results may differ from a plain program's by a relative error of at most 0.001.
Values may be sent and summed in bfloat16 or wider, within the bound.
No kernel may reach another device: no remote copies, remote signals or barrier semaphores. Data moves between devices by JAX's collectives and lax.ppermute only.
A program may use at most 64 MiB of HBM per device.

v0:
```python
import math

import jax
import jax.numpy as jnp
from jax import lax
from jax.sharding import PartitionSpec as P

LAT = 256
LON = 512
KEEP_LON = 128
KEEP_LAT = 64


HIGHEST = lax.Precision.HIGHEST


def from_behind(block, axis, distance):
    devices = range(lax.axis_size(axis))
    route = [(i - distance, i) for i in devices if i - distance in devices]
    return lax.ppermute(block, axis, route)


def lon_tables(length, count):
    column = jnp.arange(length, dtype=jnp.int32)
    number = jnp.arange(count, dtype=jnp.int32)
    phase = column[:, None] * number[None, :] % length
    angle = phase.astype(jnp.float32) * (2.0 * math.pi / length)
    factor = 1.0 / math.sqrt(length)
    return (jnp.cos(angle) * factor, jnp.sin(angle) * factor)


def lat_tables(length, half):
    signed = jnp.arange(2 * half, dtype=jnp.int32) - half
    row_index = jnp.arange(length, dtype=jnp.int32)
    phase = signed[:, None] * row_index[None, :] % length
    angle = phase.astype(jnp.float32) * (2.0 * math.pi / length)
    factor = 1.0 / math.sqrt(length)
    return (jnp.cos(angle) * factor, jnp.sin(angle) * factor)


def lat_columns(field, cos_table, sin_table):
    values = field.astype(jnp.float32)
    real_part = jnp.einsum("fl,ibln->ibfn", cos_table, values, precision=HIGHEST)
    imag_part = -jnp.einsum("fl,ibln->ibfn", sin_table, values, precision=HIGHEST)
    return jnp.stack([real_part, imag_part])


def lon_complex(spectrum, cos_table, sin_table):

    def apply(values, table):
        return jnp.einsum("ibfn,nk->ibfk", values, table, precision=HIGHEST)

    real_part = apply(spectrum[0], cos_table) + apply(spectrum[1], sin_table)
    imag_part = apply(spectrum[1], cos_table) - apply(spectrum[0], sin_table)
    return jnp.stack([real_part, imag_part])


def lon_complex_inverse(spectrum, cos_table, sin_table):

    def apply(values, table):
        return jnp.einsum("ibfk,nk->ibfn", values, table, precision=HIGHEST)

    real_part = apply(spectrum[0], cos_table) - apply(spectrum[1], sin_table)
    imag_part = apply(spectrum[1], cos_table) + apply(spectrum[0], sin_table)
    return jnp.stack([real_part, imag_part])


def lat_real_inverse(spectrum, cos_table, sin_table):
    first = jnp.einsum("fl,ibfn->ibln", cos_table, spectrum[0], precision=HIGHEST)
    second = jnp.einsum("fl,ibfn->ibln", sin_table, spectrum[1], precision=HIGHEST)
    return first - second


def mode_mask(signed, wavenumber, keep_lon, keep_lat):
    lat_kept = (signed >= -keep_lat) & (signed < keep_lat)
    lon_kept = wavenumber < keep_lon
    factor = jnp.where(wavenumber == 0, 1.0, 2.0).astype(jnp.float32)
    return (lat_kept[:, None] & lon_kept[None, :]).astype(jnp.float32) * factor[None, :]


def block_product(weights, values):
    return jnp.einsum("kij,kjm->kim", weights, values, precision=HIGHEST)


def complex_apply(weights, values):
    real_part = block_product(weights[0], values[0]) - block_product(weights[1], values[1])
    imag_part = block_product(weights[1], values[0]) + block_product(weights[0], values[1])
    return jnp.stack([real_part, imag_part])


def complex_adjoint(weights, values):
    real_t = jnp.swapaxes(weights[0], 1, 2)
    imag_t = jnp.swapaxes(weights[1], 1, 2)
    real_part = block_product(real_t, values[0]) + block_product(imag_t, values[1])
    imag_part = block_product(real_t, values[1]) - block_product(imag_t, values[0])
    return jnp.stack([real_part, imag_part])


def complex_outer(left, right):

    def outer(first, second):
        return jnp.einsum("kim,kjm->kij", first, second, precision=HIGHEST)

    real_part = outer(left[0], right[0]) + outer(left[1], right[1])
    imag_part = outer(left[1], right[0]) - outer(left[0], right[1])
    return jnp.stack([real_part, imag_part])


def gelu_pair(values):
    inner = 0.7978845608 * (values + 0.044715 * values * values * values)
    tangent = jnp.tanh(inner)
    output = 0.5 * values * (1.0 + tangent)
    slope = 0.5 * (1.0 + tangent) + 0.5 * values * (1.0 - tangent * tangent) * 0.7978845608 * (
        1.0 + 3.0 * 0.044715 * values * values
    )
    return (output, slope)


def backprop(spectrum, grad_spec, weight_in, bias_in, weight_out):
    before = complex_apply(weight_in, spectrum) + bias_in[..., None]
    hidden, slope = gelu_pair(before)
    grad_hidden = complex_adjoint(weight_out, grad_spec)
    grad_before = grad_hidden * slope
    grad_modes = complex_adjoint(weight_in, grad_before)
    grad_w_out = complex_outer(grad_spec, hidden)
    grad_w_in = complex_outer(grad_before, spectrum)
    return (
        grad_modes,
        grad_w_in,
        jnp.sum(grad_before, axis=-1),
        grad_w_out,
        jnp.sum(grad_spec, axis=-1),
    )


def shards(activations, cotangent, kept_modes, weight_in, bias_in, weight_out):
    field = activations[0]
    own_grad = cotangent[0]
    nblocks = field.shape[0]
    width = field.shape[1]
    received = from_behind(own_grad, "pipe", -1)
    section_index = lax.axis_index("pipe")
    last_section = lax.axis_size("pipe") - 1
    upstream = jnp.where(section_index == last_section, own_grad, received)
    lon_cos, lon_sin = lon_tables(LON, KEEP_LON)
    lat_cos, lat_sin = lat_tables(LAT, KEEP_LAT)
    col_field, col_grad = (
        lax.all_to_all(field, "space", split_axis=3, concat_axis=2, tiled=True),
        lax.all_to_all(upstream, "space", split_axis=3, concat_axis=2, tiled=True),
    )
    lat_field = lat_columns(col_field, lat_cos, lat_sin)
    lat_grad = lat_columns(col_grad, lat_cos, lat_sin)
    part_field, part_grad = (
        lax.all_to_all(lat_field, "space", split_axis=3, concat_axis=4, tiled=True),
        lax.all_to_all(lat_grad, "space", split_axis=3, concat_axis=4, tiled=True),
    )
    share = 2 * KEEP_LAT // lax.axis_size("space")
    signed = lax.axis_index("space") * share + jnp.arange(share, dtype=jnp.int32) - KEEP_LAT
    wavenumber = jnp.arange(KEEP_LON, dtype=jnp.int32)
    weight = mode_mask(signed, wavenumber, kept_modes[0, 0], kept_modes[0, 1])
    spectrum = lon_complex(part_field, lon_cos, lon_sin).reshape(2, nblocks, width, -1)
    grad_spec = (lon_complex(part_grad, lon_cos, lon_sin) * weight).reshape(2, nblocks, width, -1)
    grad_modes, grad_w_in, grad_b_in, grad_w_out, grad_b_out = backprop(
        spectrum, grad_spec, weight_in[0], bias_in[0], weight_out[0]
    )
    grad_modes = grad_modes.reshape(2, nblocks, width, share, KEEP_LON)
    lon_back = lon_complex_inverse(grad_modes, lon_cos, lon_sin)
    lat_parts = lax.all_to_all(lon_back, "space", split_axis=4, concat_axis=3, tiled=True)
    cols_back = lat_real_inverse(lat_parts, lat_cos, lat_sin)
    inverse = lax.all_to_all(cols_back, "space", split_axis=2, concat_axis=3, tiled=True)
    sum_w_in, sum_b_in, sum_w_out, sum_b_out = lax.psum(
        (grad_w_in, grad_b_in, grad_w_out, grad_b_out), "space"
    )
    factor = 1.0 / math.sqrt(2 * KEEP_LAT * KEEP_LON)
    grad_field = (upstream.astype(jnp.float32) + inverse).astype(jnp.bfloat16)
    return (
        grad_field[None],
        (sum_w_in * factor)[None],
        (sum_b_in * factor)[None],
        (sum_w_out * factor)[None],
        (sum_b_out * factor)[None],
    )


def solution(mesh):
    return jax.shard_map(
        shards,
        mesh=mesh,
        in_specs=(
            P("pipe", None, None, "space", None),
            P("pipe", None, None, "space", None),
            P("pipe", None),
            P("pipe", None, None, None, None),
            P("pipe", None, None, None),
            P("pipe", None, None, None, None),
        ),
        out_specs=(
            P("pipe", None, None, "space", None),
            P("pipe", None, None, None, None),
            P("pipe", None, None, None),
            P("pipe", None, None, None, None),
            P("pipe", None, None, None),
        ),
        check_vma=False,
    )
```

profile of v0, /device:TPU:1, one launch (start us, length us, event | category | flops | bytes accessed | tf_op | source)
XLA Modules:
  0.0 537.6 jit_solution(9131577581886441805)
XLA Ops:
  7.2 3.9 copy.151
  11.0 11.8 %all-to-all-start.2 = ((bf16[2,96,4,512]{1,2,0,3:T(4,128)(2,1)}), bf16[2,96,4,512]{1,2,0,3:T(4,128)(2,1)}, u32[]{:S(2)}, u32[]{:S(2)}) async-start(bf16[2,96,4,512]{1,2,0,3:T(4,128)(2,1)} %bitcast.35), calls=%async_computation.2 | async-start | bytes 2097152 | tf_op jit(solution)/shard_map/all_to_all | solution.py:148
  25.2 19.4 %collective-permute-done = bf16[2,96,4,512]{3,1,2,0:T(8,128)(2,1)} collective-permute-done((bf16[2,96,4,512]{3,1,2,0:T(8,128)(2,1)S(1)}, bf16[2,96,4,512]{3,1,2,0:T(8,128)(2,1)}, u32[]{:S(2)}, u32[]{:S(2)}) %collective-permute-start) | collective-permute-done | bytes 786464 | tf_op jit(solution)/shard_map/ppermute | solution.py:20
  44.5 1.6 copy.133
  46.2 1.8 copy.134
  48.0 3.3 all-to-all-done.2
  51.3 7.9 %all-to-all-start = ((bf16[2,96,4,512]{1,2,0,3:T(4,128)(2,1)}), bf16[2,96,4,512]{1,2,0,3:T(4,128)(2,1)}, u32[]{:S(2)}, u32[]{:S(2)}) async-start(bf16[2,96,4,512]{1,2,0,3:T(4,128)(2,1)} %copy.134), calls=%async_computation | async-start | bytes 2097152 | tf_op jit(solution)/shard_map/all_to_all | solution.py:149
  59.3 1.4 copy.298
  64.4 2.0 copy.156
  66.4 21.4 %all-to-all-done = bf16[2,96,4,512]{1,2,0,3:T(4,128)(2,1)} async-done(((bf16[2,96,4,512]{1,2,0,3:T(4,128)(2,1)}), bf16[2,96,4,512]{1,2,0,3:T(4,128)(2,1)}, u32[]{:S(2)}, u32[]{:S(2)}) %all-to-all-start) | async-done | bytes 786464 | tf_op jit(solution)/shard_map/all_to_all | solution.py:149
  87.7 6.6 %all-to-all-start.3 = ((f32[2,2,96,128,8]{2,4,1,0,3:T(8,128)}), f32[2,2,96,128,8]{2,4,1,0,3:T(8,128)S(1)}, u32[]{:S(2)}, u32[]{:S(2)}) async-start(f32[2,2,96,128,8]{2,4,1,0,3:T(8,128)} %copy.156), calls=%async_computation.3 | async-start | bytes 4194304 | tf_op jit(solution)/shard_map/all_to_all | solution.py:154
  94.3 1.4 copy.299
  96.8 2.8 copy.137
  99.7 2.5 convolution_bitcast_fusion.1
  102.2 2.5 fusion.2
  105.9 3.0 copy.139
  108.9 36.5 %all-to-all-done.3 = f32[2,2,96,128,8]{2,4,1,0,3:T(8,128)S(1)} async-done(((f32[2,2,96,128,8]{2,4,1,0,3:T(8,128)}), f32[2,2,96,128,8]{2,4,1,0,3:T(8,128)S(1)}, u32[]{:S(2)}, u32[]{:S(2)}) %all-to-all-start.3) | async-done | bytes 1572896 | tf_op jit(solution)/shard_map/all_to_all | solution.py:154
  146.8 5.8 %all-to-all-start.1 = ((f32[2,2,96,128,8]{2,4,1,0,3:T(8,128)}), f32[2,2,96,128,8]{2,4,1,0,3:T(8,128)S(1)}, u32[]{:S(2)}, u32[]{:S(2)}) async-start(f32[2,2,96,128,8]{2,4,1,0,3:T(8,128)} %copy.139), calls=%async_computation.1 | async-start | bytes 4194304 | tf_op jit(solution)/shard_map/all_to_all | solution.py:155
  155.3 1.7 copy.157
  157.2 2.6 fusion.18
  159.8 2.6 fusion.11
  162.4 2.6 fusion.22
  164.9 2.6 fusion.12
  169.6 34.3 %all-to-all-done.1 = f32[2,2,96,128,8]{2,4,1,0,3:T(8,128)S(1)} async-done(((f32[2,2,96,128,8]{2,4,1,0,3:T(8,128)}), f32[2,2,96,128,8]{2,4,1,0,3:T(8,128)S(1)}, u32[]{:S(2)}, u32[]{:S(2)}) %all-to-all-start.1) | async-done | bytes 1572896 | tf_op jit(solution)/shard_map/all_to_all | solution.py:155
  204.2 11.3 %fusion.28 = f32[2,96,2,128]{3,1,2,0:T(8,128)S(1)} fusion(f32[1,2,96,2,64,8]{2,5,3,4,1,0:T(8,128)S(1)} %get-tuple-element.28), kind=kOutput, calls=%fused_computation.54 | convolution fusion | flops 302972928 | bytes 983040 | tf_op jit(solution)/shard_map/ibfn,nk->ibfk/dot_general | solution.py:51
  215.5 2.6 fusion.24
  218.0 2.6 convolution_add_fusion.5
  220.6 2.6 convolution_subtract_fusion.5
  228.9 1.7 fusion.56
  230.7 1.7 fusion.54
  232.5 1.8 fusion.4
  234.2 1.8 fusion.3
  236.0 1.4 pad_maximum_fusion.2
  237.4 3.1 copy.174
  240.5 57.2 %all_to_all.99 = f32[2,2,96,2,512]{2,3,1,0,4:T(2,128)S(1)} all-to-all(f32[2,2,96,2,512]{2,3,1,0,4:T(2,128)S(1)} %copy.174), channel_id=1, replica_groups=mesh['pipe'=8,'space'=64] {'space'}, dimensions={4} | all-to-all | bytes 3145728 | tf_op jit(solution)/shard_map/all_to_all | solution.py:168
  300.1 1.9 fusion.103
  302.0 1.9 subtract_bitcast_fusion
  304.0 2.0 copy.180
  305.9 5.9 %all-to-all-start.5 = ((f32[2,96,256,8]{1,3,0,2:T(8,128)}), f32[2,96,256,8]{1,3,0,2:T(8,128)S(1)}, u32[]{:S(2)}, u32[]{:S(2)}) async-start(f32[2,96,256,8]{1,3,0,2:T(8,128)} %copy.180), calls=%async_computation.5 | async-start | bytes 4194304 | tf_op jit(solution)/shard_map/all_to_all | solution.py:170
  312.6 1.8 copy.184
  314.4 1.8 copy.183
  316.1 1.8 stack.109
  317.9 1.8 stack.108
  319.7 1.4 fusion.81
  329.1 147.2 %all-reduce = (f32[2,2,96]{2,1,0:T(2,128)S(1)}, f32[2,2,96]{2,1,0:T(2,128)S(1)}) all-reduce(f32[2,2,96]{2,1,0:T(2,128)S(1)} %get-tuple-element.24, f32[2,2,96]{2,1,0:T(2,128)S(1)} %fusion.44), channel_id=1, replica_groups=mesh['pipe'=8,'space'=64] {'space'}, use_global_device_ids=true, to_apply=%region_2.3 | all-reduce | flops 768 | bytes 6144 | tf_op jit(solution)/shard_map/psum | solution.py:171
  476.9 48.0 %all-reduce.4.cloned.1.call-done = (f32[2,2,96,96]{3,2,1,0:T(8,128)}, f32[2,2,96,96]{3,2,1,0:T(8,128)}) async-done(((f32[2,2,96,96]{3,2,1,0:T(8,128)}, f32[2,2,96,96]{3,2,1,0:T(8,128)}), (f32[2,2,96,96]{3,2,1,0:T(8,128)}, f32[2,2,96,96]{3,2,1,0:T(8,128)})) %all-reduce.4.cloned.1.call-update) | async-done | bytes 294928 | tf_op jit(solution)/shard_map/psum | solution.py:171
  524.9 1.8 multiply_bitcast_fusion
  527.9 2.4 copy.185
  (99 shorter events, 32.7 us)
Async XLA Ops:
  7.2 15.7 %copy-start.3 = (bf16[1,2,96,4,512]{4,3,2,1,0:T(4,128)(2,1)S(1)}, bf16[1,2,96,4,512]{4,3,2,1,0:T(4,128)(2,1)}, u32[]{:S(2)}) copy-start(bf16[1,2,96,4,512]{4,3,2,1,0:T(4,128)(2,1)} %param.7) | copy-start | bytes 2359300
  11.0 40.3 %all-to-all-start.2 = ((bf16[2,96,4,512]{1,2,0,3:T(4,128)(2,1)}), bf16[2,96,4,512]{1,2,0,3:T(4,128)(2,1)}, u32[]{:S(2)}, u32[]{:S(2)}) async-start(bf16[2,96,4,512]{1,2,0,3:T(4,128)(2,1)} %bitcast.35), calls=%async_computation.2 | async-start | bytes 2097152 | tf_op jit(solution)/shard_map/all_to_all | solution.py:148
  23.0 21.5 %collective-permute-start = (bf16[2,96,4,512]{3,1,2,0:T(8,128)(2,1)S(1)}, bf16[2,96,4,512]{3,1,2,0:T(8,128)(2,1)}, u32[]{:S(2)}, u32[]{:S(2)}) collective-permute-start(bf16[2,96,4,512]{3,1,2,0:T(8,128)(2,1)S(1)} %bitcast.291), channel_id=1, source_target_pairs={{64,0},{128,64},{192,128},{256,192},{320,256},{384,320},{448,384},... | collective-permute-start | bytes 2359304 | tf_op jit(solution)/shard_map/ppermute | solution.py:20
  51.3 36.4 %all-to-all-start = ((bf16[2,96,4,512]{1,2,0,3:T(4,128)(2,1)}), bf16[2,96,4,512]{1,2,0,3:T(4,128)(2,1)}, u32[]{:S(2)}, u32[]{:S(2)}) async-start(bf16[2,96,4,512]{1,2,0,3:T(4,128)(2,1)} %copy.134), calls=%async_computation | async-start | bytes 2097152 | tf_op jit(solution)/shard_map/all_to_all | solution.py:149
  87.7 57.7 %all-to-all-start.3 = ((f32[2,2,96,128,8]{2,4,1,0,3:T(8,128)}), f32[2,2,96,128,8]{2,4,1,0,3:T(8,128)S(1)}, u32[]{:S(2)}, u32[]{:S(2)}) async-start(f32[2,2,96,128,8]{2,4,1,0,3:T(8,128)} %copy.156), calls=%async_computation.3 | async-start | bytes 4194304 | tf_op jit(solution)/shard_map/all_to_all | solution.py:154
  108.9 43.7 %copy-start.18 = (s32[1,2]{1,0:T(1,128)S(1)}, s32[1,2]{1,0:T(1,128)}, u32[]{:S(2)}) copy-start(s32[1,2]{1,0:T(1,128)} %param.8) | copy-start | bytes 28
  145.5 1.4 copy-start
  146.8 57.0 %all-to-all-start.1 = ((f32[2,2,96,128,8]{2,4,1,0,3:T(8,128)}), f32[2,2,96,128,8]{2,4,1,0,3:T(8,128)S(1)}, u32[]{:S(2)}, u32[]{:S(2)}) async-start(f32[2,2,96,128,8]{2,4,1,0,3:T(8,128)} %copy.139), calls=%async_computation.1 | async-start | bytes 4194304 | tf_op jit(solution)/shard_map/all_to_all | solution.py:155
  153.9 3.1 copy-start.15
  154.6 2.5 copy-start.17
  159.8 7.8 %copy-start.9 = (f32[1,2,2,96,96]{4,3,2,1,0:T(8,128)S(1)}, f32[1,2,2,96,96]{4,3,2,1,0:T(8,128)}, u32[]{:S(2)}) copy-start(f32[1,2,2,96,96]{4,3,2,1,0:T(8,128)} %param.9) | copy-start | bytes 442372
  162.4 6.2 %copy-start.5 = (f32[2,2,12,8,128]{4,3,2,1,0:T(8,128)}, f32[2,2,12,8,128]{4,3,2,1,0:T(8,128)S(1)}, u32[]{:S(2)}) copy-start(f32[2,2,12,8,128]{4,3,2,1,0:T(8,128)S(1)} %fusion.11) | copy-start | bytes 589828
  167.5 1.0 copy-start.7
  220.6 2.7 copy-start.11
  220.6 3.9 copy-start.13
  223.2 0.7 copy-start.12
  223.3 2.8 copy-start.10
  223.3 2.8 copy-start.14
  224.2 1.9 copy-start.1
  224.6 1.5 copy-start.2
  300.0 2.0 copy-start.4
  305.9 6.0 %copy-start.16 = (f32[128]{0:T(128)S(1)}, f32[128]{0:T(128)}, u32[]{:S(2)}) copy-start(f32[128]{0:T(128)} %copy-done.15) | copy-start | bytes 1540
  305.9 220.8 %all-to-all-start.5 = ((f32[2,96,256,8]{1,3,0,2:T(8,128)}), f32[2,96,256,8]{1,3,0,2:T(8,128)S(1)}, u32[]{:S(2)}, u32[]{:S(2)}) async-start(f32[2,96,256,8]{1,3,0,2:T(8,128)} %copy.180), calls=%async_computation.5 | async-start | bytes 4194304 | tf_op jit(solution)/shard_map/all_to_all | solution.py:170
  311.8 213.1 %all-reduce.4.cloned.1.call-start = ((), (), s32[]{:S(2)}) async-start(), calls=%async_computation.6 | async-start | bytes 786432 | tf_op jit(solution)/shard_map/psum | solution.py:171
  319.7 6.2 %copy-start.8 = (f32[2,2,12,8,128]{4,3,2,1,0:T(8,128)S(1)}, f32[2,2,12,8,128]{4,3,2,1,0:T(8,128)}, u32[]{:S(2)}) copy-start(f32[2,2,12,8,128]{4,3,2,1,0:T(8,128)} %copy-done.7) | copy-start | bytes 589828
  319.7 6.5 %copy-start.6 = (f32[2,2,12,8,128]{4,3,2,1,0:T(8,128)S(1)}, f32[2,2,12,8,128]{4,3,2,1,0:T(8,128)}, u32[]{:S(2)}) copy-start(f32[2,2,12,8,128]{4,3,2,1,0:T(8,128)} %copy-done.5) | copy-start | bytes 589828
Sparse Core Ops, SparseCore 0:
  328.0 196.8 all-reduce.3
where the time goes:
time: 547 us; the launch traced here: 538 us
  blocking collectives  204 us (37%)
  waiting for transfers between devices  163 us (30%)
  matrix products  59.8 us (11%)
  local copies, waits for them, and re-layouts  43.1 us (8%)
  starting transfers between devices  39.3 us (7%)
  between operations  15.9 us (3%)
  other arithmetic  12.2 us (2%)
    psum x1, blocking collectives, shards(): lax.psum((grad_w_in, grad_b_in, grad_w_out, grad_b_out), 'space')  147 us
    all_to_all x1, blocking collectives, shards(): lax.all_to_all(lon_back, 'space', split_axis=4, concat_axis=3, tiled=True)  57.2 us
    psum x1, waiting for transfers between devices, shards(): lax.psum((grad_w_in, grad_b_in, grad_w_out, grad_b_out), 'space')  48 us
    all_to_all x1, waiting for transfers between devices, shards(): lax.all_to_all(lat_field, 'space', split_axis=3, concat_axis=4, tiled=True)  36.5 us
    all_to_all x1, waiting for transfers between devices, shards(): lax.all_to_all(lat_grad, 'space', split_axis=3, concat_axis=4, tiled=True)  34.3 us
    dot_general x8, matrix products, apply(): return jnp.einsum('ibfn,nk->ibfk', values, table, precision=HIGHEST)  29.3 us
    all_to_all x1, waiting for transfers between devices, shards(): lax.all_to_all(upstream, 'space', split_axis=3, concat_axis=2, tiled=True)  21.4 us
    ppermute x1, waiting for transfers between devices, from_behind(): return lax.ppermute(block, axis, route)  19.4 us
  transfers between devices with their start and end apart: 7, of which 6 were waited for; matrix products, arithmetic and copies ran while one was open for 11% of the time, Pallas kernels for 0%

commit v1 on v0

--- a/solution.py
+++ b/solution.py
@@ -38,37 +38,35 @@
     return (jnp.cos(angle) * factor, jnp.sin(angle) * factor)
 
 
-def lat_columns(field, cos_table, sin_table):
+def lon_forward_table(cos_table, sin_table, ndev):
+    share = cos_table.shape[1] // ndev
+    cos_g = cos_table.reshape(-1, ndev, 1, share)
+    sin_g = -sin_table.reshape(-1, ndev, 1, share)
+    return jnp.concatenate([cos_g, sin_g], axis=2).reshape(cos_table.shape[0], -1)
+
+
+def lon_forward(field, table):
     values = field.astype(jnp.float32)
-    real_part = jnp.einsum("fl,ibln->ibfn", cos_table, values, precision=HIGHEST)
-    imag_part = -jnp.einsum("fl,ibln->ibfn", sin_table, values, precision=HIGHEST)
-    return jnp.stack([real_part, imag_part])
-
-
-def lon_complex(spectrum, cos_table, sin_table):
-
-    def apply(values, table):
-        return jnp.einsum("ibfn,nk->ibfk", values, table, precision=HIGHEST)
-
-    real_part = apply(spectrum[0], cos_table) + apply(spectrum[1], sin_table)
-    imag_part = apply(spectrum[1], cos_table) - apply(spectrum[0], sin_table)
-    return jnp.stack([real_part, imag_part])
-
-
-def lon_complex_inverse(spectrum, cos_table, sin_table):
-
-    def apply(values, table):
-        return jnp.einsum("ibfk,nk->ibfn", values, table, precision=HIGHEST)
-
-    real_part = apply(spectrum[0], cos_table) - apply(spectrum[1], sin_table)
-    imag_part = apply(spectrum[1], cos_table) + apply(spectrum[0], sin_table)
-    return jnp.stack([real_part, imag_part])
-
-
-def lat_real_inverse(spectrum, cos_table, sin_table):
-    first = jnp.einsum("fl,ibfn->ibln", cos_table, spectrum[0], precision=HIGHEST)
-    second = jnp.einsum("fl,ibfn->ibln", sin_table, spectrum[1], precision=HIGHEST)
-    return first - second
+    return jnp.einsum("ibln,nc->iblc", values, table, precision=HIGHEST)
+
+
+def lat_forward(spectrum, cos_table, sin_table):
+    top = jnp.stack([cos_table, sin_table], axis=1)
+    bottom = jnp.stack([-sin_table, cos_table], axis=1)
+    table = jnp.stack([top, bottom])
+    return jnp.einsum("ofpl,iblpj->oibfj", table, spectrum, precision=HIGHEST)
+
+
+def lat_inverse(spectrum, cos_table, sin_table):
+    top = jnp.stack([cos_table, -sin_table])
+    bottom = jnp.stack([sin_table, cos_table])
+    table = jnp.stack([top, bottom])
+    return jnp.einsum("opfl,pibfj->oiblj", table, spectrum, precision=HIGHEST)
+
+
+def lon_inverse(spectrum, cos_table, sin_table):
+    table = jnp.stack([cos_table, -sin_table])
+    return jnp.einsum("piblk,pnk->ibln", spectrum, table, precision=HIGHEST)
 
 
 def mode_mask(signed, wavenumber, keep_lon, keep_lat):
@@ -133,53 +131,54 @@
     )
 
 
+def to_columns(spectrum, ndev):
+    moved = lax.all_to_all(spectrum, "space", split_axis=3, concat_axis=2, tiled=True)
+    nblocks, width, rows, _ = moved.shape
+    return moved.reshape(nblocks, width, rows, 2, -1)
+
+
 def shards(activations, cotangent, kept_modes, weight_in, bias_in, weight_out):
     field = activations[0]
     own_grad = cotangent[0]
     nblocks = field.shape[0]
     width = field.shape[1]
+    ndev = lax.axis_size("space")
     received = from_behind(own_grad, "pipe", -1)
     section_index = lax.axis_index("pipe")
     last_section = lax.axis_size("pipe") - 1
     upstream = jnp.where(section_index == last_section, own_grad, received)
     lon_cos, lon_sin = lon_tables(LON, KEEP_LON)
     lat_cos, lat_sin = lat_tables(LAT, KEEP_LAT)
-    col_field, col_grad = (
-        lax.all_to_all(field, "space", split_axis=3, concat_axis=2, tiled=True),
-        lax.all_to_all(upstream, "space", split_axis=3, concat_axis=2, tiled=True),
-    )
-    lat_field = lat_columns(col_field, lat_cos, lat_sin)
-    lat_grad = lat_columns(col_grad, lat_cos, lat_sin)
-    part_field, part_grad = (
-        lax.all_to_all(lat_field, "space", split_axis=3, concat_axis=4, tiled=True),
-        lax.all_to_all(lat_grad, "space", split_axis=3, concat_axis=4, tiled=True),
-    )
-    share = 2 * KEEP_LAT // lax.axis_size("space")
-    signed = lax.axis_index("space") * share + jnp.arange(share, dtype=jnp.int32) - KEEP_LAT
-    wavenumber = jnp.arange(KEEP_LON, dtype=jnp.int32)
+    table = lon_forward_table(lon_cos, lon_sin, ndev)
+    col_field = to_columns(lon_forward(field, table), ndev)
+    col_grad = to_columns(lon_forward(upstream, table), ndev)
+    spectrum = lat_forward(col_field, lat_cos, lat_sin)
+    grad_spec = lat_forward(col_grad, lat_cos, lat_sin)
+    share = KEEP_LON // ndev
+    signed = jnp.arange(2 * KEEP_LAT, dtype=jnp.int32) - KEEP_LAT
+    wavenumber = lax.axis_index("space") * share + jnp.arange(share, dtype=jnp.int32)
     weight = mode_mask(signed, wavenumber, kept_modes[0, 0], kept_modes[0, 1])
-    spectrum = lon_complex(part_field, lon_cos, lon_sin).reshape(2, nblocks, width, -1)
-    grad_spec = (lon_complex(part_grad, lon_cos, lon_sin) * weight).reshape(2, nblocks, width, -1)
+    grad_spec = grad_spec * weight
+    spectrum = spectrum.reshape(2, nblocks, width, -1)
+    grad_spec = grad_spec.reshape(2, nblocks, width, -1)
     grad_modes, grad_w_in, grad_b_in, grad_w_out, grad_b_out = backprop(
         spectrum, grad_spec, weight_in[0], bias_in[0], weight_out[0]
     )
-    grad_modes = grad_modes.reshape(2, nblocks, width, share, KEEP_LON)
-    lon_back = lon_complex_inverse(grad_modes, lon_cos, lon_sin)
-    lat_parts = lax.all_to_all(lon_back, "space", split_axis=4, concat_axis=3, tiled=True)
-    cols_back = lat_real_inverse(lat_parts, lat_cos, lat_sin)
-    inverse = lax.all_to_all(cols_back, "space", split_axis=2, concat_axis=3, tiled=True)
-    sum_w_in, sum_b_in, sum_w_out, sum_b_out = lax.psum(
-        (grad_w_in, grad_b_in, grad_w_out, grad_b_out), "space"
-    )
+    grad_modes = grad_modes.reshape(2, nblocks, width, 2 * KEEP_LAT, share)
+    lat_back = lat_inverse(grad_modes, lat_cos, lat_sin)
+    rows_back = lax.all_to_all(lat_back, "space", split_axis=3, concat_axis=4, tiled=True)
+    inverse = lon_inverse(rows_back, lon_cos, lon_sin)
+    parts = (grad_w_in, grad_b_in, grad_w_out, grad_b_out)
+    flat = lax.psum(jnp.concatenate([p.reshape(-1) for p in parts]), "space")
     factor = 1.0 / math.sqrt(2 * KEEP_LAT * KEEP_LON)
+    flat = flat * factor
+    sums = []
+    start = 0
+    for p in parts:
+        sums.append(flat[start:start + p.size].reshape(p.shape)[None])
+        start += p.size
     grad_field = (upstream.astype(jnp.float32) + inverse).astype(jnp.bfloat16)
-    return (
-        grad_field[None],
-        (sum_w_in * factor)[None],
-        (sum_b_in * factor)[None],
-        (sum_w_out * factor)[None],
-        (sum_b_out * factor)[None],
-    )
+    return (grad_field[None], *sums)
 
 
 def solution(mesh):

time: 547 us -> 322 us (0.59); the launches traced: 538 us -> 322 us
  blocking collectives: 204 us -> 0 us
  waiting for transfers between devices: 163 us -> 218 us
  matrix products: 59.8 us -> 27.7 us
  local copies, waits for them, and re-layouts: 43.1 us -> 21.3 us
  starting transfers between devices: 39.3 us -> 25.7 us
    psum x1 -> x0, blocking collectives: 147 us -> none  [shards(): lax.psum((grad_w_in, grad_b_in, grad_w_out, grad_b_out), 'space')]
    psum x1, waiting for transfers between devices: 48 us -> 181 us  [shards(): flat = lax.psum(jnp.concatenate([p.reshape(-1) for p in parts]), 'space')]
    all_to_all x5 -> x3, waiting for transfers between devices: 95.4 us -> 36.5 us  [the longest x2 36.5 us: to_columns(): lax.all_to_all(spectrum, 'space', split_axis=3, concat_axis=2, tiled=True)]
    all_to_all x1 -> x0, blocking collectives: 57.2 us -> none  [shards(): lax.all_to_all(lon_back, 'space', split_axis=4, concat_axis=3, tiled=True)]
    dot_general x18 -> x6, matrix products: 47.9 us -> 12.2 us  [the longest x2 4.32 us: lat_forward(): return jnp.einsum('ofpl,iblpj->oibfj', table, spectrum, precision=HIGHEST)]
    ppermute x1, waiting for transfers between devices: 19.4 us -> 0.01 us  [from_behind(): return lax.ppermute(block, axis, route)]
    all_to_all x5 -> x3, starting transfers between devices: 38 us -> 24.2 us  [the longest x2 18 us: to_columns(): lax.all_to_all(spectrum, 'space', split_axis=3, concat_axis=2, tiled=True)]
    another operation x5 -> x4, local copies, waits for them, and re-layouts: 11.6 us -> 2.5 us  [the longest x2 1.56 us: shards(): sums.append(flat[start:start + p.size].reshape(p.shape)[None])]
  transfers between devices with their start and end apart: 7 -> 5, of which waited for: 6 -> 3; matrix products, arithmetic and copies ran while one was open for 11% -> 10% of each run, Pallas kernels for 0% -> 0%
where the time goes in v1:
time: 322 us
  waiting for transfers between devices  218 us (68%)
  matrix products  27.7 us (9%)
  starting transfers between devices  25.7 us (8%)
  local copies, waits for them, and re-layouts  21.3 us (7%)
  between operations  15.2 us (5%)
  other arithmetic  13.7 us (4%)
    psum x1, waiting for transfers between devices, shards(): flat = lax.psum(jnp.concatenate([p.reshape(-1) for p in parts]), 'space')  181 us
    all_to_all x2, waiting for transfers between devices, to_columns(): lax.all_to_all(spectrum, 'space', split_axis=3, concat_axis=2, tiled=True)  36.5 us
    all_to_all x2, starting transfers between devices, to_columns(): lax.all_to_all(spectrum, 'space', split_axis=3, concat_axis=2, tiled=True)  18 us
    dot_general x12, matrix products, block_product(): return jnp.einsum('kij,kjm->kim', weights, values, precision=HIGHEST)  8.45 us
    dot_general x8, matrix products, outer(): return jnp.einsum('kim,kjm->kij', first, second, precision=HIGHEST)  7.06 us
  transfers between devices with their start and end apart: 5, of which 3 were waited for; matrix products, arithmetic and copies ran while one was open for 10% of the time, Pallas kernels for 0%

profile of v1, /device:TPU:1, one launch (start us, length us, event | category | flops | bytes accessed | tf_op | source)
XLA Modules:
  0.0 321.6 jit_solution(10139144057353818044)
XLA Ops:
  7.2 2.2 copy.270
  9.4 1.3 collective-permute-start
  10.7 1.1 cosine_multiply_fusion.1
  12.7 0.9 convolution_bitcast_fusion.1
  13.5 1.3 copy.181
  14.9 11.6 %all-to-all-start.1 = ((f32[2,96,4,256]{1,2,0,3:T(4,128)}), f32[2,96,4,256]{1,2,0,3:T(4,128)S(1)}, u32[]{:S(2)}, u32[]{:S(2)}) async-start(f32[2,96,4,256]{1,2,0,3:T(4,128)} %copy.181), calls=%async_computation.1 | async-start | bytes 2097152 | tf_op jit(solution)/shard_map/all_to_all | solution.py:135
  28.4 1.8 multiply_negate_fusion
  30.9 0.7 maximum_bitcast_fusion.9
  31.6 1.3 fusion.92
  32.9 1.7 broadcast_select_fusion
  34.6 1.7 fusion.16
  36.3 2.5 copy.167
  38.8 16.3 %all-to-all-done.1 = f32[2,96,4,256]{1,2,0,3:T(4,128)S(1)} async-done(((f32[2,96,4,256]{1,2,0,3:T(4,128)}), f32[2,96,4,256]{1,2,0,3:T(4,128)S(1)}, u32[]{:S(2)}, u32[]{:S(2)}) %all-to-all-start.1) | async-done | bytes 786464 | tf_op jit(solution)/shard_map/all_to_all | solution.py:135
  55.1 6.4 %all-to-all-start = ((f32[2,96,4,256]{1,2,0,3:T(4,128)}), f32[2,96,4,256]{1,2,0,3:T(4,128)}, u32[]{:S(2)}, u32[]{:S(2)}) async-start(f32[2,96,4,256]{1,2,0,3:T(4,128)} %copy.167), calls=%async_computation | async-start | bytes 2097152 | tf_op jit(solution)/shard_map/all_to_all | solution.py:135
  61.7 0.7 fusion.93
  62.4 0.8 maximum_bitcast_fusion.11
  63.5 0.7 copy.183
  64.4 1.8 convolution_bitcast_fusion.2
  67.1 1.1 fusion.5
  68.6 1.1 fusion.4
  69.7 20.2 %all-to-all-done = f32[2,96,4,256]{1,2,0,3:T(4,128)} async-done(((f32[2,96,4,256]{1,2,0,3:T(4,128)}), f32[2,96,4,256]{1,2,0,3:T(4,128)}, u32[]{:S(2)}, u32[]{:S(2)}) %all-to-all-start) | async-done | bytes 786464 | tf_op jit(solution)/shard_map/all_to_all | solution.py:135
  89.9 1.4 copy.168
  91.4 0.7 copy.169
  92.1 2.5 fusion.105
  96.6 2.1 fusion.98
  99.3 1.2 fusion.46
  100.6 1.3 fusion.45
  101.8 1.0 fusion.48
  102.9 1.0 fusion.50
  104.8 1.7 fusion.9
  106.5 1.5 fusion.8
  108.2 0.8 reshape.572
  109.0 0.7 copy.211
  109.7 0.7 pad_maximum_fusion.1
  110.5 1.3 fusion.3
  112.0 0.8 copy.197
  113.5 1.7 convolution_bitcast_fusion
  115.2 1.3 copy.199
  116.6 6.2 %all-to-all-start.2 = ((f32[2,2,96,256,2]{2,0,4,1,3:T(2,128)}), f32[2,2,96,256,2]{2,0,4,1,3:T(2,128)S(1)}, u32[]{:S(2)}, u32[]{:S(2)}) async-start(f32[2,2,96,256,2]{2,0,4,1,3:T(2,128)} %copy.199), calls=%async_computation.2 | async-start | bytes 2097152 | tf_op jit(solution)/shard_map/all_to_all | solution.py:169
  122.8 181.5 %all-reduce.2.cloned.1.call-done = f32[74496]{0:T(1024)} async-done(((f32[74496]{0:T(1024)}), f32[74496]{0:T(1024)}) %all-reduce.2.cloned.1.call-update) | async-done | bytes 298000 | tf_op jit(solution)/shard_map/psum | solution.py:172
  304.2 1.0 broadcast_multiply_fusion
  305.3 0.8 broadcast_in_dim_reshape.8
  306.0 0.8 broadcast_in_dim_reshape.9
  306.8 0.7 slice.122
  307.5 0.7 slice.125
  308.4 0.8 copy.201
  309.4 3.5 %fusion.20 = f32[2,96,4,512,1]{3,1,2,0,4:T(8,128)S(1)} fusion(f32[2,2,96,4,128]{2,4,3,1,0:T(8,128)S(1)} %bitcast.215, f32[1,512,128]{2,1,0:T(8,128)S(1)} %copy-done.5, f32[1,512,128]{2,1,0:T(8,128)S(1)} %copy-done.6), kind=kOutput, calls=%fused_computation.43 | convolution fusion | flops 1208090624 | bytes 2883584 | tf_op jit(solution)/shard_map/piblk,pnk->ibln/dot_general | solution.py:69
  313.2 1.5 copy.212
  (74 shorter events, 9.9 us)
Async XLA Ops:
  7.2 5.5 %copy-start = (bf16[1,2,96,4,512]{4,3,2,1,0:T(4,128)(2,1)S(1)}, bf16[1,2,96,4,512]{4,3,2,1,0:T(4,128)(2,1)}, u32[]{:S(2)}) copy-start(bf16[1,2,96,4,512]{4,3,2,1,0:T(4,128)(2,1)} %param.6) | copy-start | bytes 2359300
  9.4 23.5 %collective-permute-start = (bf16[2,96,4,512]{3,1,0,2:T(8,128)(2,1)}, bf16[2,96,4,512]{3,1,0,2:T(8,128)(2,1)}, u32[]{:S(2)}, u32[]{:S(2)}) collective-permute-start(bf16[2,96,4,512]{3,1,0,2:T(8,128)(2,1)} %bitcast.197), channel_id=1, source_target_pairs={{64,0},{128,64},{192,128},{256,192},{320,256},{384,320},{448,384},... | collective-permute-start | bytes 2359304 | tf_op jit(solution)/shard_map/ppermute | solution.py:20
  13.5 13.0 %copy-start.14 = (s32[1,2]{1,0:T(1,128)S(1)}, s32[1,2]{1,0:T(1,128)}, u32[]{:S(2)}) copy-start(s32[1,2]{1,0:T(1,128)} %param.8) | copy-start | bytes 28
  14.9 40.2 %all-to-all-start.1 = ((f32[2,96,4,256]{1,2,0,3:T(4,128)}), f32[2,96,4,256]{1,2,0,3:T(4,128)S(1)}, u32[]{:S(2)}, u32[]{:S(2)}) async-start(f32[2,96,4,256]{1,2,0,3:T(4,128)} %copy.181), calls=%async_computation.1 | async-start | bytes 2097152 | tf_op jit(solution)/shard_map/all_to_all | solution.py:135
  36.3 26.1 %copy-start.11 = (f32[1,128,256]{2,1,0:T(8,128)S(1)}, f32[1,128,256]{2,1,0:T(8,128)}, u32[]{:S(2)}) copy-start(f32[1,128,256]{2,1,0:T(8,128)} %get-tuple-element.53) | copy-start | bytes 393220
  36.3 26.1 %copy-start.12 = (f32[1,128,256]{2,1,0:T(8,128)S(1)}, f32[1,128,256]{2,1,0:T(8,128)}, u32[]{:S(2)}) copy-start(f32[1,128,256]{2,1,0:T(8,128)} %get-tuple-element.54) | copy-start | bytes 393220
  55.1 34.9 %all-to-all-start = ((f32[2,96,4,256]{1,2,0,3:T(4,128)}), f32[2,96,4,256]{1,2,0,3:T(4,128)}, u32[]{:S(2)}, u32[]{:S(2)}) async-start(f32[2,96,4,256]{1,2,0,3:T(4,128)} %copy.167), calls=%async_computation | async-start | bytes 2097152 | tf_op jit(solution)/shard_map/all_to_all | solution.py:135
  61.5 242.8 %all-reduce.2.cloned.1.call-start = ((), (), s32[]{:S(2)}) async-start(), calls=%async_computation.3 | async-start | bytes 598016 | tf_op jit(solution)/shard_map/psum | solution.py:172
  63.5 1.0 copy-start.4
  64.4 2.2 copy-start.1
  92.1 2.9 copy-start.10
  94.8 1.8 copy-start.13
  96.6 5.3 %copy-start.2 = (f32[1,2,2,96,96]{4,3,2,1,0:T(8,128)S(1)}, f32[1,2,2,96,96]{4,3,2,1,0:T(8,128)}, u32[]{:S(2)}) copy-start(f32[1,2,2,96,96]{4,3,2,1,0:T(8,128)} %param.9) | copy-start | bytes 442372
  104.6 5.9 %copy-start.3 = (f32[1,2,2,96,96]{4,3,2,1,0:T(8,128)S(1)}, f32[1,2,2,96,96]{4,3,2,1,0:T(8,128)}, u32[]{:S(2)}) copy-start(f32[1,2,2,96,96]{4,3,2,1,0:T(8,128)} %param.9) | copy-start | bytes 442372
  108.0 4.8 %copy-start.9 = (f32[2,256,96]{1,2,0:T(8,128)S(1)}, f32[2,256,96]{1,2,0:T(8,128)}, u32[]{:S(2)}) copy-start(f32[2,256,96]{1,2,0:T(8,128)} %fusion.50) | copy-start | bytes 589828
  110.5 3.0 copy-start.7
  110.5 3.0 copy-start.8
  116.6 191.6 %all-to-all-start.2 = ((f32[2,2,96,256,2]{2,0,4,1,3:T(2,128)}), f32[2,2,96,256,2]{2,0,4,1,3:T(2,128)S(1)}, u32[]{:S(2)}, u32[]{:S(2)}) async-start(f32[2,2,96,256,2]{2,0,4,1,3:T(2,128)} %copy.199), calls=%async_computation.2 | async-start | bytes 2097152 | tf_op jit(solution)/shard_map/all_to_all | solution.py:169
  308.4 1.0 copy-start.5
  308.4 1.0 copy-start.6
Sparse Core Ops, SparseCore 0:
  110.6 193.5 all-reduce.1

commit v2 on v1

--- a/solution.py
+++ b/solution.py
@@ -135,6 +135,17 @@
     moved = lax.all_to_all(spectrum, "space", split_axis=3, concat_axis=2, tiled=True)
     nblocks, width, rows, _ = moved.shape
     return moved.reshape(nblocks, width, rows, 2, -1)
+
+
+def sum_over(flat, axis):
+    n = lax.axis_size(axis)
+    pad = (-flat.shape[0]) % n
+    pieces = jnp.pad(flat, (0, pad)).reshape(n, -1)
+    got = lax.all_to_all(pieces, axis, split_axis=0, concat_axis=0, tiled=True)
+    mine = jnp.sum(got, axis=0)
+    spread = jnp.broadcast_to(mine[None], pieces.shape)
+    full = lax.all_to_all(spread, axis, split_axis=0, concat_axis=0, tiled=True)
+    return full.reshape(-1)[: flat.shape[0]]
 
 
 def shards(activations, cotangent, kept_modes, weight_in, bias_in, weight_out):
@@ -169,7 +180,7 @@
     rows_back = lax.all_to_all(lat_back, "space", split_axis=3, concat_axis=4, tiled=True)
     inverse = lon_inverse(rows_back, lon_cos, lon_sin)
     parts = (grad_w_in, grad_b_in, grad_w_out, grad_b_out)
-    flat = lax.psum(jnp.concatenate([p.reshape(-1) for p in parts]), "space")
+    flat = sum_over(jnp.concatenate([p.reshape(-1) for p in parts]), "space")
     factor = 1.0 / math.sqrt(2 * KEEP_LAT * KEEP_LON)
     flat = flat * factor
     sums = []

time: 322 us -> 185 us (0.57)
  waiting for transfers between devices: 218 us -> 79.3 us
  starting transfers between devices: 25.7 us -> 42.9 us
  between operations: 15.2 us -> 1.84 us
    psum x1 -> x0, waiting for transfers between devices: 181 us -> none  [shards(): flat = lax.psum(jnp.concatenate([p.reshape(-1) for p in parts]), 'space')]
    all_to_all x1, waiting for transfers between devices: 0.01 us -> 21.5 us  [shards(): lax.all_to_all(lat_back, 'space', split_axis=3, concat_axis=4, tiled=True)]
    all_to_all x0 -> x2, waiting for transfers between devices: none -> 18.5 us  [the longest x1 11.5 us: sum_over(): got = lax.all_to_all(pieces, axis, split_axis=0, concat_axis=0, tiled=True)]
    ppermute x1, waiting for transfers between devices: 0.01 us -> 18 us  [from_behind(): return lax.ppermute(block, axis, route)]
    all_to_all x2, waiting for transfers between devices: 36.5 us -> 21.3 us  [to_columns(): lax.all_to_all(spectrum, 'space', split_axis=3, concat_axis=2, tiled=True)]
    all_to_all x0 -> x2, starting transfers between devices: none -> 12.4 us  [the longest x1 6.19 us: sum_over(): got = lax.all_to_all(pieces, axis, split_axis=0, concat_axis=0, tiled=True)]
    all_to_all x2, starting transfers between devices: 18 us -> 23.1 us  [to_columns(): lax.all_to_all(spectrum, 'space', split_axis=3, concat_axis=2, tiled=True)]
  transfers between devices with their start and end apart: 5 -> 6, of which waited for: 3 -> 5; matrix products, arithmetic and copies ran while one was open for 10% -> 17% of each run, Pallas kernels for 0% -> 0%
where the time goes in v2:
time: 185 us; the launch traced here: 184 us
  waiting for transfers between devices  79.3 us (43%)
  starting transfers between devices  42.9 us (23%)
  matrix products  26.8 us (14%)
  local copies, waits for them, and re-layouts  22.2 us (12%)
  other arithmetic  10.8 us (6%)
    all_to_all x2, starting transfers between devices, to_columns(): lax.all_to_all(spectrum, 'space', split_axis=3, concat_axis=2, tiled=True)  23.1 us
    all_to_all x1, waiting for transfers between devices, shards(): lax.all_to_all(lat_back, 'space', split_axis=3, concat_axis=4, tiled=True)  21.5 us
    all_to_all x2, waiting for transfers between devices, to_columns(): lax.all_to_all(spectrum, 'space', split_axis=3, concat_axis=2, tiled=True)  21.3 us
    ppermute x1, waiting for transfers between devices, from_behind(): return lax.ppermute(block, axis, route)  18 us
    all_to_all x1, waiting for transfers between devices, sum_over(): got = lax.all_to_all(pieces, axis, split_axis=0, concat_axis=0, tiled=True)  11.5 us
    dot_general x12, matrix products, block_product(): return jnp.einsum('kij,kjm->kim', weights, values, precision=HIGHEST)  7.72 us
    all_to_all x1, waiting for transfers between devices, sum_over(): full = lax.all_to_all(spread, axis, split_axis=0, concat_axis=0, tiled=True)  6.93 us
    dot_general x8, matrix products, outer(): return jnp.einsum('kim,kjm->kij', first, second, precision=HIGHEST)  6.87 us
  transfers between devices with their start and end apart: 6, of which 5 were waited for; matrix products, arithmetic and copies ran while one was open for 17% of the time, Pallas kernels for 0%

profile of v2, /device:TPU:1, one launch (start us, length us, event | category | flops | bytes accessed | tf_op | source)
XLA Modules:
  0.0 183.7 jit_solution(6455490998223400480)
XLA Ops:
  0.7 1.1 cosine_multiply_fusion.1
  2.6 0.9 convolution_bitcast_fusion.1
  3.5 1.3 copy.279
  4.8 11.8 %all-to-all-start.1 = ((f32[2,96,4,256]{1,2,0,3:T(4,128)}), f32[2,96,4,256]{1,2,0,3:T(4,128)S(1)}, u32[]{:S(2)}, u32[]{:S(2)}) async-start(f32[2,96,4,256]{1,2,0,3:T(4,128)} %copy.279), calls=%async_computation.1 | async-start | bytes 2097152 | tf_op jit(solution)/shard_map/all_to_all | solution.py:135
  16.6 1.0 copy.370
  17.6 1.3 collective-permute-start
  20.2 0.7 compare_and_fusion
  21.5 18.0 %collective-permute-done = bf16[2,96,4,512]{3,1,0,2:T(8,128)(2,1)} collective-permute-done((bf16[2,96,4,512]{3,1,0,2:T(8,128)(2,1)}, bf16[2,96,4,512]{3,1,0,2:T(8,128)(2,1)}, u32[]{:S(2)}, u32[]{:S(2)}) %collective-permute-start) | collective-permute-done | bytes 786464 | tf_op jit(solution)/shard_map/ppermute | solution.py:20
  39.5 1.7 broadcast_select_fusion
  41.1 1.7 fusion.16
  42.8 2.5 %copy.265 = f32[2,96,4,256]{1,2,0,3:T(4,128)} copy(f32[2,96,4,256]{3,1,2,0:T(8,128)} %fusion.16) | data formatting | bytes 1572864 | tf_op jit(solution)/shard_map/ibln,nc->iblc/dot_general | solution.py:50
  45.3 11.3 %all-to-all-start = ((f32[2,96,4,256]{1,2,0,3:T(4,128)}), f32[2,96,4,256]{1,2,0,3:T(4,128)}, u32[]{:S(2)}, u32[]{:S(2)}) async-start(f32[2,96,4,256]{1,2,0,3:T(4,128)} %copy.265), calls=%async_computation | async-start | bytes 2097152 | tf_op jit(solution)/shard_map/all_to_all | solution.py:135
  56.6 0.7 fusion.93
  57.6 0.7 copy.281
  58.3 1.8 convolution_bitcast_fusion.2
  60.9 1.1 fusion.5
  62.5 1.1 fusion.4
  63.6 21.3 %all-to-all-done = f32[2,96,4,256]{1,2,0,3:T(4,128)} async-done(((f32[2,96,4,256]{1,2,0,3:T(4,128)}), f32[2,96,4,256]{1,2,0,3:T(4,128)}, u32[]{:S(2)}, u32[]{:S(2)}) %all-to-all-start) | async-done | bytes 786464 | tf_op jit(solution)/shard_map/all_to_all | solution.py:135
  84.9 1.4 copy.266
  86.3 0.7 copy.267
  87.0 2.5 %fusion.105 = (f32[2,2,96]{2,0,1:T(2,128)}, f32[2,2,96,128,2]{3,2,0,4,1:T(8,128)S(1)}) fusion(f32[128,2]{0,1:T(2,128)S(1)} %and_select_fusion, f32[1,128,2,256]{3,1,2,0:T(8,128)S(1)} %get-tuple-element.52, f32[1,128,2,256]{3,1,2,0:T(8,128)S(1)} %get-tuple-element.51, f32[2,96,256,2,2,1]{1,2,4,3,0,5:T(8,128)S(1)} %bitcast.216), kind=kOutput, calls=%fused_computation.168 | convolution fusion | flops 604307072 | bytes 1706496 | tf_op jit(solution)/shard_map/ofpl,iblpj->oibfj/dot_general | solution.py:57
  91.5 2.0 %fusion.98 = (f32[2,2,96]{2,1,0:T(2,128)}, f32[2,2,96,256]{3,2,1,0:T(8,128)S(1)}, f32[2,2,96,256]{3,2,1,0:T(8,128)S(1)}) fusion(f32[2,2,96]{2,1,0:T(2,128)S(1)} %bitcast.223, f32[1,2,96,256]{3,2,1,0:T(8,128)} %fusion.4, f32[1,2,96,256]{3,2,1,0:T(8,128)} %fusion.5, f32[1,2,96,256]{3,2,1,0:T(8,128)S(1)} %fusion.6, f32[1,2,96,256]{3,2,1,0:T(8,128)S(1)} %fusion.7), kind=kLoop, calls=%fused_computation.162 | loop fusion | flops 2260608 | bytes 1575936 | tf_op jit(solution)/shard_map/reduce_sum | solution.py:128
  94.3 1.3 fusion.46
  95.5 1.3 fusion.45
  97.6 1.5 fusion.9
  99.2 1.5 fusion.8
  101.3 1.2 all_to_all.55
  102.5 6.2 %all-to-all-start.3 = ((f32[64,1,1164]{2,1,0:T(1,128)}), f32[64,1,1164]{2,1,0:T(1,128)S(1)}, u32[]{:S(2)}, u32[]{:S(2)}) async-start(f32[64,1,1164]{2,1,0:T(1,128)} %all_to_all.55), calls=%async_computation.3 | async-start | bytes 655360 | tf_op jit(solution)/shard_map/all_to_all | solution.py:144
  109.4 1.0 fusion.48
  110.4 11.5 %all-to-all-done.3 = f32[64,1,1164]{2,1,0:T(1,128)S(1)} async-done(((f32[64,1,1164]{2,1,0:T(1,128)}), f32[64,1,1164]{2,1,0:T(1,128)S(1)}, u32[]{:S(2)}, u32[]{:S(2)}) %all-to-all-start.3) | async-done | bytes 298016 | tf_op jit(solution)/shard_map/all_to_all | solution.py:144
  122.2 0.9 broadcast_in_dim.15
  123.1 6.2 %all-to-all-start.4 = ((f32[64,1,1164]{2,1,0:T(1,128)}), f32[64,1,1164]{2,1,0:T(1,128)S(1)}, u32[]{:S(2)}, u32[]{:S(2)}) async-start(f32[64,1,1164]{2,1,0:T(1,128)} %broadcast_in_dim.15), calls=%async_computation.4 | async-start | bytes 655360 | tf_op jit(solution)/shard_map/all_to_all | solution.py:147
  129.3 1.3 fusion.3
  130.7 0.8 copy.295
  132.5 1.7 convolution_bitcast_fusion
  134.3 1.3 copy.297
  135.6 6.9 %all-to-all-done.4 = f32[64,1,1164]{2,1,0:T(1,128)S(1)} async-done(((f32[64,1,1164]{2,1,0:T(1,128)}), f32[64,1,1164]{2,1,0:T(1,128)S(1)}, u32[]{:S(2)}, u32[]{:S(2)}) %all-to-all-start.4) | async-done | bytes 298016 | tf_op jit(solution)/shard_map/all_to_all | solution.py:147
  142.5 6.2 %all-to-all-start.2 = ((f32[2,2,96,256,2]{2,0,4,1,3:T(2,128)}), f32[2,2,96,256,2]{2,0,4,1,3:T(2,128)S(1)}, u32[]{:S(2)}, u32[]{:S(2)}) async-start(f32[2,2,96,256,2]{2,0,4,1,3:T(2,128)} %copy.297), calls=%async_computation.2 | async-start | bytes 2097152 | tf_op jit(solution)/shard_map/all_to_all | solution.py:180
  148.7 1.7 multiply_negate_fusion
  150.4 0.9 multiply_reduce_fusion
  151.6 1.3 mul.470
  152.9 0.8 broadcast_in_dim_reshape.8
  153.7 0.8 broadcast_in_dim_reshape.9
  154.5 1.3 fusion.100
  155.7 21.5 %all-to-all-done.2 = f32[2,2,96,256,2]{2,0,4,1,3:T(2,128)S(1)} async-done(((f32[2,2,96,256,2]{2,0,4,1,3:T(2,128)}), f32[2,2,96,256,2]{2,0,4,1,3:T(2,128)S(1)}, u32[]{:S(2)}, u32[]{:S(2)}) %all-to-all-start.2) | async-done | bytes 786464 | tf_op jit(solution)/shard_map/all_to_all | solution.py:180
  177.5 0.8 copy.299
  178.4 3.5 %fusion.20 = f32[2,96,4,512,1]{3,1,2,0,4:T(8,128)S(1)} fusion(f32[2,2,96,4,128]{2,4,3,1,0:T(8,128)S(1)} %bitcast.215, f32[1,512,128]{2,1,0:T(8,128)S(1)} %get-tuple-element.67, f32[1,512,128]{2,1,0:T(8,128)S(1)} %copy-done.4), kind=kOutput, calls=%fused_computation.43 | convolution fusion | flops 1208090624 | bytes 2883584 | tf_op jit(solution)/shard_map/piblk,pnk->ibln/dot_general | solution.py:69
  182.2 1.5 copy.311
  (72 shorter events, 10.5 us)
Async XLA Ops:
  0.6 2.0 %copy-start = (bf16[1,2,96,4,512]{4,3,2,1,0:T(4,128)(2,1)S(1)}, bf16[1,2,96,4,512]{4,3,2,1,0:T(4,128)(2,1)}, u32[]{:S(2)}) copy-start(bf16[1,2,96,4,512]{4,3,2,1,0:T(4,128)(2,1)} %param.6) | copy-start | bytes 2359300
  3.5 13.1 %copy-start.1 = (bf16[1,2,96,4,512]{4,3,2,1,0:T(4,128)(2,1)S(1)}, bf16[1,2,96,4,512]{4,3,2,1,0:T(4,128)(2,1)}, u32[]{:S(2)}) copy-start(bf16[1,2,96,4,512]{4,3,2,1,0:T(4,128)(2,1)} %param.7) | copy-start | bytes 2359300
  4.8 14.1 %copy-start.11 = (s32[1,2]{1,0:T(1,128)S(1)}, s32[1,2]{1,0:T(1,128)}, u32[]{:S(2)}) copy-start(s32[1,2]{1,0:T(1,128)} %param.8) | copy-start | bytes 28
  4.8 40.5 %all-to-all-start.1 = ((f32[2,96,4,256]{1,2,0,3:T(4,128)}), f32[2,96,4,256]{1,2,0,3:T(4,128)S(1)}, u32[]{:S(2)}, u32[]{:S(2)}) async-start(f32[2,96,4,256]{1,2,0,3:T(4,128)} %copy.279), calls=%async_computation.1 | async-start | bytes 2097152 | tf_op jit(solution)/shard_map/all_to_all | solution.py:135
  17.6 21.8 %collective-permute-start = (bf16[2,96,4,512]{3,1,0,2:T(8,128)(2,1)}, bf16[2,96,4,512]{3,1,0,2:T(8,128)(2,1)}, u32[]{:S(2)}, u32[]{:S(2)}) collective-permute-start(bf16[2,96,4,512]{3,1,0,2:T(8,128)(2,1)} %bitcast.197), channel_id=1, source_target_pairs={{64,0},{128,64},{192,128},{256,192},{320,256},{384,320},{448,384},... | collective-permute-start | bytes 2359304 | tf_op jit(solution)/shard_map/ppermute | solution.py:20
  20.2 1.3 copy-start.9
  45.3 39.6 %all-to-all-start = ((f32[2,96,4,256]{1,2,0,3:T(4,128)}), f32[2,96,4,256]{1,2,0,3:T(4,128)}, u32[]{:S(2)}, u32[]{:S(2)}) async-start(f32[2,96,4,256]{1,2,0,3:T(4,128)} %copy.265), calls=%async_computation | async-start | bytes 2097152 | tf_op jit(solution)/shard_map/all_to_all | solution.py:135
  58.3 2.2 %copy-start.2 = (f32[1,2,2,96,96]{4,3,2,1,0:T(8,128)S(1)}, f32[1,2,2,96,96]{4,3,2,1,0:T(8,128)}, u32[]{:S(2)}) copy-start(f32[1,2,2,96,96]{4,3,2,1,0:T(8,128)} %param.9) | copy-start | bytes 442372
  87.0 2.9 %copy-start.5 = (f32[1,2,2,96,96]{4,3,2,1,0:T(8,128)S(1)}, f32[1,2,2,96,96]{4,3,2,1,0:T(8,128)}, u32[]{:S(2)}) copy-start(f32[1,2,2,96,96]{4,3,2,1,0:T(8,128)} %param.11) | copy-start | bytes 442372
  89.7 1.8 copy-start.8
  97.1 4.0 %copy-start.6 = (f32[2,2,96]{2,1,0:T(2,128)S(1)}, f32[2,2,96]{2,1,0:T(2,128)}, u32[]{:S(2)}) copy-start(f32[2,2,96]{2,1,0:T(2,128)} %get-tuple-element.40) | copy-start | bytes 4612
  97.1 4.0 %copy-start.7 = (f32[2,2,96]{2,0,1:T(2,128)S(1)}, f32[2,2,96]{2,0,1:T(2,128)}, u32[]{:S(2)}) copy-start(f32[2,2,96]{2,0,1:T(2,128)} %get-tuple-element.65) | copy-start | bytes 4612
  100.7 8.0 %copy-start.10 = (s32[128]{0:T(128)S(1)}, s32[128]{0:T(128)}, u32[]{:S(2)}) copy-start(s32[128]{0:T(128)} %copy-done.9) | copy-start | bytes 1540
  101.3 8.1 %copy-start.3 = (f32[1,2,2,96,96]{4,3,2,1,0:T(8,128)S(1)}, f32[1,2,2,96,96]{4,3,2,1,0:T(8,128)}, u32[]{:S(2)}) copy-start(f32[1,2,2,96,96]{4,3,2,1,0:T(8,128)} %param.9) | copy-start | bytes 442372
  102.5 19.5 %all-to-all-start.3 = ((f32[64,1,1164]{2,1,0:T(1,128)}), f32[64,1,1164]{2,1,0:T(1,128)S(1)}, u32[]{:S(2)}, u32[]{:S(2)}) async-start(f32[64,1,1164]{2,1,0:T(1,128)} %all_to_all.55), calls=%async_computation.3 | async-start | bytes 655360 | tf_op jit(solution)/shard_map/all_to_all | solution.py:144
  123.1 19.4 %all-to-all-start.4 = ((f32[64,1,1164]{2,1,0:T(1,128)}), f32[64,1,1164]{2,1,0:T(1,128)S(1)}, u32[]{:S(2)}, u32[]{:S(2)}) async-start(f32[64,1,1164]{2,1,0:T(1,128)} %broadcast_in_dim.15), calls=%async_computation.4 | async-start | bytes 655360 | tf_op jit(solution)/shard_map/all_to_all | solution.py:147
  142.5 34.7 %all-to-all-start.2 = ((f32[2,2,96,256,2]{2,0,4,1,3:T(2,128)}), f32[2,2,96,256,2]{2,0,4,1,3:T(2,128)S(1)}, u32[]{:S(2)}, u32[]{:S(2)}) async-start(f32[2,2,96,256,2]{2,0,4,1,3:T(2,128)} %copy.297), calls=%async_computation.2 | async-start | bytes 2097152 | tf_op jit(solution)/shard_map/all_to_all | solution.py:180
  177.5 1.0 copy-start.4

commit v3 on v2

--- a/solution.py
+++ b/solution.py
@@ -11,7 +11,7 @@
 KEEP_LAT = 64
 
 
-HIGHEST = lax.Precision.HIGHEST
+HIGHEST = lax.Precision.HIGH
 
 
 def from_behind(block, axis, distance):
@@ -157,13 +157,14 @@
     received = from_behind(own_grad, "pipe", -1)
     section_index = lax.axis_index("pipe")
     last_section = lax.axis_size("pipe") - 1
-    upstream = jnp.where(section_index == last_section, own_grad, received)
     lon_cos, lon_sin = lon_tables(LON, KEEP_LON)
     lat_cos, lat_sin = lat_tables(LAT, KEEP_LAT)
     table = lon_forward_table(lon_cos, lon_sin, ndev)
     col_field = to_columns(lon_forward(field, table), ndev)
+    spectrum = lat_forward(col_field, lat_cos, lat_sin)
+    spectrum, received = lax.optimization_barrier((spectrum, received))
+    upstream = jnp.where(section_index == last_section, own_grad, received)
     col_grad = to_columns(lon_forward(upstream, table), ndev)
-    spectrum = lat_forward(col_field, lat_cos, lat_sin)
     grad_spec = lat_forward(col_grad, lat_cos, lat_sin)
     share = KEEP_LON // ndev
     signed = jnp.arange(2 * KEEP_LAT, dtype=jnp.int32) - KEEP_LAT
@@ -177,10 +178,23 @@
     )
     grad_modes = grad_modes.reshape(2, nblocks, width, 2 * KEEP_LAT, share)
     lat_back = lat_inverse(grad_modes, lat_cos, lat_sin)
-    rows_back = lax.all_to_all(lat_back, "space", split_axis=3, concat_axis=4, tiled=True)
+    parts = (grad_w_in, grad_b_in, grad_w_out, grad_b_out)
+    flat = jnp.concatenate([p.reshape(-1) for p in parts])
+    pad = (-flat.shape[0]) % ndev
+    pieces = jnp.pad(flat, (0, pad)).reshape(ndev, -1)
+    rows = LAT // ndev
+    back = lat_back.reshape(2, nblocks, width, ndev, rows, share)
+    back = jnp.moveaxis(back, 3, 0).reshape(ndev, -1)
+    moved = lax.all_to_all(
+        jnp.concatenate([back, pieces], axis=1), "space", split_axis=0, concat_axis=0, tiled=True
+    )
+    rows_back = moved[:, : back.shape[1]].reshape(ndev, 2, nblocks, width, rows, share)
+    rows_back = jnp.moveaxis(rows_back, 0, 4).reshape(2, nblocks, width, rows, ndev * share)
+    mine = jnp.sum(moved[:, back.shape[1]:], axis=0)
+    spread = jnp.broadcast_to(mine[None], pieces.shape)
+    flat = lax.all_to_all(spread, "space", split_axis=0, concat_axis=0, tiled=True)
+    flat = flat.reshape(-1)[: flat.size - pad]
     inverse = lon_inverse(rows_back, lon_cos, lon_sin)
-    parts = (grad_w_in, grad_b_in, grad_w_out, grad_b_out)
-    flat = sum_over(jnp.concatenate([p.reshape(-1) for p in parts]), "space")
     factor = 1.0 / math.sqrt(2 * KEEP_LAT * KEEP_LON)
     flat = flat * factor
     sums = []

time: 185 us -> 169 us (0.914)
  starting transfers between devices: 42.9 us -> 32 us
  matrix products: 26.8 us -> 18.4 us
  local copies, waits for them, and re-layouts: 22.2 us -> 24.2 us
    all_to_all x2, waiting for transfers between devices: 21.3 us -> 44.9 us  [to_columns(): lax.all_to_all(spectrum, 'space', split_axis=3, concat_axis=2, tiled=True)]
    ppermute x1, waiting for transfers between devices: 18 us -> 0.01 us  [from_behind(): return lax.ppermute(block, axis, route)]
    all_to_all x3 -> x2, starting transfers between devices: 18.5 us -> 12.6 us  [the longest x1 6.41 us: shards(): lax.all_to_all(spread, 'space', split_axis=0, concat_axis=0, tiled=True)]
    all_to_all x2, starting transfers between devices: 23.1 us -> 18.1 us  [to_columns(): lax.all_to_all(spectrum, 'space', split_axis=3, concat_axis=2, tiled=True)]
    all_to_all x3 -> x2, waiting for transfers between devices: 40 us -> 35.4 us  [the longest x1 28.2 us: shards(): lax.all_to_all(jnp.concatenate([back, pieces], axis=1), 'space', split_ax...]
    dot_general x8, matrix products: 6.87 us -> 2.59 us  [outer(): return jnp.einsum('kim,kjm->kij', first, second, precision=HIGHEST)]
    transpose x0 -> x2, local copies, waits for them, and re-layouts: none -> 3.01 us  [the longest x1 2.13 us: shards(): back = jnp.moveaxis(back, 3, 0).reshape(ndev, -1)]
  transfers between devices with their start and end apart: 6 -> 5, of which waited for: 5 -> 4; matrix products, arithmetic and copies ran while one was open for 17% -> 12% of each run, Pallas kernels for 0% -> 0%
where the time goes in v3:
time: 169 us; the launch traced here: 168 us
  waiting for transfers between devices  80.3 us (48%)
  starting transfers between devices  32 us (19%)
  local copies, waits for them, and re-layouts  24.2 us (14%)
  matrix products  18.4 us (11%)
  other arithmetic  11.7 us (7%)
  between operations  1.89 us (1%)
    all_to_all x2, waiting for transfers between devices, to_columns(): lax.all_to_all(spectrum, 'space', split_axis=3, concat_axis=2, tiled=True)  44.9 us
    all_to_all x1, waiting for transfers between devices, shards(): lax.all_to_all(jnp.concatenate([back, pieces], axis=1), 'space', split_ax...  28.2 us
    all_to_all x2, starting transfers between devices, to_columns(): lax.all_to_all(spectrum, 'space', split_axis=3, concat_axis=2, tiled=True)  18.1 us
    all_to_all x1, waiting for transfers between devices, shards(): lax.all_to_all(spread, 'space', split_axis=0, concat_axis=0, tiled=True)  7.22 us
    all_to_all x1, starting transfers between devices, shards(): lax.all_to_all(spread, 'space', split_axis=0, concat_axis=0, tiled=True)  6.41 us
    all_to_all x1, starting transfers between devices, shards(): lax.all_to_all(jnp.concatenate([back, pieces], axis=1), 'space', split_ax...  6.2 us
    dot_general x12, matrix products, block_product(): return jnp.einsum('kij,kjm->kim', weights, values, precision=HIGHEST)  6.14 us
    unnamed x31, local copies, waits for them, and re-layouts  3.6 us
  transfers between devices with their start and end apart: 5, of which 4 were waited for; matrix products, arithmetic and copies ran while one was open for 12% of the time, Pallas kernels for 0%

profile of v3, /device:TPU:1, one launch (start us, length us, event | category | flops | bytes accessed | tf_op | source)
XLA Modules:
  0.0 168.5 jit_solution(18442946945334430172)
XLA Ops:
  0.7 1.1 cosine_multiply_fusion.1
  2.6 0.6 convolution_bitcast_fusion.1
  3.2 1.4 copy.220
  4.6 11.8 %all-to-all-start = ((f32[2,96,4,256]{1,2,0,3:T(4,128)}), f32[2,96,4,256]{1,2,0,3:T(4,128)S(1)}, u32[]{:S(2)}, u32[]{:S(2)}) async-start(f32[2,96,4,256]{1,2,0,3:T(4,128)} %copy.220), calls=%async_computation | async-start | bytes 2097152 | tf_op jit(solution)/shard_map/all_to_all | solution.py:135
  16.4 1.0 copy.332
  17.4 1.3 collective-permute-start
  18.7 0.6 fusion.104
  20.0 0.7 compare_and_fusion
  20.6 0.7 fusion.93
  21.3 0.6 sine_multiply_fusion.1
  21.9 0.7 maximum_bitcast_fusion.10
  22.7 22.3 %all-to-all-done = f32[2,96,4,256]{1,2,0,3:T(4,128)S(1)} async-done(((f32[2,96,4,256]{1,2,0,3:T(4,128)}), f32[2,96,4,256]{1,2,0,3:T(4,128)S(1)}, u32[]{:S(2)}, u32[]{:S(2)}) %all-to-all-start) | async-done | bytes 786464 | tf_op jit(solution)/shard_map/all_to_all | solution.py:135
  45.2 0.7 copy.222
  46.1 1.8 %convolution_bitcast_fusion.3 = f32[2,2,96,128,2]{3,2,0,4,1:T(8,128)} fusion(f32[2,96,256,2,2,1]{1,2,4,3,0,5:T(8,128)S(1)} %bitcast.235, f32[1,128,2,256]{3,1,2,0:T(8,128)S(1)} %copy-done.4, f32[1,128,2,256]{3,1,2,0:T(8,128)S(1)} %get-tuple-element.52), kind=kOutput, calls=%fused_computation.6 | convolution fusion | flops 302120960 | bytes 1703936 | tf_op jit(solution)/shard_map/ofpl,iblpj->oibfj/dot_general | solution.py:57
  47.9 1.7 %fusion.22 = f32[2,96,4,256]{3,1,2,0:T(8,128)S(1)} fusion(f32[512,256]{0,1:T(8,128)S(1)} %reshape.587, bf16[2,96,4,512]{3,1,2,0:T(8,128)(2,1)} %collective-permute-done, pred[]{:T(512)S(6)} %eq.14, bf16[1,2,96,4,512]{4,3,2,1,0:T(4,128)(2,1)S(1)} %copy-done.1), kind=kOutput, calls=%fused_computation.47 | convolution fusion | flops 604372992 | bytes 2883585 | tf_op jit(solution)/shard_map/ibln,nc->iblc/dot_general | solution.py:50
  49.6 1.4 copy.225
  51.0 6.3 %all-to-all-start.1 = ((f32[2,96,4,256]{1,2,0,3:T(4,128)}), f32[2,96,4,256]{1,2,0,3:T(4,128)S(1)}, u32[]{:S(2)}, u32[]{:S(2)}) async-start(f32[2,96,4,256]{1,2,0,3:T(4,128)} %copy.225), calls=%async_computation.1 | async-start | bytes 2097152 | tf_op jit(solution)/shard_map/all_to_all | solution.py:135
  57.3 0.6 fusion.92
  58.0 0.8 maximum_bitcast_fusion.12
  58.9 0.7 fusion.102
  59.6 1.1 copy.237
  61.1 0.9 fusion.4
  62.3 0.9 fusion.5
  63.3 22.6 %all-to-all-done.1 = f32[2,96,4,256]{1,2,0,3:T(4,128)S(1)} async-done(((f32[2,96,4,256]{1,2,0,3:T(4,128)}), f32[2,96,4,256]{1,2,0,3:T(4,128)S(1)}, u32[]{:S(2)}, u32[]{:S(2)}) %all-to-all-start.1) | async-done | bytes 786464 | tf_op jit(solution)/shard_map/all_to_all | solution.py:135
  86.1 0.7 copy.227
  86.8 1.1 fusion.105
  91.8 1.0 fusion.50
  92.8 1.0 fusion.48
  96.8 0.8 copy.250
  98.2 1.5 convolution_bitcast_fusion
  100.1 2.1 %copy.252 = f32[64,2,2,96,4,2]{0,5,4,3,2,1:T(2,128)} copy(f32[64,2,2,96,4,2]{3,4,0,5,2,1:T(4,128)S(1)} %bitcast.231) | data formatting | bytes 1572864 | tf_op jit(solution)/shard_map/transpose | solution.py:187
  102.2 1.6 maximum_bitcast_fusion
  103.7 2.6 %copy.263 = f32[64,1,4236]{2,1,0:T(1,128)} copy(f32[64,1,4236]{0,2,1:T(8,128)S(1)} %maximum_bitcast_fusion) | data formatting | bytes 2168832 | tf_op jit(solution)/shard_map/all_to_all | solution.py:188
  106.3 6.2 %all-to-all-start.2 = ((f32[64,1,4236]{2,1,0:T(1,128)}), f32[64,1,4236]{2,1,0:T(1,128)S(1)}, u32[]{:S(2)}, u32[]{:S(2)}) async-start(f32[64,1,4236]{2,1,0:T(1,128)} %copy.263), calls=%async_computation.2 | async-start | bytes 2228224 | tf_op jit(solution)/shard_map/all_to_all | solution.py:188
  112.5 1.8 %multiply_negate_fusion = (f32[1,512,128]{2,1,0:T(8,128)}, f32[1,512,128]{2,1,0:T(8,128)}) fusion(), kind=kLoop, calls=%fused_computation.80 | loop fusion | flops 1114112 | bytes 524288 | tf_op jit(solution)/shard_map/neg | solution.py:68
  114.3 28.2 %all-to-all-done.2 = f32[64,1,4236]{2,1,0:T(1,128)S(1)} async-done(((f32[64,1,4236]{2,1,0:T(1,128)}), f32[64,1,4236]{2,1,0:T(1,128)S(1)}, u32[]{:S(2)}, u32[]{:S(2)}) %all-to-all-start.2) | async-done | bytes 1084448 | tf_op jit(solution)/shard_map/all_to_all | solution.py:188
  143.1 0.9 copy.265
  144.0 0.9 broadcast_in_dim.15
  144.9 6.4 %all-to-all-start.3 = ((f32[64,1,1164]{2,1,0:T(1,128)}), f32[64,1,1164]{2,1,0:T(1,128)S(1)}, u32[]{:S(2)}, u32[]{:S(2)}) async-start(f32[64,1,1164]{2,1,0:T(1,128)} %broadcast_in_dim.15), calls=%async_computation.3 | async-start | bytes 655360 | tf_op jit(solution)/shard_map/all_to_all | solution.py:195
  151.4 2.9 %fusion.12 = f32[2,96,4,512,1]{3,1,0,2,4:T(8,128)S(1)} fusion(f32[2,2,96,4,128]{2,4,3,1,0:T(8,128)S(1)} %bitcast.230, f32[1,512,128]{2,1,0:T(8,128)} %get-tuple-element.66, f32[1,512,128]{2,1,0:T(8,128)} %get-tuple-element.67), kind=kOutput, calls=%fused_computation.29 | convolution fusion | flops 604110848 | bytes 2883584 | tf_op jit(solution)/shard_map/piblk,pnk->ibln/dot_general | solution.py:69
  154.3 1.6 fusion.16
  155.9 1.5 copy.267
  157.4 7.2 %all-to-all-done.3 = f32[64,1,1164]{2,1,0:T(1,128)S(1)} async-done(((f32[64,1,1164]{2,1,0:T(1,128)}), f32[64,1,1164]{2,1,0:T(1,128)S(1)}, u32[]{:S(2)}, u32[]{:S(2)}) %all-to-all-start.3) | async-done | bytes 298016 | tf_op jit(solution)/shard_map/all_to_all | solution.py:195
  164.6 0.9 multiply_reduce_fusion
  165.7 0.6 mul.470
  166.3 0.8 broadcast_in_dim_reshape.8
  167.1 0.6 fusion.100
  167.7 0.8 broadcast_in_dim_reshape.9
  (79 shorter events, 10.8 us)
Async XLA Ops:
  0.6 2.0 %copy-start = (bf16[1,2,96,4,512]{4,3,2,1,0:T(4,128)(2,1)S(1)}, bf16[1,2,96,4,512]{4,3,2,1,0:T(4,128)(2,1)}, u32[]{:S(2)}) copy-start(bf16[1,2,96,4,512]{4,3,2,1,0:T(4,128)(2,1)} %param.6) | copy-start | bytes 2359300
  3.2 13.2 %copy-start.1 = (bf16[1,2,96,4,512]{4,3,2,1,0:T(4,128)(2,1)S(1)}, bf16[1,2,96,4,512]{4,3,2,1,0:T(4,128)(2,1)}, u32[]{:S(2)}) copy-start(bf16[1,2,96,4,512]{4,3,2,1,0:T(4,128)(2,1)} %param.7) | copy-start | bytes 2359300
  4.6 14.1 %copy-start.13 = (s32[1,2]{1,0:T(1,128)S(1)}, s32[1,2]{1,0:T(1,128)}, u32[]{:S(2)}) copy-start(s32[1,2]{1,0:T(1,128)} %param.8) | copy-start | bytes 28
  4.6 40.3 %all-to-all-start = ((f32[2,96,4,256]{1,2,0,3:T(4,128)}), f32[2,96,4,256]{1,2,0,3:T(4,128)S(1)}, u32[]{:S(2)}, u32[]{:S(2)}) async-start(f32[2,96,4,256]{1,2,0,3:T(4,128)} %copy.220), calls=%async_computation | async-start | bytes 2097152 | tf_op jit(solution)/shard_map/all_to_all | solution.py:135
  17.4 30.4 %collective-permute-start = (bf16[2,96,4,512]{3,1,2,0:T(8,128)(2,1)}, bf16[2,96,4,512]{3,1,2,0:T(8,128)(2,1)}, u32[]{:S(2)}, u32[]{:S(2)}) collective-permute-start(bf16[2,96,4,512]{3,1,2,0:T(8,128)(2,1)} %bitcast.208), channel_id=1, source_target_pairs={{64,0},{128,64},{192,128},{256,192},{320,256},{384,320},{448,384},... | collective-permute-start | bytes 2359304 | tf_op jit(solution)/shard_map/ppermute | solution.py:20
  45.1 1.0 copy-start.4
  51.0 7.9 %copy-start.5 = (f32[2,2,96,128,2]{3,2,0,4,1:T(8,128)S(1)}, f32[2,2,96,128,2]{3,2,0,4,1:T(8,128)}, u32[]{:S(2)}) copy-start(f32[2,2,96,128,2]{3,2,0,4,1:T(8,128)} %convolution_bitcast_fusion.3) | copy-start | bytes 1179652
  51.0 34.9 %all-to-all-start.1 = ((f32[2,96,4,256]{1,2,0,3:T(4,128)}), f32[2,96,4,256]{1,2,0,3:T(4,128)S(1)}, u32[]{:S(2)}, u32[]{:S(2)}) async-start(f32[2,96,4,256]{1,2,0,3:T(4,128)} %copy.225), calls=%async_computation.1 | async-start | bytes 2097152 | tf_op jit(solution)/shard_map/all_to_all | solution.py:135
  57.3 3.5 %copy-start.3 = (f32[1,2,2,96,96]{4,3,2,1,0:T(8,128)S(1)}, f32[1,2,2,96,96]{4,3,2,1,0:T(8,128)}, u32[]{:S(2)}) copy-start(f32[1,2,2,96,96]{4,3,2,1,0:T(8,128)} %param.9) | copy-start | bytes 442372
  87.9 0.9 copy-start.11
  88.1 1.9 %copy-start.7 = (f32[1,2,96,256]{3,2,1,0:T(8,128)S(1)}, f32[1,2,96,256]{3,2,1,0:T(8,128)}, u32[]{:S(2)}) copy-start(f32[1,2,96,256]{3,2,1,0:T(8,128)} %fusion.4) | copy-start | bytes 589828
  88.1 1.9 %copy-start.8 = (f32[1,2,96,256]{3,2,1,0:T(8,128)S(1)}, f32[1,2,96,256]{3,2,1,0:T(8,128)}, u32[]{:S(2)}) copy-start(f32[1,2,96,256]{3,2,1,0:T(8,128)} %fusion.5) | copy-start | bytes 589828
  88.1 1.9 %copy-start.12 = (f32[1,2,2,96]{3,2,1,0:T(2,128)S(1)}, f32[1,2,2,96]{3,2,1,0:T(2,128)}, u32[]{:S(2)}) copy-start(f32[1,2,2,96]{3,2,1,0:T(2,128)} %param.10) | copy-start | bytes 4612
  95.4 0.9 copy-start.10
  95.6 2.0 %copy-start.9 = (f32[2,256,96]{1,2,0:T(8,128)S(1)}, f32[2,256,96]{1,2,0:T(8,128)}, u32[]{:S(2)}) copy-start(f32[2,256,96]{1,2,0:T(8,128)} %fusion.48) | copy-start | bytes 589828
  96.4 1.8 %copy-start.6 = (f32[1,2,128,256]{3,2,1,0:T(8,128)S(1)}, f32[1,2,128,256]{3,2,1,0:T(8,128)}, u32[]{:S(2)}) copy-start(f32[1,2,128,256]{3,2,1,0:T(8,128)} %get-tuple-element.50) | copy-start | bytes 786436
  106.3 36.2 %all-to-all-start.2 = ((f32[64,1,4236]{2,1,0:T(1,128)}), f32[64,1,4236]{2,1,0:T(1,128)S(1)}, u32[]{:S(2)}, u32[]{:S(2)}) async-start(f32[64,1,4236]{2,1,0:T(1,128)} %copy.263), calls=%async_computation.2 | async-start | bytes 2228224 | tf_op jit(solution)/shard_map/all_to_all | solution.py:188
  144.9 19.7 %all-to-all-start.3 = ((f32[64,1,1164]{2,1,0:T(1,128)}), f32[64,1,1164]{2,1,0:T(1,128)S(1)}, u32[]{:S(2)}, u32[]{:S(2)}) async-start(f32[64,1,1164]{2,1,0:T(1,128)} %broadcast_in_dim.15), calls=%async_computation.3 | async-start | bytes 655360 | tf_op jit(solution)/shard_map/all_to_all | solution.py:195
  151.4 3.0 %copy-start.2 = (bf16[1,2,96,4,512]{4,3,2,1,0:T(4,128)(2,1)S(1)}, bf16[1,2,96,4,512]{4,3,2,1,0:T(4,128)(2,1)}, u32[]{:S(2)}) copy-start(bf16[1,2,96,4,512]{4,3,2,1,0:T(4,128)(2,1)} %param.7) | copy-start | bytes 2359300

commit v4 on v3

--- a/solution.py
+++ b/solution.py
@@ -3,7 +3,7 @@
 import jax
 import jax.numpy as jnp
 from jax import lax
-from jax.sharding import PartitionSpec as P
+from jax.sharding import Mesh, PartitionSpec as P
 
 LAT = 256
 LON = 512
@@ -131,10 +131,20 @@
     )
 
 
-def to_columns(spectrum, ndev):
-    moved = lax.all_to_all(spectrum, "space", split_axis=3, concat_axis=2, tiled=True)
-    nblocks, width, rows, _ = moved.shape
-    return moved.reshape(nblocks, width, rows, 2, -1)
+SPACE = ("sx", "sy", "sc")
+
+
+def exchange(values, axis):
+    values = lax.all_to_all(values, SPACE[1:], split_axis=axis + 1, concat_axis=axis + 1, tiled=True)
+    return lax.all_to_all(values, SPACE[0], split_axis=axis, concat_axis=axis, tiled=True)
+
+
+def to_columns(spectrum, groups):
+    nblocks, width, rows, _ = spectrum.shape
+    split = spectrum.reshape(nblocks, width, rows, groups[0], groups[1], -1)
+    moved = exchange(split, 3)
+    moved = jnp.moveaxis(moved, 2, 4)
+    return moved.reshape(nblocks, width, groups[0] * groups[1] * rows, 2, -1)
 
 
 def sum_over(flat, axis):
@@ -153,22 +163,23 @@
     own_grad = cotangent[0]
     nblocks = field.shape[0]
     width = field.shape[1]
-    ndev = lax.axis_size("space")
+    groups = (lax.axis_size(SPACE[0]), lax.axis_size(SPACE[1:]))
+    ndev = groups[0] * groups[1]
     received = from_behind(own_grad, "pipe", -1)
     section_index = lax.axis_index("pipe")
     last_section = lax.axis_size("pipe") - 1
     lon_cos, lon_sin = lon_tables(LON, KEEP_LON)
     lat_cos, lat_sin = lat_tables(LAT, KEEP_LAT)
     table = lon_forward_table(lon_cos, lon_sin, ndev)
-    col_field = to_columns(lon_forward(field, table), ndev)
+    col_field = to_columns(lon_forward(field, table), groups)
     spectrum = lat_forward(col_field, lat_cos, lat_sin)
     spectrum, received = lax.optimization_barrier((spectrum, received))
     upstream = jnp.where(section_index == last_section, own_grad, received)
-    col_grad = to_columns(lon_forward(upstream, table), ndev)
+    col_grad = to_columns(lon_forward(upstream, table), groups)
     grad_spec = lat_forward(col_grad, lat_cos, lat_sin)
     share = KEEP_LON // ndev
     signed = jnp.arange(2 * KEEP_LAT, dtype=jnp.int32) - KEEP_LAT
-    wavenumber = lax.axis_index("space") * share + jnp.arange(share, dtype=jnp.int32)
+    wavenumber = lax.axis_index(SPACE) * share + jnp.arange(share, dtype=jnp.int32)
     weight = mode_mask(signed, wavenumber, kept_modes[0, 0], kept_modes[0, 1])
     grad_spec = grad_spec * weight
     spectrum = spectrum.reshape(2, nblocks, width, -1)
@@ -185,14 +196,13 @@
     rows = LAT // ndev
     back = lat_back.reshape(2, nblocks, width, ndev, rows, share)
     back = jnp.moveaxis(back, 3, 0).reshape(ndev, -1)
-    moved = lax.all_to_all(
-        jnp.concatenate([back, pieces], axis=1), "space", split_axis=0, concat_axis=0, tiled=True
-    )
+    joined = jnp.concatenate([back, pieces], axis=1).reshape(groups[0], groups[1], -1)
+    moved = exchange(joined, 0).reshape(ndev, -1)
     rows_back = moved[:, : back.shape[1]].reshape(ndev, 2, nblocks, width, rows, share)
     rows_back = jnp.moveaxis(rows_back, 0, 4).reshape(2, nblocks, width, rows, ndev * share)
     mine = jnp.sum(moved[:, back.shape[1]:], axis=0)
     spread = jnp.broadcast_to(mine[None], pieces.shape)
-    flat = lax.all_to_all(spread, "space", split_axis=0, concat_axis=0, tiled=True)
+    flat = exchange(spread.reshape(groups[0], groups[1], -1), 0)
     flat = flat.reshape(-1)[: flat.size - pad]
     inverse = lon_inverse(rows_back, lon_cos, lon_sin)
     factor = 1.0 / math.sqrt(2 * KEEP_LAT * KEEP_LON)
@@ -207,19 +217,25 @@
 
 
 def solution(mesh):
+    inner = {"sy": 8, "sc": 2}
+    size = mesh.shape["space"]
+    fine = Mesh(
+        mesh.devices.reshape(mesh.shape["pipe"], size // 16, inner["sy"], inner["sc"]),
+        ("pipe",) + SPACE,
+    )
     return jax.shard_map(
         shards,
-        mesh=mesh,
+        mesh=fine,
         in_specs=(
-            P("pipe", None, None, "space", None),
-            P("pipe", None, None, "space", None),
+            P("pipe", None, None, SPACE, None),
+            P("pipe", None, None, SPACE, None),
             P("pipe", None),
             P("pipe", None, None, None, None),
             P("pipe", None, None, None),
             P("pipe", None, None, None, None),
         ),
         out_specs=(
-            P("pipe", None, None, "space", None),
+            P("pipe", None, None, SPACE, None),
             P("pipe", None, None, None, None),
             P("pipe", None, None, None),
             P("pipe", None, None, None, None),

time: 169 us -> 254 us (1.50)
  blocking collectives: 0 us -> 52.7 us
  local copies, waits for them, and re-layouts: 24.2 us -> 40.9 us
  other arithmetic: 11.7 us -> 21.7 us
  waiting for transfers between devices: 80.3 us -> 83.4 us
  matrix products: 18.4 us -> 21.2 us
    all_to_all x0 -> x2, blocking collectives: none -> 52.7 us  [the longest x1 34.5 us: exchange(): lax.all_to_all(values, SPACE[1:], split_axis=axis + 1, concat_axis=axis +...]
    concatenate x0 -> x4, local copies, waits for them, and re-layouts: none -> 14.9 us  [shards(): jnp.concatenate([back, pieces], axis=1).reshape(groups[0], groups[1], -1)]
    concatenate x0 -> x1, other arithmetic: none -> 13.2 us  [shards(): jnp.concatenate([back, pieces], axis=1).reshape(groups[0], groups[1], -1)]
    all_to_all x4 -> x6, waiting for transfers between devices: 80.3 us -> 83.4 us  [the longest x3 54.8 us: exchange(): lax.all_to_all(values, SPACE[1:], split_axis=axis + 1, concat_axis=axis +...]
    dot_general x8, matrix products: 2.59 us -> 5.15 us  [outer(): return jnp.einsum('kim,kjm->kij', first, second, precision=HIGHEST)]
    all_to_all x4 -> x6, starting transfers between devices: 30.7 us -> 30.1 us  [the longest x3 19.3 us: exchange(): lax.all_to_all(values, SPACE[1:], split_axis=axis + 1, concat_axis=axis +...]
  transfers between devices with their start and end apart: 5 -> 7, of which waited for: 4 -> 6; matrix products, arithmetic and copies ran while one was open for 12% -> 9% of each run, Pallas kernels for 0% -> 0%
where the time goes in v4:
time: 254 us; the launch traced here: 253 us
  waiting for transfers between devices  83.4 us (33%)
  blocking collectives  52.7 us (21%)
  local copies, waits for them, and re-layouts  40.9 us (16%)
  starting transfers between devices  31.3 us (12%)
  other arithmetic  21.7 us (9%)
  matrix products  21.2 us (8%)
    all_to_all x3, waiting for transfers between devices, exchange(): lax.all_to_all(values, SPACE[1:], split_axis=axis + 1, concat_axis=axis +...  54.8 us
    all_to_all x1, blocking collectives, exchange(): lax.all_to_all(values, SPACE[1:], split_axis=axis + 1, concat_axis=axis +...  34.5 us
    all_to_all x3, waiting for transfers between devices, exchange(): lax.all_to_all(values, SPACE[0], split_axis=axis, concat_axis=axis, tiled...  28.6 us
    all_to_all x3, starting transfers between devices, exchange(): lax.all_to_all(values, SPACE[1:], split_axis=axis + 1, concat_axis=axis +...  19.3 us
    all_to_all x1, blocking collectives, exchange(): lax.all_to_all(values, SPACE[0], split_axis=axis, concat_axis=axis, tiled...  18.2 us
    concatenate x4, local copies, waits for them, and re-layouts, shards(): jnp.concatenate([back, pieces], axis=1).reshape(groups[0], groups[1], -1)  14.9 us
    concatenate x1, other arithmetic, shards(): jnp.concatenate([back, pieces], axis=1).reshape(groups[0], groups[1], -1)  13.2 us
    all_to_all x3, starting transfers between devices, exchange(): lax.all_to_all(values, SPACE[0], split_axis=axis, concat_axis=axis, tiled...  10.8 us
  transfers between devices with their start and end apart: 7, of which 6 were waited for; matrix products, arithmetic and copies ran while one was open for 9% of the time, Pallas kernels for 0%

profile of v4, /device:TPU:1, one launch (start us, length us, event | category | flops | bytes accessed | tf_op | source)
XLA Modules:
  0.0 253.1 jit_solution(13952767258501862140)
XLA Ops:
  0.7 1.1 cosine_multiply_fusion.1
  3.6 1.3 copy.338
  4.9 10.3 %all-to-all-start = ((f32[2,96,4,4,16,4]{1,5,3,2,0,4:T(4,128)}), f32[2,96,4,4,16,4]{1,5,3,2,0,4:T(4,128)S(1)}, u32[]{:S(2)}, u32[]{:S(2)}) async-start(f32[2,96,4,4,16,4]{1,5,3,2,0,4:T(4,128)} %copy.338), calls=%async_computation | async-start | bytes 2097152 | tf_op jit(solution)/shard_map/all_to_all | solution.py:138
  15.2 1.0 copy.453
  16.2 1.3 collective-permute-start
  17.5 25.7 %all-to-all-done = f32[2,96,4,4,16,4]{1,5,3,2,0,4:T(4,128)S(1)} async-done(((f32[2,96,4,4,16,4]{1,5,3,2,0,4:T(4,128)}), f32[2,96,4,4,16,4]{1,5,3,2,0,4:T(4,128)S(1)}, u32[]{:S(2)}, u32[]{:S(2)}) %all-to-all-start) | async-done | bytes 786464 | tf_op jit(solution)/shard_map/all_to_all | solution.py:138
  43.2 1.3 copy.339
  44.4 3.5 %all-to-all-start.1 = ((f32[2,96,4,4,16,4]{1,5,4,2,0,3:T(4,128)}), f32[2,96,4,4,16,4]{1,5,4,2,0,3:T(4,128)S(1)}, u32[]{:S(2)}, u32[]{:S(2)}) async-start(f32[2,96,4,4,16,4]{1,5,4,2,0,3:T(4,128)} %copy.339), calls=%async_computation.1 | async-start | bytes 2097152 | tf_op jit(solution)/shard_map/all_to_all | solution.py:139
  48.0 0.9 dot_general.88
  49.6 13.0 %all-to-all-done.1 = f32[2,96,4,4,16,4]{1,5,4,2,0,3:T(4,128)S(1)} async-done(((f32[2,96,4,4,16,4]{1,5,4,2,0,3:T(4,128)}), f32[2,96,4,4,16,4]{1,5,4,2,0,3:T(4,128)S(1)}, u32[]{:S(2)}, u32[]{:S(2)}) %all-to-all-start.1) | async-done | bytes 786464 | tf_op jit(solution)/shard_map/all_to_all | solution.py:139
  63.3 1.0 convolution_bitcast_fusion.3
  64.3 2.1 fusion.17
  66.4 1.4 copy.343
  67.8 4.6 %all-to-all-start.2 = ((f32[2,96,4,4,16,4]{1,5,3,2,0,4:T(4,128)}), f32[2,96,4,4,16,4]{1,5,3,2,0,4:T(4,128)S(1)}, u32[]{:S(2)}, u32[]{:S(2)}) async-start(f32[2,96,4,4,16,4]{1,5,3,2,0,4:T(4,128)} %copy.343), calls=%async_computation.2 | async-start | bytes 2097152 | tf_op jit(solution)/shard_map/all_to_all | solution.py:138
  75.6 0.8 maximum_bitcast_fusion.11
  76.7 23.6 %all-to-all-done.2 = f32[2,96,4,4,16,4]{1,5,3,2,0,4:T(4,128)S(1)} async-done(((f32[2,96,4,4,16,4]{1,5,3,2,0,4:T(4,128)}), f32[2,96,4,4,16,4]{1,5,3,2,0,4:T(4,128)S(1)}, u32[]{:S(2)}, u32[]{:S(2)}) %all-to-all-start.2) | async-done | bytes 786464 | tf_op jit(solution)/shard_map/all_to_all | solution.py:138
  100.3 1.6 copy.344
  101.9 3.8 %all-to-all-start.3 = ((f32[2,96,4,4,16,4]{1,4,5,2,0,3:T(8,128)}), f32[2,96,4,4,16,4]{1,4,5,2,0,3:T(8,128)S(1)}, u32[]{:S(2)}, u32[]{:S(2)}) async-start(f32[2,96,4,4,16,4]{1,4,5,2,0,3:T(8,128)} %copy.344), calls=%async_computation.3 | async-start | bytes 2097152 | tf_op jit(solution)/shard_map/all_to_all | solution.py:139
  105.8 0.9 fusion.78
  106.9 1.2 fusion.5
  108.4 0.9 fusion.4
  109.3 10.9 %all-to-all-done.3 = f32[2,96,4,4,16,4]{1,4,5,2,0,3:T(8,128)S(1)} async-done(((f32[2,96,4,4,16,4]{1,4,5,2,0,3:T(8,128)}), f32[2,96,4,4,16,4]{1,4,5,2,0,3:T(8,128)S(1)}, u32[]{:S(2)}, u32[]{:S(2)}) %all-to-all-start.3) | async-done | bytes 786464 | tf_op jit(solution)/shard_map/all_to_all | solution.py:139
  120.9 1.1 fusion.106
  125.2 0.9 fusion.48
  126.1 0.9 fusion.50
  127.0 1.0 fusion.47
  128.0 1.1 fusion.46
  129.5 0.8 copy.367
  130.9 2.3 convolution_bitcast_fusion
  133.2 1.5 copy.369
  134.6 2.1 copy.370
  136.7 6.4 %concatenate.16 = f32[4,16,3072]{1,0,2:T(4,128)} reshape(f32[64,2,2,96,4,2]{0,5,4,3,2,1:T(2,128)} %copy.370) | data formatting | bytes 1572864 | tf_op jit(solution)/shard_map/concatenate | solution.py:199
  145.6 1.5 copy.380
  147.1 13.2 %pad_maximum_fusion = f32[4,16,4236]{1,0,2:T(4,128)} fusion(f32[4,16,1164]{1,0,2:T(4,128)S(1)} %copy.380, f32[4,16,3072]{1,0,2:T(4,128)} %concatenate.16), kind=kLoop, calls=%fused_computation | loop fusion | flops 271104 | bytes 2168832 | tf_op jit(solution)/shard_map/concatenate | solution.py:199
  160.3 6.8 %copy.381 = f32[4,16,4236]{2,0,1:T(4,128)S(1)} copy(f32[4,16,4236]{1,0,2:T(4,128)} %pad_maximum_fusion) | data formatting | bytes 2168832 | tf_op jit(solution)/shard_map/concatenate | solution.py:199
  167.1 34.5 %all_to_all.40 = f32[4,16,4236]{2,0,1:T(4,128)S(1)} all-to-all(f32[4,16,4236]{2,0,1:T(4,128)S(1)} %copy.381), channel_id=1, replica_groups=mesh['pipe'=8,'sx'=4,'sy'=8,'sc'=2] {'sy','sc'}, dimensions={1} | all-to-all | bytes 2168832 | tf_op jit(solution)/shard_map/all_to_all | solution.py:138
  201.8 18.2 %all_to_all.41 = f32[4,16,4236]{2,1,0:T(8,128)S(1)} all-to-all(f32[4,16,4236]{2,1,0:T(8,128)S(1)} %copy.382), channel_id=1, replica_groups=mesh['pipe'=8,'sx'=4,'sy'=8,'sc'=2] {'sx'}, dimensions={0} | all-to-all | bytes 2168832 | tf_op jit(solution)/shard_map/all_to_all | solution.py:139
  220.8 4.3 %all-to-all-start.6 = ((f32[4,16,1164]{2,0,1:T(4,128)}), f32[4,16,1164]{2,0,1:T(4,128)S(1)}, u32[]{:S(2)}, u32[]{:S(2)}) async-start(f32[4,16,1164]{2,0,1:T(4,128)} %reshape.599), calls=%async_computation.6 | async-start | bytes 655360 | tf_op jit(solution)/shard_map/all_to_all | solution.py:138
  225.1 1.8 multiply_negate_fusion
  227.4 2.0 copy.384
  229.4 3.2 %fusion.12 = f32[2,96,4,512,1]{3,1,0,2,4:T(8,128)S(1)} fusion(f32[2,2,96,4,128]{2,4,3,1,0:T(8,128)} %bitcast.228, f32[1,512,128]{2,1,0:T(8,128)} %get-tuple-element.76, f32[1,512,128]{2,1,0:T(8,128)} %get-tuple-element.77), kind=kOutput, calls=%fused_computation.28 | convolution fusion | flops 604110848 | bytes 2883584 | tf_op jit(solution)/shard_map/piblk,pnk->ibln/dot_general | solution.py:69
  232.7 5.5 %all-to-all-done.6 = f32[4,16,1164]{2,0,1:T(4,128)S(1)} async-done(((f32[4,16,1164]{2,0,1:T(4,128)}), f32[4,16,1164]{2,0,1:T(4,128)S(1)}, u32[]{:S(2)}, u32[]{:S(2)}) %all-to-all-start.6) | async-done | bytes 298016 | tf_op jit(solution)/shard_map/all_to_all | solution.py:138
  238.1 0.8 copy.386
  238.9 3.5 %all-to-all-start.7 = ((f32[4,16,1164]{2,1,0:T(8,128)}), f32[4,16,1164]{2,1,0:T(8,128)S(1)}, u32[]{:S(2)}, u32[]{:S(2)}) async-start(f32[4,16,1164]{2,1,0:T(8,128)} %copy.386), calls=%async_computation.7 | async-start | bytes 655360 | tf_op jit(solution)/shard_map/all_to_all | solution.py:139
  242.4 1.5 fusion.16
  243.9 1.5 copy.387
  245.4 4.7 %all-to-all-done.7 = f32[4,16,1164]{2,1,0:T(8,128)S(1)} async-done(((f32[4,16,1164]{2,1,0:T(8,128)}), f32[4,16,1164]{2,1,0:T(8,128)S(1)}, u32[]{:S(2)}, u32[]{:S(2)}) %all-to-all-start.7) | async-done | bytes 298016 | tf_op jit(solution)/shard_map/all_to_all | solution.py:139
  250.9 0.8 broadcast_in_dim_reshape.8
  (99 shorter events, 17.2 us)
Async XLA Ops:
  0.6 2.0 copy-start
  3.6 11.6 %copy-start.1 = (bf16[1,2,96,4,512]{4,3,2,1,0:T(4,128)(2,1)S(1)}, bf16[1,2,96,4,512]{4,3,2,1,0:T(4,128)(2,1)}, u32[]{:S(2)}) copy-start(bf16[1,2,96,4,512]{4,3,2,1,0:T(4,128)(2,1)} %param.7) | copy-start | bytes 2359300
  4.9 38.3 %all-to-all-start = ((f32[2,96,4,4,16,4]{1,5,3,2,0,4:T(4,128)}), f32[2,96,4,4,16,4]{1,5,3,2,0,4:T(4,128)S(1)}, u32[]{:S(2)}, u32[]{:S(2)}) async-start(f32[2,96,4,4,16,4]{1,5,3,2,0,4:T(4,128)} %copy.338), calls=%async_computation | async-start | bytes 2097152 | tf_op jit(solution)/shard_map/all_to_all | solution.py:138
  16.2 48.1 %collective-permute-start = (bf16[2,96,4,512]{3,1,2,0:T(8,128)(2,1)}, bf16[2,96,4,512]{3,1,2,0:T(8,128)(2,1)}, u32[]{:S(2)}, u32[]{:S(2)}) collective-permute-start(bf16[2,96,4,512]{3,1,2,0:T(8,128)(2,1)} %bitcast.206), channel_id=1, source_target_pairs={{64,0},{128,64},{192,128},{256,192},{320,256},{384,320},{448,384},... | collective-permute-start | bytes 2359304 | tf_op jit(solution)/shard_map/ppermute | solution.py:20
  44.4 18.2 %all-to-all-start.1 = ((f32[2,96,4,4,16,4]{1,5,4,2,0,3:T(4,128)}), f32[2,96,4,4,16,4]{1,5,4,2,0,3:T(4,128)S(1)}, u32[]{:S(2)}, u32[]{:S(2)}) async-start(f32[2,96,4,4,16,4]{1,5,4,2,0,3:T(4,128)} %copy.339), calls=%async_computation.1 | async-start | bytes 2097152 | tf_op jit(solution)/shard_map/all_to_all | solution.py:139
  49.5 14.7 %copy-start.6 = (f32[1,128,2,256]{3,1,2,0:T(8,128)}, f32[1,128,2,256]{3,1,2,0:T(8,128)S(1)}, u32[]{:S(2)}) copy-start(f32[1,128,2,256]{3,1,2,0:T(8,128)S(1)} %get-tuple-element.63) | copy-start | bytes 786436
  62.6 1.7 copy-start.8
  67.8 4.6 %copy-start.18 = (s32[1,2]{1,0:T(1,128)S(1)}, s32[1,2]{1,0:T(1,128)}, u32[]{:S(2)}) copy-start(s32[1,2]{1,0:T(1,128)} %param.8) | copy-start | bytes 28
  67.8 32.5 %all-to-all-start.2 = ((f32[2,96,4,4,16,4]{1,5,3,2,0,4:T(4,128)}), f32[2,96,4,4,16,4]{1,5,3,2,0,4:T(4,128)S(1)}, u32[]{:S(2)}, u32[]{:S(2)}) async-start(f32[2,96,4,4,16,4]{1,5,3,2,0,4:T(4,128)} %copy.343), calls=%async_computation.2 | async-start | bytes 2097152 | tf_op jit(solution)/shard_map/all_to_all | solution.py:138
  101.9 3.8 %copy-start.5 = (f32[1,2,2,96,96]{4,3,2,1,0:T(8,128)S(1)}, f32[1,2,2,96,96]{4,3,2,1,0:T(8,128)}, u32[]{:S(2)}) copy-start(f32[1,2,2,96,96]{4,3,2,1,0:T(8,128)} %param.9) | copy-start | bytes 442372
  101.9 18.3 %all-to-all-start.3 = ((f32[2,96,4,4,16,4]{1,4,5,2,0,3:T(8,128)}), f32[2,96,4,4,16,4]{1,4,5,2,0,3:T(8,128)S(1)}, u32[]{:S(2)}, u32[]{:S(2)}) async-start(f32[2,96,4,4,16,4]{1,4,5,2,0,3:T(8,128)} %copy.344), calls=%async_computation.3 | async-start | bytes 2097152 | tf_op jit(solution)/shard_map/all_to_all | solution.py:139
  108.1 12.8 %copy-start.7 = (f32[1,128,2,256]{3,1,2,0:T(8,128)S(1)}, f32[1,128,2,256]{3,1,2,0:T(8,128)}, u32[]{:S(2)}) copy-start(f32[1,128,2,256]{3,1,2,0:T(8,128)} %copy-done.6) | copy-start | bytes 786436
  122.0 0.9 copy-start.12
  122.2 1.9 copy-start.11
  122.2 1.9 copy-start.17
  124.6 4.5 %copy-start.3 = (f32[2,2,96,256]{3,2,1,0:T(8,128)}, f32[2,2,96,256]{3,2,1,0:T(8,128)S(1)}, u32[]{:S(2)}) copy-start(f32[2,2,96,256]{3,2,1,0:T(8,128)S(1)} %get-tuple-element.53) | copy-start | bytes 1179652
  129.1 1.8 copy-start.9
  129.1 1.8 copy-start.10
  136.7 6.4 %copy-start.16 = (f32[2,96,96]{2,1,0:T(8,128)S(1)}, f32[2,96,96]{2,1,0:T(8,128)}, u32[]{:S(2)}) copy-start(f32[2,96,96]{2,1,0:T(8,128)} %fusion.48) | copy-start | bytes 221188
  136.7 6.6 %copy-start.15 = (f32[2,96,96]{2,1,0:T(8,128)S(1)}, f32[2,96,96]{2,1,0:T(8,128)}, u32[]{:S(2)}) copy-start(f32[2,96,96]{2,1,0:T(8,128)} %fusion.50) | copy-start | bytes 221188
  143.1 1.0 copy-start.4
  143.1 1.0 copy-start.14
  143.1 1.4 copy-start.13
  220.8 17.4 %all-to-all-start.6 = ((f32[4,16,1164]{2,0,1:T(4,128)}), f32[4,16,1164]{2,0,1:T(4,128)S(1)}, u32[]{:S(2)}, u32[]{:S(2)}) async-start(f32[4,16,1164]{2,0,1:T(4,128)} %reshape.599), calls=%async_computation.6 | async-start | bytes 655360 | tf_op jit(solution)/shard_map/all_to_all | solution.py:138
  229.4 13.0 %copy-start.2 = (bf16[1,2,96,4,512]{4,3,2,1,0:T(4,128)(2,1)S(1)}, bf16[1,2,96,4,512]{4,3,2,1,0:T(4,128)(2,1)}, u32[]{:S(2)}) copy-start(bf16[1,2,96,4,512]{4,3,2,1,0:T(4,128)(2,1)} %param.7) | copy-start | bytes 2359300
  238.9 11.2 %all-to-all-start.7 = ((f32[4,16,1164]{2,1,0:T(8,128)}), f32[4,16,1164]{2,1,0:T(8,128)S(1)}, u32[]{:S(2)}, u32[]{:S(2)}) async-start(f32[4,16,1164]{2,1,0:T(8,128)} %copy.386), calls=%async_computation.7 | async-start | bytes 655360 | tf_op jit(solution)/shard_map/all_to_all | solution.py:139

commit v5 on v3

--- a/solution.py
+++ b/solution.py
@@ -160,12 +160,11 @@
     lon_cos, lon_sin = lon_tables(LON, KEEP_LON)
     lat_cos, lat_sin = lat_tables(LAT, KEEP_LAT)
     table = lon_forward_table(lon_cos, lon_sin, ndev)
-    col_field = to_columns(lon_forward(field, table), ndev)
-    spectrum = lat_forward(col_field, lat_cos, lat_sin)
-    spectrum, received = lax.optimization_barrier((spectrum, received))
     upstream = jnp.where(section_index == last_section, own_grad, received)
-    col_grad = to_columns(lon_forward(upstream, table), ndev)
-    grad_spec = lat_forward(col_grad, lat_cos, lat_sin)
+    both = jnp.concatenate([lon_forward(field, table), lon_forward(upstream, table)])
+    columns = to_columns(both, ndev)
+    spectrum = lat_forward(columns[:nblocks], lat_cos, lat_sin)
+    grad_spec = lat_forward(columns[nblocks:], lat_cos, lat_sin)
     share = KEEP_LON // ndev
     signed = jnp.arange(2 * KEEP_LAT, dtype=jnp.int32) - KEEP_LAT
     wavenumber = lax.axis_index("space") * share + jnp.arange(share, dtype=jnp.int32)

time: 169 us -> 181 us (1.071)
  waiting for transfers between devices: 80.3 us -> 96.3 us
  starting transfers between devices: 32 us -> 29.9 us
    ppermute x1, waiting for transfers between devices: 0.01 us -> 13.3 us  [from_behind(): return lax.ppermute(block, axis, route)]
    dot_general x2 -> x0, local copies, waits for them, and re-layouts: 2.75 us -> none  [lon_forward(): return jnp.einsum('ibln,nc->iblc', values, table, precision=HIGHEST)]
    dot_general x8, matrix products: 2.59 us -> 5.15 us  [outer(): return jnp.einsum('kim,kjm->kij', first, second, precision=HIGHEST)]
    concatenate x0 -> x1, local copies, waits for them, and re-layouts: none -> 1.9 us  [shards(): jnp.concatenate([lon_forward(field, table), lon_forward(upstream, table)])]
    all_to_all x2 -> x1, waiting for transfers between devices: 44.9 us -> 46.5 us  [to_columns(): lax.all_to_all(spectrum, 'space', split_axis=3, concat_axis=2, tiled=True)]
    unnamed x31 -> x45, local copies, waits for them, and re-layouts: 3.6 us -> 5.11 us
    all_to_all x2 -> x1, starting transfers between devices: 18.1 us -> 16.6 us  [to_columns(): lax.all_to_all(spectrum, 'space', split_axis=3, concat_axis=2, tiled=True)]
  transfers between devices with their start and end apart: 5 -> 4, of which waited for: 4 -> 4; matrix products, arithmetic and copies ran while one was open for 12% -> 7% of each run, Pallas kernels for 0% -> 0%
where the time goes in v5:
time: 181 us; the launch traced here: 180 us
  waiting for transfers between devices  96.3 us (53%)
  starting transfers between devices  29.9 us (17%)
  local copies, waits for them, and re-layouts  24.9 us (14%)
  matrix products  17.6 us (10%)
  other arithmetic  9.91 us (5%)
  between operations  1.97 us (1%)
    all_to_all x1, waiting for transfers between devices, to_columns(): lax.all_to_all(spectrum, 'space', split_axis=3, concat_axis=2, tiled=True)  46.5 us
    all_to_all x1, waiting for transfers between devices, shards(): lax.all_to_all(jnp.concatenate([back, pieces], axis=1), 'space', split_ax...  28.2 us
    all_to_all x1, starting transfers between devices, to_columns(): lax.all_to_all(spectrum, 'space', split_axis=3, concat_axis=2, tiled=True)  16.6 us
    ppermute x1, waiting for transfers between devices, from_behind(): return lax.ppermute(block, axis, route)  13.3 us
    all_to_all x1, waiting for transfers between devices, shards(): lax.all_to_all(spread, 'space', split_axis=0, concat_axis=0, tiled=True)  8.33 us
    all_to_all x1, starting transfers between devices, shards(): lax.all_to_all(spread, 'space', split_axis=0, concat_axis=0, tiled=True)  6.19 us
    all_to_all x1, starting transfers between devices, shards(): lax.all_to_all(jnp.concatenate([back, pieces], axis=1), 'space', split_ax...  5.81 us
    dot_general x8, matrix products, outer(): return jnp.einsum('kim,kjm->kij', first, second, precision=HIGHEST)  5.15 us
  transfers between devices with their start and end apart: 4, of which 4 were waited for; matrix products, arithmetic and copies ran while one was open for 7% of the time, Pallas kernels for 0%

profile of v5, /device:TPU:1, one launch (start us, length us, event | category | flops | bytes accessed | tf_op | source)
XLA Modules:
  0.0 180.5 jit_solution(775735935861660817)
XLA Ops:
  0.6 2.2 %copy.324 = bf16[1,2,96,4,512]{4,2,3,1,0:T(8,128)(2,1)} copy(bf16[1,2,96,4,512]{4,3,2,1,0:T(4,128)(2,1)} %param.7) | data formatting | bytes 1572864 | tf_op args[1]
  2.9 1.3 collective-permute-start
  4.2 1.1 cosine_multiply_fusion.1
  6.2 0.6 convolution_bitcast_fusion.1
  6.8 13.3 %collective-permute-done = bf16[2,96,4,512]{3,1,2,0:T(8,128)(2,1)S(1)} collective-permute-done((bf16[2,96,4,512]{3,1,2,0:T(8,128)(2,1)}, bf16[2,96,4,512]{3,1,2,0:T(8,128)(2,1)S(1)}, u32[]{:S(2)}, u32[]{:S(2)}) %collective-permute-start) | collective-permute-done | bytes 786464 | tf_op jit(solution)/shard_map/ppermute | solution.py:20
  20.1 0.9 copy-done.5
  20.9 0.6 fusion.22
  21.7 1.9 %copy.215 = f32[4,96,4,256]{1,2,0,3:T(4,128)} copy(f32[4,96,4,256]{3,1,2,0:T(8,128)S(1)} %pad_maximum_fusion) | data formatting | bytes 3145728 | tf_op jit(solution)/shard_map/concatenate | solution.py:164
  23.6 16.6 %all-to-all-start = ((f32[4,96,4,256]{1,2,0,3:T(4,128)}), f32[4,96,4,256]{1,2,0,3:T(4,128)S(1)}, u32[]{:S(2)}, u32[]{:S(2)}) async-start(f32[4,96,4,256]{1,2,0,3:T(4,128)} %copy.215), calls=%async_computation | async-start | bytes 4194304 | tf_op jit(solution)/shard_map/all_to_all | solution.py:135
  40.2 0.6 fusion.105
  41.4 0.7 compare_and_fusion
  42.1 0.7 fusion.93
  42.8 0.6 sine_multiply_fusion.1
  43.4 0.6 fusion.92
  44.0 0.8 maximum_bitcast_fusion.12
  44.9 46.5 %all-to-all-done = f32[4,96,4,256]{1,2,0,3:T(4,128)S(1)} async-done(((f32[4,96,4,256]{1,2,0,3:T(4,128)}), f32[4,96,4,256]{1,2,0,3:T(4,128)S(1)}, u32[]{:S(2)}, u32[]{:S(2)}) %all-to-all-start) | async-done | bytes 1572896 | tf_op jit(solution)/shard_map/all_to_all | solution.py:135
  91.4 0.7 copy.216
  92.2 0.7 copy.227
  92.9 1.0 convolution_bitcast_fusion.2
  94.0 0.7 fusion.103
  94.8 1.0 fusion.77
  95.8 0.9 fusion.71
  96.7 0.7 copy.217
  97.4 1.1 fusion.106
  102.0 0.9 fusion.47
  102.8 0.9 fusion.49
  103.7 1.1 fusion.46
  104.8 1.1 fusion.45
  107.0 1.4 convolution_bitcast_fusion
  108.3 1.5 copy.243
  109.8 2.1 %copy.244 = f32[64,2,2,96,4,2]{0,5,4,3,2,1:T(2,128)} copy(f32[64,2,2,96,4,2]{3,4,0,5,2,1:T(4,128)S(1)} %bitcast.229) | data formatting | bytes 1572864 | tf_op jit(solution)/shard_map/transpose | solution.py:186
  114.7 1.6 maximum_bitcast_fusion
  116.3 2.7 %copy.255 = f32[64,1,4236]{2,1,0:T(1,128)} copy(f32[64,1,4236]{0,2,1:T(8,128)S(1)} %maximum_bitcast_fusion) | data formatting | bytes 2168832 | tf_op jit(solution)/shard_map/all_to_all | solution.py:187
  119.0 5.8 %all-to-all-start.1 = ((f32[64,1,4236]{2,1,0:T(1,128)}), f32[64,1,4236]{2,1,0:T(1,128)S(1)}, u32[]{:S(2)}, u32[]{:S(2)}) async-start(f32[64,1,4236]{2,1,0:T(1,128)} %copy.255), calls=%async_computation.1 | async-start | bytes 2228224 | tf_op jit(solution)/shard_map/all_to_all | solution.py:187
  124.8 1.8 multiply_negate_fusion
  126.6 28.2 %all-to-all-done.1 = f32[64,1,4236]{2,1,0:T(1,128)S(1)} async-done(((f32[64,1,4236]{2,1,0:T(1,128)}), f32[64,1,4236]{2,1,0:T(1,128)S(1)}, u32[]{:S(2)}, u32[]{:S(2)}) %all-to-all-start.1) | async-done | bytes 1084448 | tf_op jit(solution)/shard_map/all_to_all | solution.py:187
  154.9 0.5 copy.256
  155.4 0.9 copy.257
  156.3 0.9 broadcast_in_dim.15
  157.2 6.2 %all-to-all-start.2 = ((f32[64,1,1164]{2,1,0:T(1,128)}), f32[64,1,1164]{2,1,0:T(1,128)S(1)}, u32[]{:S(2)}, u32[]{:S(2)}) async-start(f32[64,1,1164]{2,1,0:T(1,128)} %broadcast_in_dim.15), calls=%async_computation.2 | async-start | bytes 655360 | tf_op jit(solution)/shard_map/all_to_all | solution.py:194
  163.4 3.0 %fusion.12 = f32[2,96,4,512,1]{3,1,0,2,4:T(8,128)S(1)} fusion(f32[2,2,96,4,128]{2,4,3,1,0:T(8,128)S(1)} %bitcast.228, f32[1,512,128]{2,1,0:T(8,128)} %get-tuple-element.64, f32[1,512,128]{2,1,0:T(8,128)} %get-tuple-element.65), kind=kOutput, calls=%fused_computation.30 | convolution fusion | flops 604110848 | bytes 2883584 | tf_op jit(solution)/shard_map/piblk,pnk->ibln/dot_general | solution.py:69
  166.8 1.5 copy.259
  168.3 8.3 %all-to-all-done.2 = f32[64,1,1164]{2,1,0:T(1,128)S(1)} async-done(((f32[64,1,1164]{2,1,0:T(1,128)}), f32[64,1,1164]{2,1,0:T(1,128)S(1)}, u32[]{:S(2)}, u32[]{:S(2)}) %all-to-all-start.2) | async-done | bytes 298016 | tf_op jit(solution)/shard_map/all_to_all | solution.py:194
  176.6 0.9 multiply_reduce_fusion
  177.8 0.6 mul.470
  178.3 0.8 broadcast_in_dim_reshape.8
  179.1 0.8 broadcast_in_dim_reshape.9
  179.9 0.6 fusion.101
  (91 shorter events, 9.2 us)
Async XLA Ops:
  0.6 5.5 %copy-start = (bf16[1,2,96,4,512]{4,3,2,1,0:T(4,128)(2,1)S(1)}, bf16[1,2,96,4,512]{4,3,2,1,0:T(4,128)(2,1)}, u32[]{:S(2)}) copy-start(bf16[1,2,96,4,512]{4,3,2,1,0:T(4,128)(2,1)} %param.6) | copy-start | bytes 2359300
  2.9 17.2 %collective-permute-start = (bf16[2,96,4,512]{3,1,2,0:T(8,128)(2,1)}, bf16[2,96,4,512]{3,1,2,0:T(8,128)(2,1)S(1)}, u32[]{:S(2)}, u32[]{:S(2)}) collective-permute-start(bf16[2,96,4,512]{3,1,2,0:T(8,128)(2,1)} %bitcast.205), channel_id=1, source_target_pairs={{64,0},{128,64},{192,128},{256,192},{320,256},{384,320},{448,384},... | collective-permute-start | bytes 2359304 | tf_op jit(solution)/shard_map/ppermute | solution.py:20
  5.8 15.2 %copy-start.1 = (bf16[1,2,96,4,512]{4,3,2,1,0:T(4,128)(2,1)S(1)}, bf16[1,2,96,4,512]{4,3,2,1,0:T(4,128)(2,1)}, u32[]{:S(2)}) copy-start(bf16[1,2,96,4,512]{4,3,2,1,0:T(4,128)(2,1)} %param.7) | copy-start | bytes 2359300
  20.1 0.9 copy-start.5
  23.6 16.6 %copy-start.20 = (s32[1,2]{1,0:T(1,128)S(1)}, s32[1,2]{1,0:T(1,128)}, u32[]{:S(2)}) copy-start(s32[1,2]{1,0:T(1,128)} %param.8) | copy-start | bytes 28
  23.6 67.8 %all-to-all-start = ((f32[4,96,4,256]{1,2,0,3:T(4,128)}), f32[4,96,4,256]{1,2,0,3:T(4,128)S(1)}, u32[]{:S(2)}, u32[]{:S(2)}) async-start(f32[4,96,4,256]{1,2,0,3:T(4,128)} %copy.215), calls=%async_computation | async-start | bytes 4194304 | tf_op jit(solution)/shard_map/all_to_all | solution.py:135
  92.9 1.9 %copy-start.7 = (f32[1,2,2,96,96]{4,3,2,1,0:T(8,128)S(1)}, f32[1,2,2,96,96]{4,3,2,1,0:T(8,128)}, u32[]{:S(2)}) copy-start(f32[1,2,2,96,96]{4,3,2,1,0:T(8,128)} %param.9) | copy-start | bytes 442372
  97.4 1.5 copy-start.13
  98.5 1.0 copy-start.14
  98.7 1.4 copy-start.10
  98.9 1.4 copy-start.12
  99.2 1.4 copy-start.11
  99.5 1.4 copy-start.19
  101.4 4.5 %copy-start.3 = (f32[2,2,96,256]{3,2,1,0:T(8,128)}, f32[2,2,96,256]{3,2,1,0:T(8,128)S(1)}, u32[]{:S(2)}) copy-start(f32[2,2,96,256]{3,2,1,0:T(8,128)S(1)} %get-tuple-element.41) | copy-start | bytes 1179652
  105.8 1.1 copy-start.8
  105.8 1.1 copy-start.9
  109.8 2.2 %copy-start.18 = (f32[2,96,96]{2,1,0:T(8,128)S(1)}, f32[2,96,96]{2,1,0:T(8,128)}, u32[]{:S(2)}) copy-start(f32[2,96,96]{2,1,0:T(8,128)} %fusion.47) | copy-start | bytes 221188
  109.8 2.4 %copy-start.17 = (f32[2,96,96]{2,1,0:T(8,128)S(1)}, f32[2,96,96]{2,1,0:T(8,128)}, u32[]{:S(2)}) copy-start(f32[2,96,96]{2,1,0:T(8,128)} %fusion.49) | copy-start | bytes 221188
  112.0 1.0 copy-start.4
  112.0 1.0 copy-start.16
  112.0 1.4 copy-start.15
  119.0 35.8 %all-to-all-start.1 = ((f32[64,1,4236]{2,1,0:T(1,128)}), f32[64,1,4236]{2,1,0:T(1,128)S(1)}, u32[]{:S(2)}, u32[]{:S(2)}) async-start(f32[64,1,4236]{2,1,0:T(1,128)} %copy.255), calls=%async_computation.1 | async-start | bytes 2228224 | tf_op jit(solution)/shard_map/all_to_all | solution.py:187
  157.2 19.5 %all-to-all-start.2 = ((f32[64,1,1164]{2,1,0:T(1,128)}), f32[64,1,1164]{2,1,0:T(1,128)S(1)}, u32[]{:S(2)}, u32[]{:S(2)}) async-start(f32[64,1,1164]{2,1,0:T(1,128)} %broadcast_in_dim.15), calls=%async_computation.2 | async-start | bytes 655360 | tf_op jit(solution)/shard_map/all_to_all | solution.py:194
  163.4 3.0 %copy-start.2 = (bf16[1,2,96,4,512]{4,3,2,1,0:T(4,128)(2,1)S(1)}, bf16[1,2,96,4,512]{4,3,2,1,0:T(4,128)(2,1)}, u32[]{:S(2)}) copy-start(bf16[1,2,96,4,512]{4,3,2,1,0:T(4,128)(2,1)} %param.7) | copy-start | bytes 2359300
  163.4 3.0 %copy-start.6 = (bf16[2,96,4,512]{3,1,2,0:T(8,128)(2,1)S(1)}, bf16[2,96,4,512]{3,1,2,0:T(8,128)(2,1)}, u32[]{:S(2)}) copy-start(bf16[2,96,4,512]{3,1,2,0:T(8,128)(2,1)} %copy-done.5) | copy-start | bytes 2359300

commit v6 on v2

--- a/solution.py
+++ b/solution.py
@@ -11,7 +11,7 @@
 KEEP_LAT = 64
 
 
-HIGHEST = lax.Precision.HIGHEST
+HIGHEST = lax.Precision.HIGH
 
 
 def from_behind(block, axis, distance):
@@ -157,38 +157,65 @@
     received = from_behind(own_grad, "pipe", -1)
     section_index = lax.axis_index("pipe")
     last_section = lax.axis_size("pipe") - 1
-    upstream = jnp.where(section_index == last_section, own_grad, received)
     lon_cos, lon_sin = lon_tables(LON, KEEP_LON)
     lat_cos, lat_sin = lat_tables(LAT, KEEP_LAT)
     table = lon_forward_table(lon_cos, lon_sin, ndev)
     col_field = to_columns(lon_forward(field, table), ndev)
-    col_grad = to_columns(lon_forward(upstream, table), ndev)
     spectrum = lat_forward(col_field, lat_cos, lat_sin)
-    grad_spec = lat_forward(col_grad, lat_cos, lat_sin)
+    spectrum, received = lax.optimization_barrier((spectrum, received))
+    upstream = jnp.where(section_index == last_section, own_grad, received)
     share = KEEP_LON // ndev
     signed = jnp.arange(2 * KEEP_LAT, dtype=jnp.int32) - KEEP_LAT
     wavenumber = lax.axis_index("space") * share + jnp.arange(share, dtype=jnp.int32)
     weight = mode_mask(signed, wavenumber, kept_modes[0, 0], kept_modes[0, 1])
-    grad_spec = grad_spec * weight
-    spectrum = spectrum.reshape(2, nblocks, width, -1)
-    grad_spec = grad_spec.reshape(2, nblocks, width, -1)
-    grad_modes, grad_w_in, grad_b_in, grad_w_out, grad_b_out = backprop(
-        spectrum, grad_spec, weight_in[0], bias_in[0], weight_out[0]
-    )
-    grad_modes = grad_modes.reshape(2, nblocks, width, 2 * KEEP_LAT, share)
-    lat_back = lat_inverse(grad_modes, lat_cos, lat_sin)
-    rows_back = lax.all_to_all(lat_back, "space", split_axis=3, concat_axis=4, tiled=True)
-    inverse = lon_inverse(rows_back, lon_cos, lon_sin)
-    parts = (grad_w_in, grad_b_in, grad_w_out, grad_b_out)
-    flat = sum_over(jnp.concatenate([p.reshape(-1) for p in parts]), "space")
+    rows = LAT // ndev
     factor = 1.0 / math.sqrt(2 * KEEP_LAT * KEEP_LON)
-    flat = flat * factor
-    sums = []
-    start = 0
-    for p in parts:
-        sums.append(flat[start:start + p.size].reshape(p.shape)[None])
-        start += p.size
-    grad_field = (upstream.astype(jnp.float32) + inverse).astype(jnp.bfloat16)
+    fields = []
+    mine = []
+    layouts = []
+    for b in range(nblocks):
+        one = slice(b, b + 1)
+        col_grad = to_columns(lon_forward(upstream[one], table), ndev)
+        grad_spec = lat_forward(col_grad, lat_cos, lat_sin) * weight
+        grad_modes, grad_w_in, grad_b_in, grad_w_out, grad_b_out = backprop(
+            spectrum[:, one].reshape(2, 1, width, -1),
+            grad_spec.reshape(2, 1, width, -1),
+            weight_in[0][:, one],
+            bias_in[0][:, one],
+            weight_out[0][:, one],
+        )
+        grad_modes = grad_modes.reshape(2, 1, width, 2 * KEEP_LAT, share)
+        lat_back = lat_inverse(grad_modes, lat_cos, lat_sin)
+        parts = (grad_w_in, grad_b_in, grad_w_out, grad_b_out)
+        flat = jnp.concatenate([p.reshape(-1) for p in parts])
+        pad = (-flat.shape[0]) % ndev
+        pieces = jnp.pad(flat, (0, pad)).reshape(ndev, -1)
+        back = lat_back.reshape(2, 1, width, ndev, rows, share)
+        back = jnp.moveaxis(back, 3, 0).reshape(ndev, -1)
+        moved = lax.all_to_all(
+            jnp.concatenate([back, pieces], axis=1), "space", split_axis=0, concat_axis=0, tiled=True
+        )
+        rows_back = moved[:, : back.shape[1]].reshape(ndev, 2, 1, width, rows, share)
+        rows_back = jnp.moveaxis(rows_back, 0, 4).reshape(2, 1, width, rows, ndev * share)
+        mine.append(jnp.sum(moved[:, back.shape[1]:], axis=0))
+        layouts.append(([p.shape for p in parts], flat.shape[0]))
+        inverse = lon_inverse(rows_back, lon_cos, lon_sin)
+        fields.append((upstream[one].astype(jnp.float32) + inverse).astype(jnp.bfloat16))
+    joined = jnp.concatenate(mine)
+    spread = jnp.broadcast_to(joined[None], (ndev, joined.shape[0]))
+    full = lax.all_to_all(spread, "space", split_axis=0, concat_axis=0, tiled=True) * factor
+    width_b = joined.shape[0] // nblocks
+    grads = [[], [], [], []]
+    for b in range(nblocks):
+        shapes, size = layouts[b]
+        flat = full[:, b * width_b:(b + 1) * width_b].reshape(-1)[:size]
+        start = 0
+        for n, shape in enumerate(shapes):
+            count = math.prod(shape)
+            grads[n].append(flat[start:start + count].reshape(shape))
+            start += count
+    sums = [jnp.concatenate(g, axis=1)[None] for g in grads]
+    grad_field = jnp.concatenate(fields)
     return (grad_field[None], *sums)
 
 

time: 185 us -> 205 us (1.11)
  local copies, waits for them, and re-layouts: 22.2 us -> 32.4 us
  other arithmetic: 10.8 us -> 14 us
  starting transfers between devices: 42.9 us -> 45.4 us
    all_to_all x2 -> x3, waiting for transfers between devices: 21.3 us -> 45.1 us  [to_columns(): lax.all_to_all(spectrum, 'space', split_axis=3, concat_axis=2, tiled=True)]
    ppermute x1, waiting for transfers between devices: 18 us -> 0.01 us  [from_behind(): return lax.ppermute(block, axis, route)]
    dot_general x12 -> x24, matrix products: 7.72 us -> 13.2 us  [block_product(): return jnp.einsum('kij,kjm->kim', weights, values, precision=HIGHEST)]
    all_to_all x3, waiting for transfers between devices: 40 us -> 35.7 us  [the longest x2 26.1 us: shards(): lax.all_to_all(jnp.concatenate([back, pieces], axis=1), 'space', split_ax...]
    transpose x0 -> x4, local copies, waits for them, and re-layouts: none -> 3.36 us  [the longest x2 1.8 us: shards(): back = jnp.moveaxis(back, 3, 0).reshape(ndev, -1)]
    reshape x4 -> x18, local copies, waits for them, and re-layouts: 0.67 us -> 3.68 us  [the longest x4 2.19 us: shards(): pieces = jnp.pad(flat, (0, pad)).reshape(ndev, -1)]
    unnamed x26 -> x51, local copies, waits for them, and re-layouts: 2.7 us -> 5.42 us
    all_to_all x0 -> x2, other arithmetic: none -> 2.34 us  [shards(): lax.all_to_all(jnp.concatenate([back, pieces], axis=1), 'space', split_ax...]
  transfers between devices with their start and end apart: 6 -> 7, of which waited for: 5 -> 6; matrix products, arithmetic and copies ran while one was open for 17% -> 16% of each run, Pallas kernels for 0% -> 0%
where the time goes in v6:
time: 205 us; the launch traced here: 204 us
  waiting for transfers between devices  80.8 us (39%)
  starting transfers between devices  45.4 us (22%)
  local copies, waits for them, and re-layouts  32.4 us (16%)
  matrix products  28.8 us (14%)
  other arithmetic  14 us (7%)
  between operations  2.34 us (1%)
    all_to_all x3, waiting for transfers between devices, to_columns(): lax.all_to_all(spectrum, 'space', split_axis=3, concat_axis=2, tiled=True)  45.1 us
    all_to_all x2, waiting for transfers between devices, shards(): lax.all_to_all(jnp.concatenate([back, pieces], axis=1), 'space', split_ax...  26.1 us
    all_to_all x3, starting transfers between devices, to_columns(): lax.all_to_all(spectrum, 'space', split_axis=3, concat_axis=2, tiled=True)  24.9 us
    dot_general x24, matrix products, block_product(): return jnp.einsum('kij,kjm->kim', weights, values, precision=HIGHEST)  13.2 us
    all_to_all x2, starting transfers between devices, shards(): lax.all_to_all(jnp.concatenate([back, pieces], axis=1), 'space', split_ax...  12.8 us
    all_to_all x1, waiting for transfers between devices, shards(): lax.all_to_all(spread, 'space', split_axis=0, concat_axis=0, tiled=True)  9.57 us
    dot_general x16, matrix products, outer(): return jnp.einsum('kim,kjm->kij', first, second, precision=HIGHEST)  7.54 us
    all_to_all x1, starting transfers between devices, shards(): lax.all_to_all(spread, 'space', split_axis=0, concat_axis=0, tiled=True)  6.41 us
  transfers between devices with their start and end apart: 7, of which 6 were waited for; matrix products, arithmetic and copies ran while one was open for 16% of the time, Pallas kernels for 0%

profile of v6, /device:TPU:1, one launch (start us, length us, event | category | flops | bytes accessed | tf_op | source)
XLA Modules:
  0.0 203.8 jit_solution(10967129670095068104)
XLA Ops:
  0.7 1.1 cosine_multiply_fusion.1
  3.2 1.3 copy.156
  4.5 11.9 %all-to-all-start = ((f32[2,96,4,256]{1,2,0,3:T(4,128)}), f32[2,96,4,256]{1,2,0,3:T(4,128)}, u32[]{:S(2)}, u32[]{:S(2)}) async-start(f32[2,96,4,256]{1,2,0,3:T(4,128)} %copy.156), calls=%async_computation | async-start | bytes 2097152 | tf_op jit(solution)/shard_map/all_to_all | solution.py:135
  16.5 1.0 copy.250
  17.5 1.3 collective-permute-start
  23.6 21.3 %all-to-all-done = f32[2,96,4,256]{1,2,0,3:T(4,128)} async-done(((f32[2,96,4,256]{1,2,0,3:T(4,128)}), f32[2,96,4,256]{1,2,0,3:T(4,128)}, u32[]{:S(2)}, u32[]{:S(2)}) %all-to-all-start) | async-done | bytes 786464 | tf_op jit(solution)/shard_map/all_to_all | solution.py:135
  45.0 1.4 copy.157
  47.1 1.0 convolution_bitcast_fusion.5
  49.2 1.5 broadcast_select_fusion
  50.8 1.2 convolution_bitcast_fusion.7
  51.9 1.2 convolution_bitcast_fusion.6
  53.3 2.0 copy.161
  55.3 6.4 %all-to-all-start.1 = ((f32[1,96,4,256]{1,2,0,3:T(4,128)}), f32[1,96,4,256]{1,2,0,3:T(4,128)}, u32[]{:S(2)}, u32[]{:S(2)}) async-start(f32[1,96,4,256]{1,2,0,3:T(4,128)} %copy.161), calls=%async_computation.1 | async-start | bytes 1048576 | tf_op jit(solution)/shard_map/all_to_all | solution.py:135
  61.9 2.0 copy.181
  67.8 11.2 %all-to-all-done.1 = f32[1,96,4,256]{1,2,0,3:T(4,128)} async-done(((f32[1,96,4,256]{1,2,0,3:T(4,128)}), f32[1,96,4,256]{1,2,0,3:T(4,128)}, u32[]{:S(2)}, u32[]{:S(2)}) %all-to-all-start.1) | async-done | bytes 393248 | tf_op jit(solution)/shard_map/all_to_all | solution.py:135
  79.0 6.5 %all-to-all-start.3 = ((f32[1,96,4,256]{1,2,0,3:T(4,128)}), f32[1,96,4,256]{1,2,0,3:T(4,128)}, u32[]{:S(2)}, u32[]{:S(2)}) async-start(f32[1,96,4,256]{1,2,0,3:T(4,128)} %copy.181), calls=%async_computation.3 | async-start | bytes 1048576 | tf_op jit(solution)/shard_map/all_to_all | solution.py:135
  85.5 1.1 copy.162
  88.1 0.9 fusion.16
  90.2 12.6 %all-to-all-done.3 = f32[1,96,4,256]{1,2,0,3:T(4,128)} async-done(((f32[1,96,4,256]{1,2,0,3:T(4,128)}), f32[1,96,4,256]{1,2,0,3:T(4,128)}, u32[]{:S(2)}, u32[]{:S(2)}) %all-to-all-start.3) | async-done | bytes 393248 | tf_op jit(solution)/shard_map/all_to_all | solution.py:135
  102.7 1.1 copy.182
  106.1 1.5 fusion.110
  108.3 0.9 fusion.83
  109.2 0.9 fusion.91
  110.1 0.9 fusion.89
  112.6 0.9 fusion.80
  113.5 0.9 fusion.81
  116.1 1.1 fusion.19
  118.6 1.1 fusion.6
  120.0 1.1 fusion.7
  121.9 1.2 copy.194
  123.1 1.3 maximum_bitcast_fusion.1
  124.4 1.6 copy.196
  126.0 6.6 %all-to-all-start.4 = ((f32[64,1,2118]{2,1,0:T(1,128)}), f32[64,1,2118]{2,1,0:T(1,128)}, u32[]{:S(2)}, u32[]{:S(2)}) async-start(f32[64,1,2118]{2,1,0:T(1,128)} %copy.196), calls=%async_computation.4 | async-start | bytes 1114112 | tf_op jit(solution)/shard_map/all_to_all | solution.py:195
  137.6 1.0 maximum_bitcast_fusion
  138.7 1.6 copy.176
  140.3 10.3 %all-to-all-done.4 = f32[64,1,2118]{2,1,0:T(1,128)} async-done(((f32[64,1,2118]{2,1,0:T(1,128)}), f32[64,1,2118]{2,1,0:T(1,128)}, u32[]{:S(2)}, u32[]{:S(2)}) %all-to-all-start.4) | async-done | bytes 542240 | tf_op jit(solution)/shard_map/all_to_all | solution.py:195
  150.6 6.2 %all-to-all-start.2 = ((f32[64,1,2118]{2,1,0:T(1,128)}), f32[64,1,2118]{2,1,0:T(1,128)S(1)}, u32[]{:S(2)}, u32[]{:S(2)}) async-start(f32[64,1,2118]{2,1,0:T(1,128)} %copy.176), calls=%async_computation.2 | async-start | bytes 1114112 | tf_op jit(solution)/shard_map/all_to_all | solution.py:195
  156.8 1.1 multiply_negate_fusion
  157.9 1.1 copy.251
  159.1 15.8 %all-to-all-done.2 = f32[64,1,2118]{2,1,0:T(1,128)S(1)} async-done(((f32[64,1,2118]{2,1,0:T(1,128)}), f32[64,1,2118]{2,1,0:T(1,128)S(1)}, u32[]{:S(2)}, u32[]{:S(2)}) %all-to-all-start.2) | async-done | bytes 542240 | tf_op jit(solution)/shard_map/all_to_all | solution.py:195
  176.0 1.1 copy.198
  177.9 0.9 broadcast_in_dim.23
  178.8 6.4 %all-to-all-start.5 = ((f32[64,1,1164]{2,1,0:T(1,128)}), f32[64,1,1164]{2,1,0:T(1,128)}, u32[]{:S(2)}, u32[]{:S(2)}) async-start(f32[64,1,1164]{2,1,0:T(1,128)} %broadcast_in_dim.23), calls=%async_computation.5 | async-start | bytes 655360 | tf_op jit(solution)/shard_map/all_to_all | solution.py:206
  185.3 1.0 fusion.2
  186.3 1.0 fusion.3
  187.4 1.5 copy.200
  188.9 9.6 %all-to-all-done.5 = f32[64,1,1164]{2,1,0:T(1,128)} async-done(((f32[64,1,1164]{2,1,0:T(1,128)}), f32[64,1,1164]{2,1,0:T(1,128)}, u32[]{:S(2)}, u32[]{:S(2)}) %all-to-all-start.5) | async-done | bytes 298016 | tf_op jit(solution)/shard_map/all_to_all | solution.py:206
  198.5 1.3 broadcast_multiply_fusion
  (169 shorter events, 33.4 us)
Async XLA Ops:
  0.6 2.0 copy-start
  4.5 12.0 %copy-start.1 = (bf16[1,2,96,4,512]{4,3,2,1,0:T(4,128)(2,1)S(1)}, bf16[1,2,96,4,512]{4,3,2,1,0:T(4,128)(2,1)}, u32[]{:S(2)}) copy-start(bf16[1,2,96,4,512]{4,3,2,1,0:T(4,128)(2,1)} %param.7) | copy-start | bytes 2359300
  4.5 40.4 %all-to-all-start = ((f32[2,96,4,256]{1,2,0,3:T(4,128)}), f32[2,96,4,256]{1,2,0,3:T(4,128)}, u32[]{:S(2)}, u32[]{:S(2)}) async-start(f32[2,96,4,256]{1,2,0,3:T(4,128)} %copy.156), calls=%async_computation | async-start | bytes 2097152 | tf_op jit(solution)/shard_map/all_to_all | solution.py:135
  16.5 2.3 %copy-start.21 = (s32[1,2]{1,0:T(1,128)S(1)}, s32[1,2]{1,0:T(1,128)}, u32[]{:S(2)}) copy-start(s32[1,2]{1,0:T(1,128)} %param.8) | copy-start | bytes 28
  17.5 30.6 %collective-permute-start = (bf16[2,96,4,512]{3,1,2,0:T(8,128)(2,1)}, bf16[2,96,4,512]{3,1,2,0:T(8,128)(2,1)S(1)}, u32[]{:S(2)}, u32[]{:S(2)}) collective-permute-start(bf16[2,96,4,512]{3,1,2,0:T(8,128)(2,1)} %bitcast.370), channel_id=1, source_target_pairs={{64,0},{128,64},{192,128},{256,192},{320,256},{384,320},{448,384},... | collective-permute-start | bytes 2359304 | tf_op jit(solution)/shard_map/ppermute | solution.py:20
  21.4 2.3 %copy-start.20 = (f32[1,2,2,96]{3,2,1,0:T(2,128)S(1)}, f32[1,2,2,96]{3,2,1,0:T(2,128)}, u32[]{:S(2)}) copy-start(f32[1,2,2,96]{3,2,1,0:T(2,128)} %param.10) | copy-start | bytes 4612
  47.1 1.2 copy-start.2
  48.1 0.9 copy-start.12
  55.3 23.7 %all-to-all-start.1 = ((f32[1,96,4,256]{1,2,0,3:T(4,128)}), f32[1,96,4,256]{1,2,0,3:T(4,128)}, u32[]{:S(2)}, u32[]{:S(2)}) async-start(f32[1,96,4,256]{1,2,0,3:T(4,128)} %copy.161), calls=%async_computation.1 | async-start | bytes 1048576 | tf_op jit(solution)/shard_map/all_to_all | solution.py:135
  79.0 23.7 %all-to-all-start.3 = ((f32[1,96,4,256]{1,2,0,3:T(4,128)}), f32[1,96,4,256]{1,2,0,3:T(4,128)}, u32[]{:S(2)}, u32[]{:S(2)}) async-start(f32[1,96,4,256]{1,2,0,3:T(4,128)} %copy.181), calls=%async_computation.3 | async-start | bytes 1048576 | tf_op jit(solution)/shard_map/all_to_all | solution.py:135
  86.9 1.0 copy-start.13
  104.9 1.3 copy-start.14
  107.7 5.8 %copy-start.9 = (f32[2,1,96,256]{3,2,1,0:T(8,128)}, f32[2,1,96,256]{3,2,1,0:T(8,128)S(1)}, u32[]{:S(2)}) copy-start(f32[2,1,96,256]{3,2,1,0:T(8,128)S(1)} %get-tuple-element.48) | copy-start | bytes 589828
  117.7 3.6 %copy-start.4 = (f32[1,2,128,256]{3,2,1,0:T(8,128)S(1)}, f32[1,2,128,256]{3,2,1,0:T(8,128)}, u32[]{:S(2)}) copy-start(f32[1,2,128,256]{3,2,1,0:T(8,128)} %get-tuple-element.58) | copy-start | bytes 786436
  117.8 3.6 %copy-start.6 = (f32[1,2,128,256]{3,2,1,0:T(8,128)S(1)}, f32[1,2,128,256]{3,2,1,0:T(8,128)}, u32[]{:S(2)}) copy-start(f32[1,2,128,256]{3,2,1,0:T(8,128)} %get-tuple-element.59) | copy-start | bytes 786436
  124.4 8.2 %copy-start.19 = (f32[96,96]{1,0:T(8,128)S(1)}, f32[96,96]{1,0:T(8,128)}, u32[]{:S(2)}) copy-start(f32[96,96]{1,0:T(8,128)} %fusion.86) | copy-start | bytes 110596
  126.0 6.8 %copy-start.18 = (f32[96,96]{1,0:T(8,128)S(1)}, f32[96,96]{1,0:T(8,128)}, u32[]{:S(2)}) copy-start(f32[96,96]{1,0:T(8,128)} %fusion.84) | copy-start | bytes 110596
  126.0 7.2 %copy-start.10 = (f32[2,1,96,256]{3,2,1,0:T(8,128)S(1)}, f32[2,1,96,256]{3,2,1,0:T(8,128)}, u32[]{:S(2)}) copy-start(f32[2,1,96,256]{3,2,1,0:T(8,128)} %copy-done.9) | copy-start | bytes 589828
  126.0 7.2 %copy-start.17 = (f32[96,96]{1,0:T(8,128)S(1)}, f32[96,96]{1,0:T(8,128)}, u32[]{:S(2)}) copy-start(f32[96,96]{1,0:T(8,128)} %fusion.80) | copy-start | bytes 110596
  126.0 7.5 %copy-start.16 = (f32[96,96]{1,0:T(8,128)S(1)}, f32[96,96]{1,0:T(8,128)}, u32[]{:S(2)}) copy-start(f32[96,96]{1,0:T(8,128)} %fusion.81) | copy-start | bytes 110596
  126.0 24.6 %all-to-all-start.4 = ((f32[64,1,2118]{2,1,0:T(1,128)}), f32[64,1,2118]{2,1,0:T(1,128)}, u32[]{:S(2)}, u32[]{:S(2)}) async-start(f32[64,1,2118]{2,1,0:T(1,128)} %copy.196), calls=%async_computation.4 | async-start | bytes 1114112 | tf_op jit(solution)/shard_map/all_to_all | solution.py:195
  132.6 1.2 copy-start.3
  132.6 1.2 copy-start.15
  134.4 2.0 copy-start.5
  134.4 2.0 copy-start.7
  150.6 24.3 %all-to-all-start.2 = ((f32[64,1,2118]{2,1,0:T(1,128)}), f32[64,1,2118]{2,1,0:T(1,128)S(1)}, u32[]{:S(2)}, u32[]{:S(2)}) async-start(f32[64,1,2118]{2,1,0:T(1,128)} %copy.176), calls=%async_computation.2 | async-start | bytes 1114112 | tf_op jit(solution)/shard_map/all_to_all | solution.py:195
  176.0 1.1 copy-start.11
  177.8 7.4 %copy-start.8 = (f32[2,1,96,4,64,2]{2,5,4,3,0,1:T(2,128)S(1)}, f32[2,1,96,4,64,2]{2,5,4,3,0,1:T(2,128)}, u32[]{:S(2)}) copy-start(f32[2,1,96,4,64,2]{2,5,4,3,0,1:T(2,128)} %copy.198) | copy-start | bytes 1179652
  178.8 19.6 %all-to-all-start.5 = ((f32[64,1,1164]{2,1,0:T(1,128)}), f32[64,1,1164]{2,1,0:T(1,128)}, u32[]{:S(2)}, u32[]{:S(2)}) async-start(f32[64,1,1164]{2,1,0:T(1,128)} %broadcast_in_dim.23), calls=%async_computation.5 | async-start | bytes 655360 | tf_op jit(solution)/shard_map/all_to_all | solution.py:206

commit v7 on v3

--- a/solution.py
+++ b/solution.py
@@ -67,6 +67,20 @@
 def lon_inverse(spectrum, cos_table, sin_table):
     table = jnp.stack([cos_table, -sin_table])
     return jnp.einsum("piblk,pnk->ibln", spectrum, table, precision=HIGHEST)
+
+
+def lat_inverse_split(spectrum, cos_table, sin_table, ndev):
+    top = jnp.stack([cos_table, -sin_table])
+    bottom = jnp.stack([sin_table, cos_table])
+    table = jnp.stack([top, bottom])
+    table = table.reshape(table.shape[:3] + (ndev, -1))
+    return jnp.einsum("opfdr,pibfj->doibrj", table, spectrum, precision=HIGHEST)
+
+
+def lon_inverse_split(spectrum, cos_table, sin_table, ndev):
+    table = jnp.stack([cos_table, -sin_table])
+    table = table.reshape(table.shape[:2] + (ndev, -1))
+    return jnp.einsum("dpiblj,pndj->ibln", spectrum, table, precision=HIGHEST)
 
 
 def mode_mask(signed, wavenumber, keep_lon, keep_lat):
@@ -161,8 +175,8 @@
     lat_cos, lat_sin = lat_tables(LAT, KEEP_LAT)
     table = lon_forward_table(lon_cos, lon_sin, ndev)
     col_field = to_columns(lon_forward(field, table), ndev)
+    col_field, received = lax.optimization_barrier((col_field, received))
     spectrum = lat_forward(col_field, lat_cos, lat_sin)
-    spectrum, received = lax.optimization_barrier((spectrum, received))
     upstream = jnp.where(section_index == last_section, own_grad, received)
     col_grad = to_columns(lon_forward(upstream, table), ndev)
     grad_spec = lat_forward(col_grad, lat_cos, lat_sin)
@@ -177,24 +191,21 @@
         spectrum, grad_spec, weight_in[0], bias_in[0], weight_out[0]
     )
     grad_modes = grad_modes.reshape(2, nblocks, width, 2 * KEEP_LAT, share)
-    lat_back = lat_inverse(grad_modes, lat_cos, lat_sin)
+    rows = LAT // ndev
+    back = lat_inverse_split(grad_modes, lat_cos, lat_sin, ndev).reshape(ndev, -1)
     parts = (grad_w_in, grad_b_in, grad_w_out, grad_b_out)
     flat = jnp.concatenate([p.reshape(-1) for p in parts])
     pad = (-flat.shape[0]) % ndev
     pieces = jnp.pad(flat, (0, pad)).reshape(ndev, -1)
-    rows = LAT // ndev
-    back = lat_back.reshape(2, nblocks, width, ndev, rows, share)
-    back = jnp.moveaxis(back, 3, 0).reshape(ndev, -1)
     moved = lax.all_to_all(
         jnp.concatenate([back, pieces], axis=1), "space", split_axis=0, concat_axis=0, tiled=True
     )
     rows_back = moved[:, : back.shape[1]].reshape(ndev, 2, nblocks, width, rows, share)
-    rows_back = jnp.moveaxis(rows_back, 0, 4).reshape(2, nblocks, width, rows, ndev * share)
     mine = jnp.sum(moved[:, back.shape[1]:], axis=0)
     spread = jnp.broadcast_to(mine[None], pieces.shape)
     flat = lax.all_to_all(spread, "space", split_axis=0, concat_axis=0, tiled=True)
     flat = flat.reshape(-1)[: flat.size - pad]
-    inverse = lon_inverse(rows_back, lon_cos, lon_sin)
+    inverse = lon_inverse_split(rows_back, lon_cos, lon_sin, ndev)
     factor = 1.0 / math.sqrt(2 * KEEP_LAT * KEEP_LON)
     flat = flat * factor
     sums = []

time: 169 us -> 166 us (0.982)
  blocking collectives: 0 us -> 36.1 us
  waiting for transfers between devices: 80.3 us -> 51 us
  starting transfers between devices: 32 us -> 25.7 us
  matrix products: 18.4 us -> 15.8 us
    all_to_all x0 -> x1, blocking collectives: none -> 36.1 us  [shards(): lax.all_to_all(jnp.concatenate([back, pieces], axis=1), 'space', split_ax...]
    all_to_all x1 -> x0, waiting for transfers between devices: 28.2 us -> none  [shards(): lax.all_to_all(jnp.concatenate([back, pieces], axis=1), 'space', split_ax...]
    all_to_all x1 -> x0, starting transfers between devices: 6.2 us -> none  [shards(): lax.all_to_all(jnp.concatenate([back, pieces], axis=1), 'space', split_ax...]
    all_to_all x1, waiting for transfers between devices: 7.22 us -> 4.66 us  [shards(): lax.all_to_all(spread, 'space', split_axis=0, concat_axis=0, tiled=True)]
    slice x2, local copies, waits for them, and re-layouts: 0.52 us -> 2.6 us  [shards(): moved[:, :back.shape[1]].reshape(ndev, 2, nblocks, width, rows, share)]
    mul x1 -> x2, other arithmetic: 1.11 us -> 3.07 us  [lon_tables(): return (jnp.cos(angle) * factor, jnp.sin(angle) * factor)]
    neg x1 -> x0, other arithmetic: 1.79 us -> none  [lon_inverse(): table = jnp.stack([cos_table, -sin_table])]
    unnamed x31 -> x43, local copies, waits for them, and re-layouts: 3.6 us -> 3.78 us
  transfers between devices with their start and end apart: 5 -> 4, of which waited for: 4 -> 3; matrix products, arithmetic and copies ran while one was open for 12% -> 11% of each run, Pallas kernels for 0% -> 0%
where the time goes in v7:
time: 166 us; the launch traced here: 165 us
  waiting for transfers between devices  51 us (31%)
  blocking collectives  36.1 us (22%)
  starting transfers between devices  25.7 us (15%)
  local copies, waits for them, and re-layouts  24.1 us (15%)
  matrix products  15.8 us (10%)
  other arithmetic  10.2 us (6%)
  between operations  1.94 us (1%)
    all_to_all x2, waiting for transfers between devices, to_columns(): lax.all_to_all(spectrum, 'space', split_axis=3, concat_axis=2, tiled=True)  46.3 us
    all_to_all x1, blocking collectives, shards(): lax.all_to_all(jnp.concatenate([back, pieces], axis=1), 'space', split_ax...  36.1 us
    all_to_all x2, starting transfers between devices, to_columns(): lax.all_to_all(spectrum, 'space', split_axis=3, concat_axis=2, tiled=True)  18 us
    all_to_all x1, starting transfers between devices, shards(): lax.all_to_all(spread, 'space', split_axis=0, concat_axis=0, tiled=True)  6.41 us
    dot_general x12, matrix products, block_product(): return jnp.einsum('kij,kjm->kim', weights, values, precision=HIGHEST)  4.78 us
    all_to_all x1, waiting for transfers between devices, shards(): lax.all_to_all(spread, 'space', split_axis=0, concat_axis=0, tiled=True)  4.66 us
    dot_general x2, local copies, waits for them, and re-layouts, lon_forward(): return jnp.einsum('ibln,nc->iblc', values, table, precision=HIGHEST)  3.9 us
    unnamed x43, local copies, waits for them, and re-layouts  3.78 us
  transfers between devices with their start and end apart: 4, of which 3 were waited for; matrix products, arithmetic and copies ran while one was open for 11% of the time, Pallas kernels for 0%

profile of v7, /device:TPU:1, one launch (start us, length us, event | category | flops | bytes accessed | tf_op | source)
XLA Modules:
  0.0 164.9 jit_solution(9862339804070203242)
XLA Ops:
  0.7 1.1 cosine_multiply_fusion.1
  1.8 0.4 copy.212
  2.3 0.4 reshape.584
  2.6 0.6 convolution_bitcast_fusion.1
  3.3 1.4 copy.215
  4.6 11.8 %all-to-all-start = ((f32[2,96,4,256]{1,2,0,3:T(4,128)}), f32[2,96,4,256]{1,2,0,3:T(4,128)S(1)}, u32[]{:S(2)}, u32[]{:S(2)}) async-start(f32[2,96,4,256]{1,2,0,3:T(4,128)} %copy.215), calls=%async_computation | async-start | bytes 2097152 | tf_op jit(solution)/shard_map/all_to_all | solution.py:149
  16.4 1.0 copy.322
  17.4 1.3 collective-permute-start
  18.7 0.6 fusion.107
  20.0 0.7 compare_and_fusion
  20.7 0.7 fusion.96
  21.4 1.3 sine_multiply_fusion.1
  22.7 22.2 %all-to-all-done = f32[2,96,4,256]{1,2,0,3:T(4,128)S(1)} async-done(((f32[2,96,4,256]{1,2,0,3:T(4,128)}), f32[2,96,4,256]{1,2,0,3:T(4,128)S(1)}, u32[]{:S(2)}, u32[]{:S(2)}) %all-to-all-start) | async-done | bytes 786464 | tf_op jit(solution)/shard_map/all_to_all | solution.py:149
  45.2 0.7 copy.217
  45.9 2.6 %fusion.28 = f32[2,96,4,256]{3,1,2,0:T(8,128)} fusion(f32[512,256]{0,1:T(8,128)S(1)} %reshape.584, bf16[2,96,4,512]{3,1,2,0:T(8,128)(2,1)} %collective-permute-done, pred[]{:T(512)S(6)} %eq.14, bf16[1,2,96,4,512]{4,3,2,1,0:T(4,128)(2,1)S(1)} %copy-done.1), kind=kOutput, calls=%fused_computation.51 | convolution fusion | flops 604372992 | bytes 2883585 | tf_op jit(solution)/shard_map/ibln,nc->iblc/dot_general | solution.py:50
  48.5 2.5 %copy.219 = f32[2,96,4,256]{1,2,0,3:T(4,128)} copy(f32[2,96,4,256]{3,1,2,0:T(8,128)} %fusion.28) | data formatting | bytes 1572864 | tf_op jit(solution)/shard_map/ibln,nc->iblc/dot_general | solution.py:50
  51.0 6.2 %all-to-all-start.1 = ((f32[2,96,4,256]{1,2,0,3:T(4,128)}), f32[2,96,4,256]{1,2,0,3:T(4,128)S(1)}, u32[]{:S(2)}, u32[]{:S(2)}) async-start(f32[2,96,4,256]{1,2,0,3:T(4,128)} %copy.219), calls=%async_computation.1 | async-start | bytes 2097152 | tf_op jit(solution)/shard_map/all_to_all | solution.py:149
  57.3 1.3 fusion.95
  58.7 1.0 convolution_bitcast_fusion.2
  60.1 0.5 copy-done.3
  61.7 24.1 %all-to-all-done.1 = f32[2,96,4,256]{1,2,0,3:T(4,128)S(1)} async-done(((f32[2,96,4,256]{1,2,0,3:T(4,128)}), f32[2,96,4,256]{1,2,0,3:T(4,128)S(1)}, u32[]{:S(2)}, u32[]{:S(2)}) %all-to-all-start.1) | async-done | bytes 786464 | tf_op jit(solution)/shard_map/all_to_all | solution.py:149
  86.0 0.7 copy.221
  87.0 1.1 fusion.108
  89.7 0.5 fusion.101
  90.2 0.4 fusion.51
  90.6 0.4 fusion.52
  91.5 1.0 fusion.56
  92.5 1.0 fusion.54
  93.5 0.4 fusion.10
  94.0 0.4 fusion.11
  97.3 0.6 convolution_bitcast_fusion
  97.9 2.1 %copy.246 = f32[64,2,2,96,4,2]{0,5,4,3,2,1:T(2,128)} copy(f32[64,2,2,96,4,2]{3,0,4,1,5,2:T(8,128)S(1)} %convolution_bitcast_fusion) | data formatting | bytes 1572864 | tf_op jit(solution)/shard_map/opfdr,pibfj->doibrj/transpose | solution.py:77
  100.0 1.6 maximum_bitcast_fusion
  101.6 2.6 %copy.257 = f32[64,1,4236]{2,1,0:T(1,128)} copy(f32[64,1,4236]{0,2,1:T(8,128)S(1)} %maximum_bitcast_fusion) | data formatting | bytes 2168832 | tf_op jit(solution)/shard_map/all_to_all | solution.py:200
  104.2 36.1 %all_to_all.48 = f32[64,1,4236]{2,1,0:T(1,128)S(1)} all-to-all(f32[64,1,4236]{2,1,0:T(1,128)} %copy.257), channel_id=1, replica_groups=mesh['pipe'=8,'space'=64] {'space'}, dimensions={0} | all-to-all | bytes 2168832 | tf_op jit(solution)/shard_map/all_to_all | solution.py:200
  140.5 0.9 broadcast_in_dim.15
  141.4 6.4 %all-to-all-start.3 = ((f32[64,1,1164]{2,1,0:T(1,128)}), f32[64,1,1164]{2,1,0:T(1,128)S(1)}, u32[]{:S(2)}, u32[]{:S(2)}) async-start(f32[64,1,1164]{2,1,0:T(1,128)} %broadcast_in_dim.15), calls=%async_computation.3 | async-start | bytes 655360 | tf_op jit(solution)/shard_map/all_to_all | solution.py:206
  147.8 2.0 %cosine_multiply_fusion = (f32[1,512,64,2]{1,2,0,3:T(8,128)}, f32[1,512,64,2]{1,2,0,3:T(8,128)}) fusion(s32[64,2]{0,1:T(2,128)S(1)} %copy-done.17), kind=kLoop, calls=%fused_computation.83 | loop fusion | flops 1114112 | bytes 524800 | tf_op jit(solution)/shard_map/mul | solution.py:29
  149.8 0.9 slice.122
  150.7 1.7 %copy.258 = f32[64,3072]{0,1:T(8,128)S(1)} copy(f32[64,3072]{1,0:T(8,128)} %slice.122) | data formatting | bytes 1572864 | tf_op jit(solution)/shard_map/slice | solution.py:203
  152.4 2.5 %fusion.16 = bf16[1,2,96,4,512]{4,2,3,1,0:T(8,128)(2,1)S(1)} fusion(f32[64,2,2,96,4,2]{0,5,4,3,2,1:T(2,128)S(1)} %bitcast.222, f32[1,512,64,2]{1,2,0,3:T(8,128)} %get-tuple-element.56, f32[1,512,64,2]{1,2,0,3:T(8,128)} %get-tuple-element.55, bf16[2,96,4,512]{3,1,2,0:T(8,128)(2,1)} %collective-permute-done, pred[]{:T(512)S(6)} %eq.14, ...), kind=kOutput, calls=%fused_computation.33 | convolution fusion | flops 605683712 | bytes 3670017 | tf_op jit(solution)/shard_map/dpiblj,pndj->ibln/dot_general | solution.py:83
  154.9 1.5 copy.260
  156.4 4.7 %all-to-all-done.3 = f32[64,1,1164]{2,1,0:T(1,128)S(1)} async-done(((f32[64,1,1164]{2,1,0:T(1,128)}), f32[64,1,1164]{2,1,0:T(1,128)S(1)}, u32[]{:S(2)}, u32[]{:S(2)}) %all-to-all-start.3) | async-done | bytes 298016 | tf_op jit(solution)/shard_map/all_to_all | solution.py:206
  161.0 0.9 multiply_reduce_fusion
  162.2 0.6 mul.535
  162.8 0.8 broadcast_in_dim_reshape.8
  163.6 0.6 fusion.103
  164.1 0.8 broadcast_in_dim_reshape.9
  (87 shorter events, 7.6 us)
Async XLA Ops:
  0.6 2.0 %copy-start = (bf16[1,2,96,4,512]{4,3,2,1,0:T(4,128)(2,1)S(1)}, bf16[1,2,96,4,512]{4,3,2,1,0:T(4,128)(2,1)}, u32[]{:S(2)}) copy-start(bf16[1,2,96,4,512]{4,3,2,1,0:T(4,128)(2,1)} %param.6) | copy-start | bytes 2359300
  0.7 1.1 copy-start.16
  3.3 13.1 %copy-start.1 = (bf16[1,2,96,4,512]{4,3,2,1,0:T(4,128)(2,1)S(1)}, bf16[1,2,96,4,512]{4,3,2,1,0:T(4,128)(2,1)}, u32[]{:S(2)}) copy-start(bf16[1,2,96,4,512]{4,3,2,1,0:T(4,128)(2,1)} %param.7) | copy-start | bytes 2359300
  4.6 14.1 %copy-start.19 = (s32[1,2]{1,0:T(1,128)S(1)}, s32[1,2]{1,0:T(1,128)}, u32[]{:S(2)}) copy-start(s32[1,2]{1,0:T(1,128)} %param.8) | copy-start | bytes 28
  4.6 40.3 %all-to-all-start = ((f32[2,96,4,256]{1,2,0,3:T(4,128)}), f32[2,96,4,256]{1,2,0,3:T(4,128)S(1)}, u32[]{:S(2)}, u32[]{:S(2)}) async-start(f32[2,96,4,256]{1,2,0,3:T(4,128)} %copy.215), calls=%async_computation | async-start | bytes 2097152 | tf_op jit(solution)/shard_map/all_to_all | solution.py:149
  17.4 28.4 %collective-permute-start = (bf16[2,96,4,512]{3,1,2,0:T(8,128)(2,1)}, bf16[2,96,4,512]{3,1,2,0:T(8,128)(2,1)}, u32[]{:S(2)}, u32[]{:S(2)}) collective-permute-start(bf16[2,96,4,512]{3,1,2,0:T(8,128)(2,1)} %bitcast.204), channel_id=1, source_target_pairs={{64,0},{128,64},{192,128},{256,192},{320,256},{384,320},{448,384},... | collective-permute-start | bytes 2359304 | tf_op jit(solution)/shard_map/ppermute | solution.py:20
  48.5 8.8 %copy-start.14 = (f32[128,1,256]{2,0,1:T(8,128)S(1)}, f32[128,1,256]{2,0,1:T(8,128)}, u32[]{:S(2)}) copy-start(f32[128,1,256]{2,0,1:T(8,128)} %get-tuple-element.62) | copy-start | bytes 393220
  48.5 8.8 %copy-start.15 = (f32[128,1,256]{2,0,1:T(8,128)S(1)}, f32[128,1,256]{2,0,1:T(8,128)}, u32[]{:S(2)}) copy-start(f32[128,1,256]{2,0,1:T(8,128)} %get-tuple-element.63) | copy-start | bytes 393220
  51.0 34.8 %all-to-all-start.1 = ((f32[2,96,4,256]{1,2,0,3:T(4,128)}), f32[2,96,4,256]{1,2,0,3:T(4,128)S(1)}, u32[]{:S(2)}, u32[]{:S(2)}) async-start(f32[2,96,4,256]{1,2,0,3:T(4,128)} %copy.219), calls=%async_computation.1 | async-start | bytes 2097152 | tf_op jit(solution)/shard_map/all_to_all | solution.py:149
  57.3 2.4 %copy-start.4 = (f32[1,128,2,256]{3,1,2,0:T(8,128)}, f32[1,128,2,256]{3,1,2,0:T(8,128)S(1)}, u32[]{:S(2)}) copy-start(f32[1,128,2,256]{3,1,2,0:T(8,128)S(1)} %get-tuple-element.50) | copy-start | bytes 786436
  57.3 2.4 %copy-start.6 = (f32[1,128,2,256]{3,1,2,0:T(8,128)}, f32[1,128,2,256]{3,1,2,0:T(8,128)S(1)}, u32[]{:S(2)}) copy-start(f32[1,128,2,256]{3,1,2,0:T(8,128)S(1)} %get-tuple-element.51) | copy-start | bytes 786436
  59.7 0.9 copy-start.3
  86.0 1.0 copy-start.5
  86.0 1.0 copy-start.7
  87.0 1.5 copy-start.10
  88.3 1.4 copy-start.18
  95.1 0.9 copy-start.9
  95.3 1.3 copy-start.8
  96.1 1.1 copy-start.11
  96.1 1.1 copy-start.12
  96.4 0.9 copy-start.13
  140.4 7.4 %copy-start.17 = (s32[64,2]{0,1:T(2,128)S(1)}, s32[64,2]{0,1:T(2,128)}, u32[]{:S(2)}) copy-start(s32[64,2]{0,1:T(2,128)} %copy-done.16) | copy-start | bytes 1540
  141.4 19.7 %all-to-all-start.3 = ((f32[64,1,1164]{2,1,0:T(1,128)}), f32[64,1,1164]{2,1,0:T(1,128)S(1)}, u32[]{:S(2)}, u32[]{:S(2)}) async-start(f32[64,1,1164]{2,1,0:T(1,128)} %broadcast_in_dim.15), calls=%async_computation.3 | async-start | bytes 655360 | tf_op jit(solution)/shard_map/all_to_all | solution.py:206
  150.7 1.7 %copy-start.2 = (bf16[1,2,96,4,512]{4,3,2,1,0:T(4,128)(2,1)S(1)}, bf16[1,2,96,4,512]{4,3,2,1,0:T(4,128)(2,1)}, u32[]{:S(2)}) copy-start(bf16[1,2,96,4,512]{4,3,2,1,0:T(4,128)(2,1)} %param.7) | copy-start | bytes 2359300

commit v8 on v7

--- a/solution.py
+++ b/solution.py
@@ -54,7 +54,7 @@
     top = jnp.stack([cos_table, sin_table], axis=1)
     bottom = jnp.stack([-sin_table, cos_table], axis=1)
     table = jnp.stack([top, bottom])
-    return jnp.einsum("ofpl,iblpj->oibfj", table, spectrum, precision=HIGHEST)
+    return jnp.einsum("ofpl,iblpj->iobfj", table, spectrum, precision=HIGHEST)
 
 
 def lat_inverse(spectrum, cos_table, sin_table):
@@ -74,7 +74,7 @@
     bottom = jnp.stack([sin_table, cos_table])
     table = jnp.stack([top, bottom])
     table = table.reshape(table.shape[:3] + (ndev, -1))
-    return jnp.einsum("opfdr,pibfj->doibrj", table, spectrum, precision=HIGHEST)
+    return jnp.einsum("opfdr,ipbfj->doibrj", table, spectrum, precision=HIGHEST)
 
 
 def lon_inverse_split(spectrum, cos_table, sin_table, ndev):
@@ -90,31 +90,26 @@
     return (lat_kept[:, None] & lon_kept[None, :]).astype(jnp.float32) * factor[None, :]
 
 
-def block_product(weights, values):
+def real_form(weights):
+    real_part, imag_part = weights[0], weights[1]
+    top = jnp.concatenate([real_part, -imag_part], axis=2)
+    bottom = jnp.concatenate([imag_part, real_part], axis=2)
+    return jnp.concatenate([top, bottom], axis=1)
+
+
+def apply(weights, values):
     return jnp.einsum("kij,kjm->kim", weights, values, precision=HIGHEST)
 
 
-def complex_apply(weights, values):
-    real_part = block_product(weights[0], values[0]) - block_product(weights[1], values[1])
-    imag_part = block_product(weights[1], values[0]) + block_product(weights[0], values[1])
-    return jnp.stack([real_part, imag_part])
-
-
-def complex_adjoint(weights, values):
-    real_t = jnp.swapaxes(weights[0], 1, 2)
-    imag_t = jnp.swapaxes(weights[1], 1, 2)
-    real_part = block_product(real_t, values[0]) + block_product(imag_t, values[1])
-    imag_part = block_product(real_t, values[1]) - block_product(imag_t, values[0])
-    return jnp.stack([real_part, imag_part])
-
-
-def complex_outer(left, right):
-
-    def outer(first, second):
-        return jnp.einsum("kim,kjm->kij", first, second, precision=HIGHEST)
-
-    real_part = outer(left[0], right[0]) + outer(left[1], right[1])
-    imag_part = outer(left[1], right[0]) - outer(left[0], right[1])
+def apply_adjoint(weights, values):
+    return jnp.einsum("kji,kjm->kim", weights, values, precision=HIGHEST)
+
+
+def complex_outer(left, right, width):
+    full = jnp.einsum("kim,kjm->kij", left, right, precision=HIGHEST)
+    full = full.reshape(full.shape[0], 2, width, 2, width)
+    real_part = full[:, 0, :, 0] + full[:, 1, :, 1]
+    imag_part = full[:, 1, :, 0] - full[:, 0, :, 1]
     return jnp.stack([real_part, imag_part])
 
 
@@ -128,20 +123,28 @@
     return (output, slope)
 
 
+def split_parts(stacked, width):
+    return jnp.swapaxes(stacked.reshape(stacked.shape[0], 2, width), 0, 1)
+
+
 def backprop(spectrum, grad_spec, weight_in, bias_in, weight_out):
-    before = complex_apply(weight_in, spectrum) + bias_in[..., None]
+    width = weight_in.shape[-1]
+    forward_in = real_form(weight_in)
+    forward_out = real_form(weight_out)
+    bias = jnp.concatenate([bias_in[0], bias_in[1]], axis=1)
+    before = apply(forward_in, spectrum) + bias[..., None]
     hidden, slope = gelu_pair(before)
-    grad_hidden = complex_adjoint(weight_out, grad_spec)
+    grad_hidden = apply_adjoint(forward_out, grad_spec)
     grad_before = grad_hidden * slope
-    grad_modes = complex_adjoint(weight_in, grad_before)
-    grad_w_out = complex_outer(grad_spec, hidden)
-    grad_w_in = complex_outer(grad_before, spectrum)
+    grad_modes = apply_adjoint(forward_in, grad_before)
+    grad_w_out = complex_outer(grad_spec, hidden, width)
+    grad_w_in = complex_outer(grad_before, spectrum, width)
     return (
         grad_modes,
         grad_w_in,
-        jnp.sum(grad_before, axis=-1),
+        split_parts(jnp.sum(grad_before, axis=-1), width),
         grad_w_out,
-        jnp.sum(grad_spec, axis=-1),
+        split_parts(jnp.sum(grad_spec, axis=-1), width),
     )
 
 
@@ -185,12 +188,12 @@
     wavenumber = lax.axis_index("space") * share + jnp.arange(share, dtype=jnp.int32)
     weight = mode_mask(signed, wavenumber, kept_modes[0, 0], kept_modes[0, 1])
     grad_spec = grad_spec * weight
-    spectrum = spectrum.reshape(2, nblocks, width, -1)
-    grad_spec = grad_spec.reshape(2, nblocks, width, -1)
+    spectrum = spectrum.reshape(nblocks, 2 * width, -1)
+    grad_spec = grad_spec.reshape(nblocks, 2 * width, -1)
     grad_modes, grad_w_in, grad_b_in, grad_w_out, grad_b_out = backprop(
         spectrum, grad_spec, weight_in[0], bias_in[0], weight_out[0]
     )
-    grad_modes = grad_modes.reshape(2, nblocks, width, 2 * KEEP_LAT, share)
+    grad_modes = grad_modes.reshape(nblocks, 2, width, 2 * KEEP_LAT, share)
     rows = LAT // ndev
     back = lat_inverse_split(grad_modes, lat_cos, lat_sin, ndev).reshape(ndev, -1)
     parts = (grad_w_in, grad_b_in, grad_w_out, grad_b_out)

time: 166 us -> 162 us (0.976)
  waiting for transfers between devices: 51 us -> 44.3 us
  local copies, waits for them, and re-layouts: 24.1 us -> 28.6 us
  matrix products: 15.8 us -> 12.1 us
  other arithmetic: 10.2 us -> 12.9 us
    all_to_all x2, waiting for transfers between devices: 46.3 us -> 39.7 us  [to_columns(): lax.all_to_all(spectrum, 'space', split_axis=3, concat_axis=2, tiled=True)]
    dot_general x23 -> x8, matrix products: 10.1 us -> 6.29 us  [the longest x2 2.85 us: lat_forward(): return jnp.einsum('ofpl,iblpj->iobfj', table, spectrum, precision=HIGHEST)]
    neg x0 -> x2, other arithmetic: none -> 2.44 us  [real_form(): top = jnp.concatenate([real_part, -imag_part], axis=2)]
    transpose x1 -> x4, local copies, waits for them, and re-layouts: 2.11 us -> 3.5 us  [the longest x1 2.14 us: lat_inverse_split(): return jnp.einsum('opfdr,ipbfj->doibrj', table, spectrum, precision=HIGHEST)]
    unnamed x43 -> x45, local copies, waits for them, and re-layouts: 3.78 us -> 4.53 us
  transfers between devices with their start and end apart: 4 -> 4, of which waited for: 3 -> 3; matrix products, arithmetic and copies ran while one was open for 11% -> 15% of each run, Pallas kernels for 0% -> 0%
where the time goes in v8:
time: 162 us
  waiting for transfers between devices  44.3 us (27%)
  blocking collectives  36.1 us (22%)
  local copies, waits for them, and re-layouts  28.6 us (18%)
  starting transfers between devices  25.8 us (16%)
  other arithmetic  12.9 us (8%)
  matrix products  12.1 us (7%)
  between operations  1.86 us (1%)
    all_to_all x2, waiting for transfers between devices, to_columns(): lax.all_to_all(spectrum, 'space', split_axis=3, concat_axis=2, tiled=True)  39.7 us
    all_to_all x1, blocking collectives, shards(): lax.all_to_all(jnp.concatenate([back, pieces], axis=1), 'space', split_ax...  36.1 us
    all_to_all x2, starting transfers between devices, to_columns(): lax.all_to_all(spectrum, 'space', split_axis=3, concat_axis=2, tiled=True)  18.1 us
    all_to_all x1, starting transfers between devices, shards(): lax.all_to_all(spread, 'space', split_axis=0, concat_axis=0, tiled=True)  6.41 us
    all_to_all x1, waiting for transfers between devices, shards(): lax.all_to_all(spread, 'space', split_axis=0, concat_axis=0, tiled=True)  4.63 us
    unnamed x45, local copies, waits for them, and re-layouts  4.53 us
    dot_general x2, local copies, waits for them, and re-layouts, lon_forward(): return jnp.einsum('ibln,nc->iblc', values, table, precision=HIGHEST)  3.8 us
    dot_general x2, matrix products, lon_forward(): return jnp.einsum('ibln,nc->iblc', values, table, precision=HIGHEST)  3.25 us
  transfers between devices with their start and end apart: 4, of which 3 were waited for; matrix products, arithmetic and copies ran while one was open for 15% of the time, Pallas kernels for 0%

profile of v8, /device:TPU:1, one launch (start us, length us, event | category | flops | bytes accessed | tf_op | source)
XLA Modules:
  0.0 161.7 jit_solution(10115966068139815482)
XLA Ops:
  0.7 1.1 cosine_multiply_fusion.1
  2.6 0.6 convolution_bitcast_fusion.1
  3.3 1.3 copy.123
  4.6 11.8 %all-to-all-start = ((f32[2,96,4,256]{1,2,0,3:T(4,128)}), f32[2,96,4,256]{1,2,0,3:T(4,128)S(1)}, u32[]{:S(2)}, u32[]{:S(2)}) async-start(f32[2,96,4,256]{1,2,0,3:T(4,128)} %copy.123), calls=%async_computation | async-start | bytes 2097152 | tf_op jit(solution)/shard_map/all_to_all | solution.py:152
  16.4 1.0 copy.210
  17.4 1.3 collective-permute-start
  18.7 0.6 fusion.85
  20.0 0.7 copy.183
  20.7 0.7 copy.182
  21.5 0.7 compare_and_fusion
  22.1 0.7 fusion.67
  22.9 0.6 sine_multiply_fusion.1
  23.5 0.9 maximum_bitcast_fusion.10
  24.4 20.5 %all-to-all-done = f32[2,96,4,256]{1,2,0,3:T(4,128)S(1)} async-done(((f32[2,96,4,256]{1,2,0,3:T(4,128)}), f32[2,96,4,256]{1,2,0,3:T(4,128)S(1)}, u32[]{:S(2)}, u32[]{:S(2)}) %all-to-all-start) | async-done | bytes 786464 | tf_op jit(solution)/shard_map/all_to_all | solution.py:152
  45.1 0.7 copy.125
  45.8 2.6 %fusion.19 = f32[2,96,4,256]{3,1,2,0:T(8,128)} fusion(f32[512,256]{0,1:T(8,128)S(1)} %reshape.666, bf16[2,96,4,512]{3,1,2,0:T(8,128)(2,1)} %collective-permute-done, pred[]{:T(512)S(6)} %eq.14, bf16[1,2,96,4,512]{4,3,2,1,0:T(4,128)(2,1)S(1)} %copy-done.1), kind=kOutput, calls=%fused_computation.34 | convolution fusion | flops 604372992 | bytes 2883585 | tf_op jit(solution)/shard_map/ibln,nc->iblc/dot_general | solution.py:50
  48.5 2.5 %copy.129 = f32[2,96,4,256]{1,2,0,3:T(4,128)} copy(f32[2,96,4,256]{3,1,2,0:T(8,128)} %fusion.19) | data formatting | bytes 1572864 | tf_op jit(solution)/shard_map/ibln,nc->iblc/dot_general | solution.py:50
  50.9 6.3 %all-to-all-start.1 = ((f32[2,96,4,256]{1,2,0,3:T(4,128)}), f32[2,96,4,256]{1,2,0,3:T(4,128)S(1)}, u32[]{:S(2)}, u32[]{:S(2)}) async-start(f32[2,96,4,256]{1,2,0,3:T(4,128)} %copy.129), calls=%async_computation.1 | async-start | bytes 2097152 | tf_op jit(solution)/shard_map/all_to_all | solution.py:152
  57.4 0.9 fusion.79
  58.3 1.5 bitcast_negate_fusion
  59.8 1.6 %slice_bitcast_fusion = (f32[2,96,96]{2,1,0:T(8,128)}, f32[2,96,96]{2,1,0:T(8,128)}) fusion(f32[1,2,2,96,96]{4,3,2,1,0:T(8,128)} %param.9), kind=kLoop, calls=%fused_computation.113 | loop fusion | bytes 294912 | tf_op jit(solution)/shard_map/squeeze | solution.py:94
  61.4 1.3 fusion.66
  62.8 1.8 %convolution_bitcast_fusion.2 = f32[2,2,96,128,2]{3,2,1,4,0:T(8,128)} fusion(f32[1,128,2,256]{3,1,2,0:T(8,128)S(1)} %copy-done.5, f32[1,128,2,256]{3,1,2,0:T(8,128)S(1)} %copy-done.3, f32[2,96,256,2,2]{1,2,4,3,0:T(8,128)S(1)} %bitcast.143), kind=kOutput, calls=%fused_computation.7 | convolution fusion | flops 302120960 | bytes 1703936 | tf_op jit(solution)/shard_map/ofpl,iblpj->iobfj/dot_general | solution.py:57
  64.5 1.4 copy.136
  66.7 19.2 %all-to-all-done.1 = f32[2,96,4,256]{1,2,0,3:T(4,128)S(1)} async-done(((f32[2,96,4,256]{1,2,0,3:T(4,128)}), f32[2,96,4,256]{1,2,0,3:T(4,128)S(1)}, u32[]{:S(2)}, u32[]{:S(2)}) %all-to-all-start.1) | async-done | bytes 786464 | tf_op jit(solution)/shard_map/all_to_all | solution.py:152
  86.1 0.7 copy.131
  87.1 1.1 fusion.86
  88.8 0.6 fusion.34
  89.5 0.7 fusion.87
  90.5 0.8 fusion.39
  94.0 0.6 convolution_bitcast_fusion
  94.6 2.1 %copy.141 = f32[64,2,2,96,4,2]{0,5,4,3,2,1:T(2,128)} copy(f32[64,2,2,96,4,2]{3,0,4,1,5,2:T(8,128)S(1)} %convolution_bitcast_fusion) | data formatting | bytes 1572864 | tf_op jit(solution)/shard_map/opfdr,ipbfj->doibrj/transpose | solution.py:77
  96.8 1.6 maximum_bitcast_fusion
  98.3 2.7 %copy.151 = f32[64,1,4236]{2,1,0:T(1,128)} copy(f32[64,1,4236]{0,2,1:T(8,128)S(1)} %maximum_bitcast_fusion) | data formatting | bytes 2168832 | tf_op jit(solution)/shard_map/all_to_all | solution.py:203
  101.0 36.1 %all_to_all.48 = f32[64,1,4236]{2,1,0:T(1,128)S(1)} all-to-all(f32[64,1,4236]{2,1,0:T(1,128)} %copy.151), channel_id=1, replica_groups=mesh['pipe'=8,'space'=64] {'space'}, dimensions={0} | all-to-all | bytes 2168832 | tf_op jit(solution)/shard_map/all_to_all | solution.py:203
  137.2 0.9 broadcast_in_dim.15
  138.1 6.4 %all-to-all-start.3 = ((f32[64,1,1164]{2,1,0:T(1,128)}), f32[64,1,1164]{2,1,0:T(1,128)S(1)}, u32[]{:S(2)}, u32[]{:S(2)}) async-start(f32[64,1,1164]{2,1,0:T(1,128)} %broadcast_in_dim.15), calls=%async_computation.3 | async-start | bytes 655360 | tf_op jit(solution)/shard_map/all_to_all | solution.py:209
  144.6 2.0 %cosine_multiply_fusion = (f32[1,512,64,2]{1,2,0,3:T(8,128)}, f32[1,512,64,2]{1,2,0,3:T(8,128)}) fusion(s32[64,2]{0,1:T(2,128)S(1)} %copy-done.17), kind=kLoop, calls=%fused_computation.73 | loop fusion | flops 1114112 | bytes 524800 | tf_op jit(solution)/shard_map/mul | solution.py:29
  146.6 0.9 slice.104
  147.5 1.7 %copy.152 = f32[64,3072]{0,1:T(8,128)S(1)} copy(f32[64,3072]{1,0:T(8,128)} %slice.104) | data formatting | bytes 1572864 | tf_op jit(solution)/shard_map/slice | solution.py:206
  149.2 2.5 %fusion.6 = bf16[1,2,96,4,512]{4,2,3,1,0:T(8,128)(2,1)S(1)} fusion(f32[64,2,2,96,4,2]{0,5,4,3,2,1:T(2,128)S(1)} %bitcast.136, f32[1,512,64,2]{1,2,0,3:T(8,128)} %get-tuple-element.56, f32[1,512,64,2]{1,2,0,3:T(8,128)} %get-tuple-element.55, bf16[2,96,4,512]{3,1,2,0:T(8,128)(2,1)} %collective-permute-done, pred[]{:T(512)S(6)} %eq.14, ...), kind=kOutput, calls=%fused_computation.15 | convolution fusion | flops 605683712 | bytes 3670017 | tf_op jit(solution)/shard_map/dpiblj,pndj->ibln/dot_general | solution.py:83
  151.7 1.5 copy.154
  153.2 4.6 %all-to-all-done.3 = f32[64,1,1164]{2,1,0:T(1,128)S(1)} async-done(((f32[64,1,1164]{2,1,0:T(1,128)}), f32[64,1,1164]{2,1,0:T(1,128)S(1)}, u32[]{:S(2)}, u32[]{:S(2)}) %all-to-all-start.3) | async-done | bytes 298016 | tf_op jit(solution)/shard_map/all_to_all | solution.py:209
  157.8 0.9 multiply_reduce_fusion
  158.9 0.6 mul.535
  159.5 0.8 broadcast_in_dim_reshape.8
  160.3 0.8 broadcast_in_dim_reshape.9
  161.1 0.6 fusion.80
  (82 shorter events, 6.5 us)
Async XLA Ops:
  0.6 2.0 %copy-start = (bf16[1,2,96,4,512]{4,3,2,1,0:T(4,128)(2,1)S(1)}, bf16[1,2,96,4,512]{4,3,2,1,0:T(4,128)(2,1)}, u32[]{:S(2)}) copy-start(bf16[1,2,96,4,512]{4,3,2,1,0:T(4,128)(2,1)} %param.6) | copy-start | bytes 2359300
  0.7 1.1 copy-start.16
  3.3 13.1 %copy-start.1 = (bf16[1,2,96,4,512]{4,3,2,1,0:T(4,128)(2,1)S(1)}, bf16[1,2,96,4,512]{4,3,2,1,0:T(4,128)(2,1)}, u32[]{:S(2)}) copy-start(bf16[1,2,96,4,512]{4,3,2,1,0:T(4,128)(2,1)} %param.7) | copy-start | bytes 2359300
  4.6 14.1 %copy-start.19 = (s32[1,2]{1,0:T(1,128)S(1)}, s32[1,2]{1,0:T(1,128)}, u32[]{:S(2)}) copy-start(s32[1,2]{1,0:T(1,128)} %param.8) | copy-start | bytes 28
  4.6 15.4 %copy-start.13 = (f32[1,2,2,96,96]{4,3,2,1,0:T(8,128)S(1)}, f32[1,2,2,96,96]{4,3,2,1,0:T(8,128)}, u32[]{:S(2)}) copy-start(f32[1,2,2,96,96]{4,3,2,1,0:T(8,128)} %param.11) | copy-start | bytes 442372
  4.6 40.3 %all-to-all-start = ((f32[2,96,4,256]{1,2,0,3:T(4,128)}), f32[2,96,4,256]{1,2,0,3:T(4,128)S(1)}, u32[]{:S(2)}, u32[]{:S(2)}) async-start(f32[2,96,4,256]{1,2,0,3:T(4,128)} %copy.123), calls=%async_computation | async-start | bytes 2097152 | tf_op jit(solution)/shard_map/all_to_all | solution.py:152
  16.4 6.4 %copy-start.18 = (f32[1,2,2,96]{3,2,1,0:T(2,128)S(1)}, f32[1,2,2,96]{3,2,1,0:T(2,128)}, u32[]{:S(2)}) copy-start(f32[1,2,2,96]{3,2,1,0:T(2,128)} %param.10) | copy-start | bytes 4612
  17.4 28.4 %collective-permute-start = (bf16[2,96,4,512]{3,1,2,0:T(8,128)(2,1)}, bf16[2,96,4,512]{3,1,2,0:T(8,128)(2,1)}, u32[]{:S(2)}, u32[]{:S(2)}) collective-permute-start(bf16[2,96,4,512]{3,1,2,0:T(8,128)(2,1)} %bitcast.134), channel_id=1, source_target_pairs={{64,0},{128,64},{192,128},{256,192},{320,256},{384,320},{448,384},... | collective-permute-start | bytes 2359304 | tf_op jit(solution)/shard_map/ppermute | solution.py:20
  50.9 11.8 %copy-start.3 = (f32[1,128,2,256]{3,1,2,0:T(8,128)S(1)}, f32[1,128,2,256]{3,1,2,0:T(8,128)}, u32[]{:S(2)}) copy-start(f32[1,128,2,256]{3,1,2,0:T(8,128)} %get-tuple-element.48) | copy-start | bytes 786436
  50.9 11.8 %copy-start.5 = (f32[1,128,2,256]{3,1,2,0:T(8,128)S(1)}, f32[1,128,2,256]{3,1,2,0:T(8,128)}, u32[]{:S(2)}) copy-start(f32[1,128,2,256]{3,1,2,0:T(8,128)} %get-tuple-element.49) | copy-start | bytes 786436
  50.9 34.9 %all-to-all-start.1 = ((f32[2,96,4,256]{1,2,0,3:T(4,128)}), f32[2,96,4,256]{1,2,0,3:T(4,128)S(1)}, u32[]{:S(2)}, u32[]{:S(2)}) async-start(f32[2,96,4,256]{1,2,0,3:T(4,128)} %copy.129), calls=%async_computation.1 | async-start | bytes 2097152 | tf_op jit(solution)/shard_map/all_to_all | solution.py:152
  64.5 1.7 %copy-start.7 = (f32[2,96,96]{2,1,0:T(8,128)S(1)}, f32[2,96,96]{2,1,0:T(8,128)}, u32[]{:S(2)}) copy-start(f32[2,96,96]{2,1,0:T(8,128)} %get-tuple-element.46) | copy-start | bytes 221188
  64.5 1.7 %copy-start.8 = (f32[2,96,96]{2,1,0:T(8,128)S(1)}, f32[2,96,96]{2,1,0:T(8,128)}, u32[]{:S(2)}) copy-start(f32[2,96,96]{2,1,0:T(8,128)} %get-tuple-element.47) | copy-start | bytes 221188
  86.0 1.0 copy-start.4
  86.0 1.0 copy-start.6
  88.2 1.3 copy-start.12
  88.2 1.3 copy-start.14
  88.2 1.3 copy-start.15
  93.0 1.0 copy-start.9
  93.0 1.0 copy-start.10
  93.0 1.0 copy-start.11
  137.1 7.4 %copy-start.17 = (s32[64,2]{0,1:T(2,128)S(1)}, s32[64,2]{0,1:T(2,128)}, u32[]{:S(2)}) copy-start(s32[64,2]{0,1:T(2,128)} %copy-done.16) | copy-start | bytes 1540
  138.1 19.7 %all-to-all-start.3 = ((f32[64,1,1164]{2,1,0:T(1,128)}), f32[64,1,1164]{2,1,0:T(1,128)S(1)}, u32[]{:S(2)}, u32[]{:S(2)}) async-start(f32[64,1,1164]{2,1,0:T(1,128)} %broadcast_in_dim.15), calls=%async_computation.3 | async-start | bytes 655360 | tf_op jit(solution)/shard_map/all_to_all | solution.py:209
  147.5 1.7 %copy-start.2 = (bf16[1,2,96,4,512]{4,3,2,1,0:T(4,128)(2,1)S(1)}, bf16[1,2,96,4,512]{4,3,2,1,0:T(4,128)(2,1)}, u32[]{:S(2)}) copy-start(bf16[1,2,96,4,512]{4,3,2,1,0:T(4,128)(2,1)} %param.7) | copy-start | bytes 2359300

commit v9 on v8

--- a/solution.py
+++ b/solution.py
@@ -50,10 +50,13 @@
     return jnp.einsum("ibln,nc->iblc", values, table, precision=HIGHEST)
 
 
-def lat_forward(spectrum, cos_table, sin_table):
+def lat_forward_table(cos_table, sin_table):
     top = jnp.stack([cos_table, sin_table], axis=1)
     bottom = jnp.stack([-sin_table, cos_table], axis=1)
-    table = jnp.stack([top, bottom])
+    return jnp.stack([top, bottom])
+
+
+def lat_forward(spectrum, table):
     return jnp.einsum("ofpl,iblpj->iobfj", table, spectrum, precision=HIGHEST)
 
 
@@ -69,17 +72,23 @@
     return jnp.einsum("piblk,pnk->ibln", spectrum, table, precision=HIGHEST)
 
 
-def lat_inverse_split(spectrum, cos_table, sin_table, ndev):
+def lat_inverse_table(cos_table, sin_table, ndev):
     top = jnp.stack([cos_table, -sin_table])
     bottom = jnp.stack([sin_table, cos_table])
     table = jnp.stack([top, bottom])
-    table = table.reshape(table.shape[:3] + (ndev, -1))
+    return table.reshape(table.shape[:3] + (ndev, -1))
+
+
+def lat_inverse_split(spectrum, table):
     return jnp.einsum("opfdr,ipbfj->doibrj", table, spectrum, precision=HIGHEST)
 
 
-def lon_inverse_split(spectrum, cos_table, sin_table, ndev):
+def lon_inverse_table(cos_table, sin_table, ndev):
     table = jnp.stack([cos_table, -sin_table])
-    table = table.reshape(table.shape[:2] + (ndev, -1))
+    return table.reshape(table.shape[:2] + (ndev, -1))
+
+
+def lon_inverse_split(spectrum, table):
     return jnp.einsum("dpiblj,pndj->ibln", spectrum, table, precision=HIGHEST)
 
 
@@ -177,16 +186,23 @@
     lon_cos, lon_sin = lon_tables(LON, KEEP_LON)
     lat_cos, lat_sin = lat_tables(LAT, KEEP_LAT)
     table = lon_forward_table(lon_cos, lon_sin, ndev)
-    col_field = to_columns(lon_forward(field, table), ndev)
-    col_field, received = lax.optimization_barrier((col_field, received))
-    spectrum = lat_forward(col_field, lat_cos, lat_sin)
-    upstream = jnp.where(section_index == last_section, own_grad, received)
-    col_grad = to_columns(lon_forward(upstream, table), ndev)
-    grad_spec = lat_forward(col_grad, lat_cos, lat_sin)
     share = KEEP_LON // ndev
     signed = jnp.arange(2 * KEEP_LAT, dtype=jnp.int32) - KEEP_LAT
     wavenumber = lax.axis_index("space") * share + jnp.arange(share, dtype=jnp.int32)
     weight = mode_mask(signed, wavenumber, kept_modes[0, 0], kept_modes[0, 1])
+    tables = (
+        lat_forward_table(lat_cos, lat_sin),
+        lat_inverse_table(lat_cos, lat_sin, ndev),
+        lon_inverse_table(lon_cos, lon_sin, ndev),
+        weight,
+    )
+    col_field = to_columns(lon_forward(field, table), ndev)
+    col_field, received, tables = lax.optimization_barrier((col_field, received, tables))
+    lat_table, lat_back_table, lon_back_table, weight = tables
+    spectrum = lat_forward(col_field, lat_table)
+    upstream = jnp.where(section_index == last_section, own_grad, received)
+    col_grad = to_columns(lon_forward(upstream, table), ndev)
+    grad_spec = lat_forward(col_grad, lat_table)
     grad_spec = grad_spec * weight
     spectrum = spectrum.reshape(nblocks, 2 * width, -1)
     grad_spec = grad_spec.reshape(nblocks, 2 * width, -1)
@@ -195,7 +211,7 @@
     )
     grad_modes = grad_modes.reshape(nblocks, 2, width, 2 * KEEP_LAT, share)
     rows = LAT // ndev
-    back = lat_inverse_split(grad_modes, lat_cos, lat_sin, ndev).reshape(ndev, -1)
+    back = lat_inverse_split(grad_modes, lat_back_table).reshape(ndev, -1)
     parts = (grad_w_in, grad_b_in, grad_w_out, grad_b_out)
     flat = jnp.concatenate([p.reshape(-1) for p in parts])
     pad = (-flat.shape[0]) % ndev
@@ -208,7 +224,7 @@
     spread = jnp.broadcast_to(mine[None], pieces.shape)
     flat = lax.all_to_all(spread, "space", split_axis=0, concat_axis=0, tiled=True)
     flat = flat.reshape(-1)[: flat.size - pad]
-    inverse = lon_inverse_split(rows_back, lon_cos, lon_sin, ndev)
+    inverse = lon_inverse_split(rows_back, lon_back_table)
     factor = 1.0 / math.sqrt(2 * KEEP_LAT * KEEP_LON)
     flat = flat * factor
     sums = []

time: 162 us -> 165 us (1.019)
  waiting for transfers between devices: 44.3 us -> 48.8 us
  other arithmetic: 12.9 us -> 10.4 us
    all_to_all x4, local copies, waits for them, and re-layouts: 1.76 us -> 5.2 us  [to_columns(): lax.all_to_all(spectrum, 'space', split_axis=3, concat_axis=2, tiled=True)]
    all_to_all x2, waiting for transfers between devices: 39.7 us -> 42.1 us  [to_columns(): lax.all_to_all(spectrum, 'space', split_axis=3, concat_axis=2, tiled=True)]
    all_to_all x1, waiting for transfers between devices: 4.63 us -> 6.63 us  [shards(): lax.all_to_all(spread, 'space', split_axis=0, concat_axis=0, tiled=True)]
    neg x2, other arithmetic: 2.44 us -> 0.66 us  [real_form(): top = jnp.concatenate([real_part, -imag_part], axis=2)]
    unnamed x45 -> x35, local copies, waits for them, and re-layouts: 4.53 us -> 3.56 us
  transfers between devices with their start and end apart: 4 -> 4, of which waited for: 3 -> 3; matrix products, arithmetic and copies ran while one was open for 15% -> 14% of each run, Pallas kernels for 0% -> 0%
where the time goes in v9:
time: 165 us
  waiting for transfers between devices  48.8 us (30%)
  blocking collectives  36.1 us (22%)
  local copies, waits for them, and re-layouts  30.2 us (18%)
  starting transfers between devices  26 us (16%)
  matrix products  11.2 us (7%)
  other arithmetic  10.4 us (6%)
  between operations  1.89 us (1%)
    all_to_all x2, waiting for transfers between devices, to_columns(): lax.all_to_all(spectrum, 'space', split_axis=3, concat_axis=2, tiled=True)  42.1 us
    all_to_all x1, blocking collectives, shards(): lax.all_to_all(jnp.concatenate([back, pieces], axis=1), 'space', split_ax...  36.1 us
    all_to_all x2, starting transfers between devices, to_columns(): lax.all_to_all(spectrum, 'space', split_axis=3, concat_axis=2, tiled=True)  18.5 us
    all_to_all x1, waiting for transfers between devices, shards(): lax.all_to_all(spread, 'space', split_axis=0, concat_axis=0, tiled=True)  6.63 us
    all_to_all x1, starting transfers between devices, shards(): lax.all_to_all(spread, 'space', split_axis=0, concat_axis=0, tiled=True)  6.19 us
    all_to_all x4, local copies, waits for them, and re-layouts, to_columns(): lax.all_to_all(spectrum, 'space', split_axis=3, concat_axis=2, tiled=True)  5.2 us
    dot_general x2, local copies, waits for them, and re-layouts, lon_forward(): return jnp.einsum('ibln,nc->iblc', values, table, precision=HIGHEST)  3.76 us
    unnamed x35, local copies, waits for them, and re-layouts  3.56 us
  transfers between devices with their start and end apart: 4, of which 3 were waited for; matrix products, arithmetic and copies ran while one was open for 14% of the time, Pallas kernels for 0%

profile of v9, /device:TPU:1, one launch (start us, length us, event | category | flops | bytes accessed | tf_op | source)
XLA Modules:
  0.0 164.6 jit_solution(12307106002737518981)
XLA Ops:
  0.7 1.1 cosine_multiply_fusion.1
  2.6 0.6 convolution_bitcast_fusion.1
  3.2 1.3 copy.123
  4.6 11.9 %all-to-all-start = ((f32[2,96,4,256]{1,2,0,3:T(4,128)}), f32[2,96,4,256]{1,2,0,3:T(4,128)}, u32[]{:S(2)}, u32[]{:S(2)}) async-start(f32[2,96,4,256]{1,2,0,3:T(4,128)} %copy.123), calls=%async_computation | async-start | bytes 2097152 | tf_op jit(solution)/shard_map/all_to_all | solution.py:161
  16.5 1.0 copy.210
  17.6 1.3 collective-permute-start
  18.9 0.6 fusion.79
  20.1 0.7 compare_and_fusion
  20.8 0.6 sine_multiply_fusion.1
  21.5 1.1 cosine_multiply_fusion
  22.6 0.7 fusion.65
  23.3 0.8 pad_maximum_fusion.2
  24.1 0.6 fusion.64
  24.7 0.9 maximum_maximum_fusion
  25.7 19.3 %all-to-all-done = f32[2,96,4,256]{1,2,0,3:T(4,128)} async-done(((f32[2,96,4,256]{1,2,0,3:T(4,128)}), f32[2,96,4,256]{1,2,0,3:T(4,128)}, u32[]{:S(2)}, u32[]{:S(2)}) %all-to-all-start) | async-done | bytes 786464 | tf_op jit(solution)/shard_map/all_to_all | solution.py:161
  45.0 1.4 copy.124
  46.4 1.7 %copy.125 = f32[2,96,64,4,4]{1,3,2,4,0:T(4,128)} copy(f32[2,96,64,4,4]{1,4,2,3,0:T(4,128)S(1)} %bitcast.142) | data formatting | bytes 1572864 | tf_op jit(solution)/shard_map/all_to_all | solution.py:161
  48.1 1.5 fusion.17
  49.6 2.4 %copy.129 = f32[2,96,4,256]{1,2,0,3:T(4,128)} copy(f32[2,96,4,256]{3,1,2,0:T(8,128)} %fusion.17) | data formatting | bytes 1572864 | tf_op jit(solution)/shard_map/ibln,nc->iblc/dot_general | solution.py:50
  52.0 6.6 %all-to-all-start.1 = ((f32[2,96,4,256]{1,2,0,3:T(4,128)}), f32[2,96,4,256]{1,2,0,3:T(4,128)}, u32[]{:S(2)}, u32[]{:S(2)}) async-start(f32[2,96,4,256]{1,2,0,3:T(4,128)} %copy.129), calls=%async_computation.1 | async-start | bytes 2097152 | tf_op jit(solution)/shard_map/all_to_all | solution.py:161
  58.6 1.0 fusion.78
  59.6 0.7 copy.182
  60.6 0.6 bitcast_negate_fusion
  61.2 1.0 slice_bitcast_fusion
  62.2 1.0 convolution_bitcast_fusion.2
  64.3 22.8 %all-to-all-done.1 = f32[2,96,4,256]{1,2,0,3:T(4,128)} async-done(((f32[2,96,4,256]{1,2,0,3:T(4,128)}), f32[2,96,4,256]{1,2,0,3:T(4,128)}, u32[]{:S(2)}, u32[]{:S(2)}) %all-to-all-start.1) | async-done | bytes 786464 | tf_op jit(solution)/shard_map/all_to_all | solution.py:161
  87.1 1.4 copy.130
  88.5 0.7 copy.131
  89.2 1.1 fusion.80
  91.0 0.6 fusion.32
  91.6 1.7 %fusion.81 = (f32[2,192]{1,0:T(2,128)S(1)}, f32[2,192,256]{2,1,0:T(8,128)S(1)}) fusion(f32[2,192,256]{2,1,0:T(8,128)S(1)} %convolution_add_fusion, f32[2,192,256]{1,2,0:T(8,128)S(1)} %reshape.628, f32[2,96,96]{1,2,0:T(8,128)} %bitcast.153, f32[2,96,96]{1,2,0:T(8,128)S(1)} %bitcast.146, f32[2,96,96]{1,2,0:T(8,128)} %bitcast_negate_fusion), kind=kOutput, calls=%fused_computation.140 | convolution fusion | flops 115334784 | bytes 1402368 | tf_op jit(solution)/shard_map/kji,kjm->kim/dot_general | solution.py:114
  93.7 0.8 fusion.37
  97.2 0.6 convolution_bitcast_fusion
  97.8 2.1 %copy.141 = f32[64,2,2,96,4,2]{0,5,4,3,2,1:T(2,128)} copy(f32[64,2,2,96,4,2]{3,0,4,1,5,2:T(8,128)S(1)} %convolution_bitcast_fusion) | data formatting | bytes 1572864 | tf_op jit(solution)/shard_map/opfdr,ipbfj->doibrj/transpose | solution.py:83
  99.9 1.6 maximum_bitcast_fusion
  101.5 2.7 %copy.151 = f32[64,1,4236]{2,1,0:T(1,128)} copy(f32[64,1,4236]{0,2,1:T(8,128)S(1)} %maximum_bitcast_fusion) | data formatting | bytes 2168832 | tf_op jit(solution)/shard_map/all_to_all | solution.py:219
  104.1 36.1 %all_to_all.48 = f32[64,1,4236]{2,1,0:T(1,128)S(1)} all-to-all(f32[64,1,4236]{2,1,0:T(1,128)} %copy.151), channel_id=1, replica_groups=mesh['pipe'=8,'space'=64] {'space'}, dimensions={0} | all-to-all | bytes 2168832 | tf_op jit(solution)/shard_map/all_to_all | solution.py:219
  140.4 0.9 broadcast_in_dim.15
  141.3 6.2 %all-to-all-start.3 = ((f32[64,1,1164]{2,1,0:T(1,128)}), f32[64,1,1164]{2,1,0:T(1,128)S(1)}, u32[]{:S(2)}, u32[]{:S(2)}) async-start(f32[64,1,1164]{2,1,0:T(1,128)} %broadcast_in_dim.15), calls=%async_computation.3 | async-start | bytes 655360 | tf_op jit(solution)/shard_map/all_to_all | solution.py:225
  147.5 0.9 slice.104
  148.4 1.7 %copy.152 = f32[64,3072]{0,1:T(8,128)S(1)} copy(f32[64,3072]{1,0:T(8,128)} %slice.104) | data formatting | bytes 1572864 | tf_op jit(solution)/shard_map/slice | solution.py:222
  150.1 2.5 %fusion.6 = bf16[1,2,96,4,512]{4,2,3,1,0:T(8,128)(2,1)S(1)} fusion(f32[2,512,64,2]{1,2,0,3:T(8,128)} %pad_maximum_fusion.2, f32[64,2,2,96,4,2]{0,5,4,3,2,1:T(2,128)S(1)} %bitcast.137, bf16[2,96,4,512]{3,1,2,0:T(8,128)(2,1)} %copy-done.4, pred[]{:T(512)S(6)} %eq.14, bf16[1,2,96,4,512]{4,3,2,1,0:T(4,128)(2,1)S(1)} %copy-done.2), kind=kOutput, calls=%fused_computation.15 | convolution fusion | flops 605552640 | bytes 3670017 | tf_op jit(solution)/shard_map/dpiblj,pndj->ibln/dot_general | solution.py:92
  152.6 1.5 copy.154
  154.1 6.6 %all-to-all-done.3 = f32[64,1,1164]{2,1,0:T(1,128)S(1)} async-done(((f32[64,1,1164]{2,1,0:T(1,128)}), f32[64,1,1164]{2,1,0:T(1,128)S(1)}, u32[]{:S(2)}, u32[]{:S(2)}) %all-to-all-start.3) | async-done | bytes 298016 | tf_op jit(solution)/shard_map/all_to_all | solution.py:225
  160.7 0.9 multiply_reduce_fusion
  162.5 0.8 broadcast_in_dim_reshape.8
  163.2 0.6 fusion.74
  163.8 0.8 broadcast_in_dim_reshape.9
  (75 shorter events, 6.8 us)
Async XLA Ops:
  0.6 2.0 %copy-start = (bf16[1,2,96,4,512]{4,3,2,1,0:T(4,128)(2,1)S(1)}, bf16[1,2,96,4,512]{4,3,2,1,0:T(4,128)(2,1)}, u32[]{:S(2)}) copy-start(bf16[1,2,96,4,512]{4,3,2,1,0:T(4,128)(2,1)} %param.6) | copy-start | bytes 2359300
  3.2 13.3 %copy-start.1 = (bf16[1,2,96,4,512]{4,3,2,1,0:T(4,128)(2,1)S(1)}, bf16[1,2,96,4,512]{4,3,2,1,0:T(4,128)(2,1)}, u32[]{:S(2)}) copy-start(bf16[1,2,96,4,512]{4,3,2,1,0:T(4,128)(2,1)} %param.7) | copy-start | bytes 2359300
  4.6 14.3 %copy-start.14 = (s32[1,2]{1,0:T(1,128)S(1)}, s32[1,2]{1,0:T(1,128)}, u32[]{:S(2)}) copy-start(s32[1,2]{1,0:T(1,128)} %param.8) | copy-start | bytes 28
  4.6 40.4 %all-to-all-start = ((f32[2,96,4,256]{1,2,0,3:T(4,128)}), f32[2,96,4,256]{1,2,0,3:T(4,128)}, u32[]{:S(2)}, u32[]{:S(2)}) async-start(f32[2,96,4,256]{1,2,0,3:T(4,128)} %copy.123), calls=%async_computation | async-start | bytes 2097152 | tf_op jit(solution)/shard_map/all_to_all | solution.py:161
  17.6 30.5 %collective-permute-start = (bf16[2,96,4,512]{3,1,2,0:T(8,128)(2,1)}, bf16[2,96,4,512]{3,1,2,0:T(8,128)(2,1)S(1)}, u32[]{:S(2)}, u32[]{:S(2)}) collective-permute-start(bf16[2,96,4,512]{3,1,2,0:T(8,128)(2,1)} %bitcast.135), channel_id=1, source_target_pairs={{64,0},{128,64},{192,128},{256,192},{320,256},{384,320},{448,384},... | collective-permute-start | bytes 2359304 | tf_op jit(solution)/shard_map/ppermute | solution.py:20
  48.1 3.9 %copy-start.4 = (bf16[2,96,4,512]{3,1,2,0:T(8,128)(2,1)}, bf16[2,96,4,512]{3,1,2,0:T(8,128)(2,1)S(1)}, u32[]{:S(2)}) copy-start(bf16[2,96,4,512]{3,1,2,0:T(8,128)(2,1)S(1)} %collective-permute-done) | copy-start | bytes 2359300
  52.0 8.4 %copy-start.13 = (f32[1,2,2,96]{3,2,1,0:T(2,128)S(1)}, f32[1,2,2,96]{3,2,1,0:T(2,128)}, u32[]{:S(2)}) copy-start(f32[1,2,2,96]{3,2,1,0:T(2,128)} %param.10) | copy-start | bytes 4612
  52.0 8.5 %copy-start.10 = (f32[1,2,2,96,96]{4,3,2,1,0:T(8,128)S(1)}, f32[1,2,2,96,96]{4,3,2,1,0:T(8,128)}, u32[]{:S(2)}) copy-start(f32[1,2,2,96,96]{4,3,2,1,0:T(8,128)} %param.9) | copy-start | bytes 442372
  52.0 10.1 %copy-start.3 = (f32[2,96,64,4,4]{1,3,2,4,0:T(4,128)S(1)}, f32[2,96,64,4,4]{1,3,2,4,0:T(4,128)}, u32[]{:S(2)}) copy-start(f32[2,96,64,4,4]{1,3,2,4,0:T(4,128)} %copy.125) | copy-start | bytes 2359300
  52.0 35.1 %all-to-all-start.1 = ((f32[2,96,4,256]{1,2,0,3:T(4,128)}), f32[2,96,4,256]{1,2,0,3:T(4,128)}, u32[]{:S(2)}, u32[]{:S(2)}) async-start(f32[2,96,4,256]{1,2,0,3:T(4,128)} %copy.129), calls=%async_computation.1 | async-start | bytes 2097152 | tf_op jit(solution)/shard_map/all_to_all | solution.py:161
  60.4 0.8 copy-start.11
  62.2 1.7 %copy-start.6 = (f32[2,96,96]{2,1,0:T(8,128)}, f32[2,96,96]{2,1,0:T(8,128)S(1)}, u32[]{:S(2)}) copy-start(f32[2,96,96]{2,1,0:T(8,128)S(1)} %get-tuple-element.54) | copy-start | bytes 221188
  62.2 1.7 %copy-start.8 = (f32[2,96,96]{2,1,0:T(8,128)}, f32[2,96,96]{2,1,0:T(8,128)S(1)}, u32[]{:S(2)}) copy-start(f32[2,96,96]{2,1,0:T(8,128)S(1)} %get-tuple-element.55) | copy-start | bytes 221188
  90.6 0.9 copy-start.12
  91.6 2.1 %copy-start.7 = (f32[2,96,96]{2,1,0:T(8,128)S(1)}, f32[2,96,96]{2,1,0:T(8,128)}, u32[]{:S(2)}) copy-start(f32[2,96,96]{2,1,0:T(8,128)} %copy-done.6) | copy-start | bytes 221188
  91.6 2.1 %copy-start.9 = (f32[2,96,96]{2,1,0:T(8,128)S(1)}, f32[2,96,96]{2,1,0:T(8,128)}, u32[]{:S(2)}) copy-start(f32[2,96,96]{2,1,0:T(8,128)} %copy-done.8) | copy-start | bytes 221188
  96.2 1.0 copy-start.5
  141.3 19.5 %all-to-all-start.3 = ((f32[64,1,1164]{2,1,0:T(1,128)}), f32[64,1,1164]{2,1,0:T(1,128)S(1)}, u32[]{:S(2)}, u32[]{:S(2)}) async-start(f32[64,1,1164]{2,1,0:T(1,128)} %broadcast_in_dim.15), calls=%async_computation.3 | async-start | bytes 655360 | tf_op jit(solution)/shard_map/all_to_all | solution.py:225
  148.4 1.7 %copy-start.2 = (bf16[1,2,96,4,512]{4,3,2,1,0:T(4,128)(2,1)S(1)}, bf16[1,2,96,4,512]{4,3,2,1,0:T(4,128)(2,1)}, u32[]{:S(2)}) copy-start(bf16[1,2,96,4,512]{4,3,2,1,0:T(4,128)(2,1)} %param.7) | copy-start | bytes 2359300

commit v10 on v8

--- a/solution.py
+++ b/solution.py
@@ -178,10 +178,10 @@
     lat_cos, lat_sin = lat_tables(LAT, KEEP_LAT)
     table = lon_forward_table(lon_cos, lon_sin, ndev)
     col_field = to_columns(lon_forward(field, table), ndev)
-    col_field, received = lax.optimization_barrier((col_field, received))
+    upstream = jnp.where(section_index == last_section, own_grad, received)
+    col_field, lon_grad = lax.optimization_barrier((col_field, lon_forward(upstream, table)))
     spectrum = lat_forward(col_field, lat_cos, lat_sin)
-    upstream = jnp.where(section_index == last_section, own_grad, received)
-    col_grad = to_columns(lon_forward(upstream, table), ndev)
+    col_grad = to_columns(lon_grad, ndev)
     grad_spec = lat_forward(col_grad, lat_cos, lat_sin)
     share = KEEP_LON // ndev
     signed = jnp.arange(2 * KEEP_LAT, dtype=jnp.int32) - KEEP_LAT

time: 162 us -> 164 us (1.012); the launches traced: 162 us -> 162 us
    dot_general x2 -> x1, local copies, waits for them, and re-layouts: 3.8 us -> 1.33 us  [lon_forward(): return jnp.einsum('ibln,nc->iblc', values, table, precision=HIGHEST)]
    unnamed x45 -> x47, local copies, waits for them, and re-layouts: 4.53 us -> 6.16 us
  transfers between devices with their start and end apart: 4 -> 4, of which waited for: 3 -> 3; matrix products, arithmetic and copies ran while one was open for 15% -> 18% of each run, Pallas kernels for 0% -> 0%
where the time goes in v10:
time: 164 us; the launch traced here: 162 us
  waiting for transfers between devices  44.1 us (27%)
  blocking collectives  36.1 us (22%)
  local copies, waits for them, and re-layouts  29 us (18%)
  starting transfers between devices  25.8 us (16%)
  other arithmetic  12.9 us (8%)
  matrix products  12.1 us (7%)
  between operations  1.86 us (1%)
    all_to_all x2, waiting for transfers between devices, to_columns(): lax.all_to_all(spectrum, 'space', split_axis=3, concat_axis=2, tiled=True)  39.4 us
    all_to_all x1, blocking collectives, shards(): lax.all_to_all(jnp.concatenate([back, pieces], axis=1), 'space', split_ax...  36.1 us
    all_to_all x2, starting transfers between devices, to_columns(): lax.all_to_all(spectrum, 'space', split_axis=3, concat_axis=2, tiled=True)  18.1 us
    all_to_all x1, starting transfers between devices, shards(): lax.all_to_all(spread, 'space', split_axis=0, concat_axis=0, tiled=True)  6.41 us
    unnamed x47, local copies, waits for them, and re-layouts  6.16 us
    all_to_all x1, waiting for transfers between devices, shards(): lax.all_to_all(spread, 'space', split_axis=0, concat_axis=0, tiled=True)  4.65 us
  transfers between devices with their start and end apart: 4, of which 3 were waited for; matrix products, arithmetic and copies ran while one was open for 18% of the time, Pallas kernels for 0%

profile of v10, /device:TPU:1, one launch (start us, length us, event | category | flops | bytes accessed | tf_op | source)
XLA Modules:
  0.0 161.8 jit_solution(15485397095282385140)
XLA Ops:
  0.6 2.2 %copy.210 = bf16[1,2,96,4,512]{4,2,3,1,0:T(8,128)(2,1)} copy(bf16[1,2,96,4,512]{4,3,2,1,0:T(4,128)(2,1)} %param.7) | data formatting | bytes 1572864 | tf_op args[1]
  2.9 1.3 collective-permute-start
  4.2 1.1 cosine_multiply_fusion.1
  6.2 0.6 convolution_bitcast_fusion.1
  6.8 1.3 copy.125
  8.1 11.7 %all-to-all-start = ((f32[2,96,4,256]{1,2,0,3:T(4,128)}), f32[2,96,4,256]{1,2,0,3:T(4,128)S(1)}, u32[]{:S(2)}, u32[]{:S(2)}) async-start(f32[2,96,4,256]{1,2,0,3:T(4,128)} %copy.125), calls=%async_computation | async-start | bytes 2097152 | tf_op jit(solution)/shard_map/all_to_all | solution.py:152
  19.9 0.6 fusion.85
  21.2 0.7 copy.183
  21.9 0.7 copy.182
  22.6 0.7 compare_and_fusion
  23.3 0.7 fusion.67
  24.1 0.6 sine_multiply_fusion.1
  24.7 0.9 maximum_bitcast_fusion.10
  25.6 2.6 %fusion.19 = f32[2,96,4,256]{3,1,2,0:T(8,128)} fusion(f32[512,256]{0,1:T(8,128)S(1)} %reshape.666, bf16[2,96,4,512]{3,1,2,0:T(8,128)(2,1)} %collective-permute-done, pred[]{:T(512)S(6)} %eq.14, bf16[1,2,96,4,512]{4,3,2,1,0:T(4,128)(2,1)S(1)} %copy-done.1), kind=kOutput, calls=%fused_computation.34 | convolution fusion | flops 604372992 | bytes 2883585 | tf_op jit(solution)/shard_map/ibln,nc->iblc/dot_general | solution.py:50
  28.2 20.3 %all-to-all-done = f32[2,96,4,256]{1,2,0,3:T(4,128)S(1)} async-done(((f32[2,96,4,256]{1,2,0,3:T(4,128)}), f32[2,96,4,256]{1,2,0,3:T(4,128)S(1)}, u32[]{:S(2)}, u32[]{:S(2)}) %all-to-all-start) | async-done | bytes 786464 | tf_op jit(solution)/shard_map/all_to_all | solution.py:152
  48.7 0.7 copy.127
  49.8 1.3 copy.129
  51.1 6.3 %all-to-all-start.1 = ((f32[2,96,4,256]{1,2,0,3:T(4,128)}), f32[2,96,4,256]{1,2,0,3:T(4,128)S(1)}, u32[]{:S(2)}, u32[]{:S(2)}) async-start(f32[2,96,4,256]{1,2,0,3:T(4,128)} %copy.129), calls=%async_computation.1 | async-start | bytes 2097152 | tf_op jit(solution)/shard_map/all_to_all | solution.py:152
  57.5 0.9 fusion.79
  58.4 1.5 bitcast_negate_fusion
  60.0 1.6 %slice_bitcast_fusion = (f32[2,96,96]{2,1,0:T(8,128)}, f32[2,96,96]{2,1,0:T(8,128)}) fusion(f32[1,2,2,96,96]{4,3,2,1,0:T(8,128)} %param.9), kind=kLoop, calls=%fused_computation.113 | loop fusion | bytes 294912 | tf_op jit(solution)/shard_map/squeeze | solution.py:94
  61.6 1.3 fusion.66
  62.9 1.8 %convolution_bitcast_fusion.2 = f32[2,2,96,128,2]{3,2,1,4,0:T(8,128)} fusion(f32[1,128,2,256]{3,1,2,0:T(8,128)S(1)} %copy-done.6, f32[1,128,2,256]{3,1,2,0:T(8,128)S(1)} %copy-done.4, f32[2,96,256,2,2]{1,2,4,3,0:T(8,128)S(1)} %bitcast.143), kind=kOutput, calls=%fused_computation.7 | convolution fusion | flops 302120960 | bytes 1703936 | tf_op jit(solution)/shard_map/ofpl,iblpj->iobfj/dot_general | solution.py:57
  64.7 1.4 copy.136
  66.8 19.2 %all-to-all-done.1 = f32[2,96,4,256]{1,2,0,3:T(4,128)S(1)} async-done(((f32[2,96,4,256]{1,2,0,3:T(4,128)}), f32[2,96,4,256]{1,2,0,3:T(4,128)S(1)}, u32[]{:S(2)}, u32[]{:S(2)}) %all-to-all-start.1) | async-done | bytes 786464 | tf_op jit(solution)/shard_map/all_to_all | solution.py:152
  86.2 0.7 copy.131
  87.3 1.1 fusion.86
  89.0 0.6 fusion.34
  89.6 0.7 fusion.87
  90.7 0.8 fusion.39
  94.2 0.6 convolution_bitcast_fusion
  94.8 2.1 %copy.141 = f32[64,2,2,96,4,2]{0,5,4,3,2,1:T(2,128)} copy(f32[64,2,2,96,4,2]{3,0,4,1,5,2:T(8,128)S(1)} %convolution_bitcast_fusion) | data formatting | bytes 1572864 | tf_op jit(solution)/shard_map/opfdr,ipbfj->doibrj/transpose | solution.py:77
  96.9 1.6 maximum_bitcast_fusion
  98.5 2.6 %copy.151 = f32[64,1,4236]{2,1,0:T(1,128)} copy(f32[64,1,4236]{0,2,1:T(8,128)S(1)} %maximum_bitcast_fusion) | data formatting | bytes 2168832 | tf_op jit(solution)/shard_map/all_to_all | solution.py:203
  101.1 36.1 %all_to_all.48 = f32[64,1,4236]{2,1,0:T(1,128)S(1)} all-to-all(f32[64,1,4236]{2,1,0:T(1,128)} %copy.151), channel_id=1, replica_groups=mesh['pipe'=8,'space'=64] {'space'}, dimensions={0} | all-to-all | bytes 2168832 | tf_op jit(solution)/shard_map/all_to_all | solution.py:203
  137.4 0.9 broadcast_in_dim.15
  138.3 6.4 %all-to-all-start.3 = ((f32[64,1,1164]{2,1,0:T(1,128)}), f32[64,1,1164]{2,1,0:T(1,128)S(1)}, u32[]{:S(2)}, u32[]{:S(2)}) async-start(f32[64,1,1164]{2,1,0:T(1,128)} %broadcast_in_dim.15), calls=%async_computation.3 | async-start | bytes 655360 | tf_op jit(solution)/shard_map/all_to_all | solution.py:209
  144.7 2.0 %cosine_multiply_fusion = (f32[1,512,64,2]{1,2,0,3:T(8,128)}, f32[1,512,64,2]{1,2,0,3:T(8,128)}) fusion(s32[64,2]{0,1:T(2,128)S(1)} %copy-done.18), kind=kLoop, calls=%fused_computation.73 | loop fusion | flops 1114112 | bytes 524800 | tf_op jit(solution)/shard_map/mul | solution.py:29
  146.7 0.9 slice.104
  147.6 1.7 %copy.152 = f32[64,3072]{0,1:T(8,128)S(1)} copy(f32[64,3072]{1,0:T(8,128)} %slice.104) | data formatting | bytes 1572864 | tf_op jit(solution)/shard_map/slice | solution.py:206
  149.3 2.5 %fusion.6 = bf16[1,2,96,4,512]{4,2,3,1,0:T(8,128)(2,1)S(1)} fusion(f32[64,2,2,96,4,2]{0,5,4,3,2,1:T(2,128)S(1)} %bitcast.136, f32[1,512,64,2]{1,2,0,3:T(8,128)} %get-tuple-element.56, f32[1,512,64,2]{1,2,0,3:T(8,128)} %get-tuple-element.55, bf16[2,96,4,512]{3,1,2,0:T(8,128)(2,1)} %collective-permute-done, pred[]{:T(512)S(6)} %eq.14, ...), kind=kOutput, calls=%fused_computation.15 | convolution fusion | flops 605683712 | bytes 3670017 | tf_op jit(solution)/shard_map/dpiblj,pndj->ibln/dot_general | solution.py:83
  151.8 1.5 copy.154
  153.3 4.7 %all-to-all-done.3 = f32[64,1,1164]{2,1,0:T(1,128)S(1)} async-done(((f32[64,1,1164]{2,1,0:T(1,128)}), f32[64,1,1164]{2,1,0:T(1,128)S(1)}, u32[]{:S(2)}, u32[]{:S(2)}) %all-to-all-start.3) | async-done | bytes 298016 | tf_op jit(solution)/shard_map/all_to_all | solution.py:209
  157.9 0.9 multiply_reduce_fusion
  159.1 0.6 mul.535
  159.7 0.8 broadcast_in_dim_reshape.8
  160.4 0.8 broadcast_in_dim_reshape.9
  161.2 0.6 fusion.80
  (84 shorter events, 6.9 us)
Async XLA Ops:
  0.6 5.5 %copy-start = (bf16[1,2,96,4,512]{4,3,2,1,0:T(4,128)(2,1)S(1)}, bf16[1,2,96,4,512]{4,3,2,1,0:T(4,128)(2,1)}, u32[]{:S(2)}) copy-start(bf16[1,2,96,4,512]{4,3,2,1,0:T(4,128)(2,1)} %param.6) | copy-start | bytes 2359300
  2.9 22.7 %collective-permute-start = (bf16[2,96,4,512]{3,1,2,0:T(8,128)(2,1)}, bf16[2,96,4,512]{3,1,2,0:T(8,128)(2,1)}, u32[]{:S(2)}, u32[]{:S(2)}) collective-permute-start(bf16[2,96,4,512]{3,1,2,0:T(8,128)(2,1)} %bitcast.134), channel_id=1, source_target_pairs={{64,0},{128,64},{192,128},{256,192},{320,256},{384,320},{448,384},... | collective-permute-start | bytes 2359304 | tf_op jit(solution)/shard_map/ppermute | solution.py:20
  4.2 1.1 copy-start.17
  6.8 13.1 %copy-start.20 = (s32[1,2]{1,0:T(1,128)S(1)}, s32[1,2]{1,0:T(1,128)}, u32[]{:S(2)}) copy-start(s32[1,2]{1,0:T(1,128)} %param.8) | copy-start | bytes 28
  6.8 14.4 %copy-start.14 = (f32[1,2,2,96,96]{4,3,2,1,0:T(8,128)S(1)}, f32[1,2,2,96,96]{4,3,2,1,0:T(8,128)}, u32[]{:S(2)}) copy-start(f32[1,2,2,96,96]{4,3,2,1,0:T(8,128)} %param.11) | copy-start | bytes 442372
  8.1 15.9 %copy-start.19 = (f32[1,2,2,96]{3,2,1,0:T(2,128)S(1)}, f32[1,2,2,96]{3,2,1,0:T(2,128)}, u32[]{:S(2)}) copy-start(f32[1,2,2,96]{3,2,1,0:T(2,128)} %param.10) | copy-start | bytes 4612
  8.1 40.3 %all-to-all-start = ((f32[2,96,4,256]{1,2,0,3:T(4,128)}), f32[2,96,4,256]{1,2,0,3:T(4,128)S(1)}, u32[]{:S(2)}, u32[]{:S(2)}) async-start(f32[2,96,4,256]{1,2,0,3:T(4,128)} %copy.125), calls=%async_computation | async-start | bytes 2097152 | tf_op jit(solution)/shard_map/all_to_all | solution.py:152
  19.9 5.7 %copy-start.1 = (bf16[1,2,96,4,512]{4,3,2,1,0:T(4,128)(2,1)S(1)}, bf16[1,2,96,4,512]{4,3,2,1,0:T(4,128)(2,1)}, u32[]{:S(2)}) copy-start(bf16[1,2,96,4,512]{4,3,2,1,0:T(4,128)(2,1)} %param.7) | copy-start | bytes 2359300
  48.7 1.1 copy-start.3
  51.1 11.8 %copy-start.4 = (f32[1,128,2,256]{3,1,2,0:T(8,128)S(1)}, f32[1,128,2,256]{3,1,2,0:T(8,128)}, u32[]{:S(2)}) copy-start(f32[1,128,2,256]{3,1,2,0:T(8,128)} %get-tuple-element.48) | copy-start | bytes 786436
  51.1 11.8 %copy-start.6 = (f32[1,128,2,256]{3,1,2,0:T(8,128)S(1)}, f32[1,128,2,256]{3,1,2,0:T(8,128)}, u32[]{:S(2)}) copy-start(f32[1,128,2,256]{3,1,2,0:T(8,128)} %get-tuple-element.49) | copy-start | bytes 786436
  51.1 34.9 %all-to-all-start.1 = ((f32[2,96,4,256]{1,2,0,3:T(4,128)}), f32[2,96,4,256]{1,2,0,3:T(4,128)S(1)}, u32[]{:S(2)}, u32[]{:S(2)}) async-start(f32[2,96,4,256]{1,2,0,3:T(4,128)} %copy.129), calls=%async_computation.1 | async-start | bytes 2097152 | tf_op jit(solution)/shard_map/all_to_all | solution.py:152
  64.7 1.7 %copy-start.8 = (f32[2,96,96]{2,1,0:T(8,128)S(1)}, f32[2,96,96]{2,1,0:T(8,128)}, u32[]{:S(2)}) copy-start(f32[2,96,96]{2,1,0:T(8,128)} %get-tuple-element.46) | copy-start | bytes 221188
  64.7 1.7 %copy-start.9 = (f32[2,96,96]{2,1,0:T(8,128)S(1)}, f32[2,96,96]{2,1,0:T(8,128)}, u32[]{:S(2)}) copy-start(f32[2,96,96]{2,1,0:T(8,128)} %get-tuple-element.47) | copy-start | bytes 221188
  86.2 1.0 copy-start.5
  86.2 1.0 copy-start.7
  88.4 1.3 copy-start.13
  88.4 1.3 copy-start.15
  88.4 1.3 copy-start.16
  93.2 1.0 copy-start.10
  93.2 1.0 copy-start.11
  93.2 1.0 copy-start.12
  137.3 7.4 %copy-start.18 = (s32[64,2]{0,1:T(2,128)S(1)}, s32[64,2]{0,1:T(2,128)}, u32[]{:S(2)}) copy-start(s32[64,2]{0,1:T(2,128)} %copy-done.17) | copy-start | bytes 1540
  138.3 19.7 %all-to-all-start.3 = ((f32[64,1,1164]{2,1,0:T(1,128)}), f32[64,1,1164]{2,1,0:T(1,128)S(1)}, u32[]{:S(2)}, u32[]{:S(2)}) async-start(f32[64,1,1164]{2,1,0:T(1,128)} %broadcast_in_dim.15), calls=%async_computation.3 | async-start | bytes 655360 | tf_op jit(solution)/shard_map/all_to_all | solution.py:209
  147.6 1.7 %copy-start.2 = (bf16[1,2,96,4,512]{4,3,2,1,0:T(4,128)(2,1)S(1)}, bf16[1,2,96,4,512]{4,3,2,1,0:T(4,128)(2,1)}, u32[]{:S(2)}) copy-start(bf16[1,2,96,4,512]{4,3,2,1,0:T(4,128)(2,1)} %param.7) | copy-start | bytes 2359300

commit v11 on v10

--- a/solution.py
+++ b/solution.py
@@ -177,11 +177,13 @@
     lon_cos, lon_sin = lon_tables(LON, KEEP_LON)
     lat_cos, lat_sin = lat_tables(LAT, KEEP_LAT)
     table = lon_forward_table(lon_cos, lon_sin, ndev)
+    own_lon = lon_forward(own_grad, table)
+    received_lon = from_behind(own_lon, "pipe", -1)
     col_field = to_columns(lon_forward(field, table), ndev)
-    upstream = jnp.where(section_index == last_section, own_grad, received)
-    col_field, lon_grad = lax.optimization_barrier((col_field, lon_forward(upstream, table)))
+    upstream_lon = jnp.where(section_index == last_section, own_lon, received_lon)
+    col_field, upstream_lon = lax.optimization_barrier((col_field, upstream_lon))
     spectrum = lat_forward(col_field, lat_cos, lat_sin)
-    col_grad = to_columns(lon_grad, ndev)
+    col_grad = to_columns(upstream_lon, ndev)
     grad_spec = lat_forward(col_grad, lat_cos, lat_sin)
     share = KEEP_LON // ndev
     signed = jnp.arange(2 * KEEP_LAT, dtype=jnp.int32) - KEEP_LAT
@@ -200,9 +202,8 @@
     flat = jnp.concatenate([p.reshape(-1) for p in parts])
     pad = (-flat.shape[0]) % ndev
     pieces = jnp.pad(flat, (0, pad)).reshape(ndev, -1)
-    moved = lax.all_to_all(
-        jnp.concatenate([back, pieces], axis=1), "space", split_axis=0, concat_axis=0, tiled=True
-    )
+    joined, received = lax.optimization_barrier((jnp.concatenate([back, pieces], axis=1), received))
+    moved = lax.all_to_all(joined, "space", split_axis=0, concat_axis=0, tiled=True)
     rows_back = moved[:, : back.shape[1]].reshape(ndev, 2, nblocks, width, rows, share)
     mine = jnp.sum(moved[:, back.shape[1]:], axis=0)
     spread = jnp.broadcast_to(mine[None], pieces.shape)
@@ -216,6 +217,7 @@
     for p in parts:
         sums.append(flat[start:start + p.size].reshape(p.shape)[None])
         start += p.size
+    upstream = jnp.where(section_index == last_section, own_grad, received)
     grad_field = (upstream.astype(jnp.float32) + inverse).astype(jnp.bfloat16)
     return (grad_field[None], *sums)
 

time: 164 us -> 166 us (1.012)
  blocking collectives: 36.1 us -> 0 us
  waiting for transfers between devices: 44.1 us -> 74.6 us
  starting transfers between devices: 25.8 us -> 33.2 us
  other arithmetic: 12.9 us -> 15.7 us
  local copies, waits for them, and re-layouts: 29 us -> 26.8 us
    all_to_all x1 -> x0, blocking collectives: 36.1 us -> none  [shards(): lax.all_to_all(jnp.concatenate([back, pieces], axis=1), 'space', split_ax...]
    all_to_all x0 -> x1, waiting for transfers between devices: none -> 28 us  [shards(): lax.all_to_all(joined, 'space', split_axis=0, concat_axis=0, tiled=True)]
    all_to_all x0 -> x1, starting transfers between devices: none -> 6.33 us  [shards(): lax.all_to_all(joined, 'space', split_axis=0, concat_axis=0, tiled=True)]
    all_to_all x1, waiting for transfers between devices: 4.65 us -> 8.13 us  [shards(): lax.all_to_all(spread, 'space', split_axis=0, concat_axis=0, tiled=True)]
    slice x2, local copies, waits for them, and re-layouts: 2.6 us -> 0.52 us  [shards(): moved[:, :back.shape[1]].reshape(ndev, 2, nblocks, width, rows, share)]
    unnamed x47 -> x39, local copies, waits for them, and re-layouts: 6.16 us -> 4.83 us
  transfers between devices with their start and end apart: 4 -> 6, of which waited for: 3 -> 4; matrix products, arithmetic and copies ran while one was open for 18% -> 26% of each run, Pallas kernels for 0% -> 0%
where the time goes in v11:
time: 166 us; the launch traced here: 164 us
  waiting for transfers between devices  74.6 us (45%)
  starting transfers between devices  33.2 us (20%)
  local copies, waits for them, and re-layouts  26.8 us (16%)
  other arithmetic  15.7 us (9%)
  matrix products  11.5 us (7%)
  between operations  1.87 us (1%)
    all_to_all x2, waiting for transfers between devices, to_columns(): lax.all_to_all(spectrum, 'space', split_axis=3, concat_axis=2, tiled=True)  38.4 us
    all_to_all x1, waiting for transfers between devices, shards(): lax.all_to_all(joined, 'space', split_axis=0, concat_axis=0, tiled=True)  28 us
    all_to_all x2, starting transfers between devices, to_columns(): lax.all_to_all(spectrum, 'space', split_axis=3, concat_axis=2, tiled=True)  18.1 us
    all_to_all x1, waiting for transfers between devices, shards(): lax.all_to_all(spread, 'space', split_axis=0, concat_axis=0, tiled=True)  8.13 us
    all_to_all x1, starting transfers between devices, shards(): lax.all_to_all(joined, 'space', split_axis=0, concat_axis=0, tiled=True)  6.33 us
    all_to_all x1, starting transfers between devices, shards(): lax.all_to_all(spread, 'space', split_axis=0, concat_axis=0, tiled=True)  6.19 us
    unnamed x39, local copies, waits for them, and re-layouts  4.83 us
  transfers between devices with their start and end apart: 6, of which 4 were waited for; matrix products, arithmetic and copies ran while one was open for 26% of the time, Pallas kernels for 0%

profile of v11, /device:TPU:1, one launch (start us, length us, event | category | flops | bytes accessed | tf_op | source)
XLA Modules:
  0.0 163.5 jit_solution(12574500931067330035)
XLA Ops:
  0.7 1.1 cosine_multiply_fusion.1
  2.9 0.6 convolution_bitcast_fusion.1
  3.6 1.3 collective-permute-start
  4.9 1.5 convolution_bitcast_fusion.2
  6.4 2.5 %copy.125 = f32[2,96,4,256]{1,2,0,3:T(4,128)} copy(f32[2,96,4,256]{3,1,2,0:T(8,128)} %convolution_bitcast_fusion.2) | data formatting | bytes 1572864 | tf_op jit(solution)/shard_map/ibln,nc->iblc/dot_general | solution.py:50
  8.8 11.8 %all-to-all-start = ((f32[2,96,4,256]{1,2,0,3:T(4,128)}), f32[2,96,4,256]{1,2,0,3:T(4,128)S(1)}, u32[]{:S(2)}, u32[]{:S(2)}) async-start(f32[2,96,4,256]{1,2,0,3:T(4,128)} %copy.125), calls=%async_computation | async-start | bytes 2097152 | tf_op jit(solution)/shard_map/all_to_all | solution.py:152
  20.6 1.0 copy.206
  21.6 1.3 collective-permute-start.1
  23.0 0.6 fusion.82
  24.2 0.7 copy.183
  24.9 0.7 copy.182
  25.7 0.7 compare_and_fusion
  26.3 0.7 fusion.64
  27.1 0.6 sine_multiply_fusion.1
  27.7 0.9 maximum_bitcast_fusion.7
  28.6 1.2 broadcast_select_fusion
  29.8 19.3 %all-to-all-done = f32[2,96,4,256]{1,2,0,3:T(4,128)S(1)} async-done(((f32[2,96,4,256]{1,2,0,3:T(4,128)}), f32[2,96,4,256]{1,2,0,3:T(4,128)S(1)}, u32[]{:S(2)}, u32[]{:S(2)}) %all-to-all-start) | async-done | bytes 786464 | tf_op jit(solution)/shard_map/all_to_all | solution.py:152
  49.3 0.7 copy.127
  50.0 1.3 copy.129
  51.4 6.3 %all-to-all-start.1 = ((f32[2,96,4,256]{1,2,0,3:T(4,128)}), f32[2,96,4,256]{1,2,0,3:T(4,128)S(1)}, u32[]{:S(2)}, u32[]{:S(2)}) async-start(f32[2,96,4,256]{1,2,0,3:T(4,128)} %copy.129), calls=%async_computation.1 | async-start | bytes 2097152 | tf_op jit(solution)/shard_map/all_to_all | solution.py:152
  57.8 0.9 fusion.76
  58.7 1.5 bitcast_negate_fusion
  60.2 1.6 slice_bitcast_fusion
  61.8 1.4 fusion.63
  63.2 1.8 %convolution_bitcast_fusion.3 = f32[2,2,96,128,2]{3,2,1,4,0:T(8,128)} fusion(f32[1,128,2,256]{3,1,2,0:T(8,128)S(1)} %copy-done.5, f32[1,128,2,256]{3,1,2,0:T(8,128)S(1)} %copy-done.3, f32[2,96,256,2,2]{1,2,4,3,0:T(8,128)S(1)} %bitcast.141), kind=kOutput, calls=%fused_computation.8 | convolution fusion | flops 302120960 | bytes 1703936 | tf_op jit(solution)/shard_map/ofpl,iblpj->iobfj/dot_general | solution.py:57
  65.0 1.4 copy.136
  67.1 19.1 %all-to-all-done.1 = f32[2,96,4,256]{1,2,0,3:T(4,128)S(1)} async-done(((f32[2,96,4,256]{1,2,0,3:T(4,128)}), f32[2,96,4,256]{1,2,0,3:T(4,128)S(1)}, u32[]{:S(2)}, u32[]{:S(2)}) %all-to-all-start.1) | async-done | bytes 786464 | tf_op jit(solution)/shard_map/all_to_all | solution.py:152
  86.5 0.7 copy.131
  87.5 1.1 fusion.83
  89.2 0.6 fusion.31
  89.8 1.8 %fusion.84 = (f32[2,192]{1,0:T(2,128)S(1)}, f32[2,192,256]{2,1,0:T(8,128)S(1)}) fusion(f32[2,192,256]{2,1,0:T(8,128)S(1)} %convolution_add_fusion, f32[2,192,256]{1,2,0:T(8,128)S(1)} %reshape.669, f32[2,96,96]{1,2,0:T(8,128)} %bitcast.150, f32[2,96,96]{1,2,0:T(8,128)} %bitcast.143, f32[2,96,96]{1,2,0:T(8,128)} %bitcast_negate_fusion), kind=kOutput, calls=%fused_computation.148 | convolution fusion | flops 115334784 | bytes 1402368 | tf_op jit(solution)/shard_map/kji,kjm->kim/dot_general | solution.py:105
  93.7 0.8 fusion.36
  95.5 0.6 convolution_bitcast_fusion
  96.1 2.1 %copy.141 = f32[64,2,2,96,4,2]{0,5,4,3,2,1:T(2,128)} copy(f32[64,2,2,96,4,2]{3,0,4,1,5,2:T(8,128)S(1)} %convolution_bitcast_fusion) | data formatting | bytes 1572864 | tf_op jit(solution)/shard_map/opfdr,ipbfj->doibrj/transpose | solution.py:77
  98.2 1.6 pad_maximum_fusion
  99.7 2.6 %copy.151 = f32[64,1,4236]{2,1,0:T(1,128)} copy(f32[64,1,4236]{0,2,1:T(8,128)S(1)} %bitcast.133) | data formatting | bytes 2168832 | tf_op jit(solution)/shard_map/all_to_all | solution.py:206
  102.4 6.3 %all-to-all-start.2 = ((f32[64,1,4236]{2,1,0:T(1,128)}), f32[64,1,4236]{2,1,0:T(1,128)S(1)}, u32[]{:S(2)}, u32[]{:S(2)}) async-start(f32[64,1,4236]{2,1,0:T(1,128)} %copy.151), calls=%async_computation.2 | async-start | bytes 2228224 | tf_op jit(solution)/shard_map/all_to_all | solution.py:206
  108.7 1.9 %cosine_multiply_fusion = (f32[1,512,64,2]{1,2,0,3:T(8,128)S(1)}, f32[1,512,64,2]{1,2,0,3:T(8,128)}) fusion(s32[64,2]{0,1:T(2,128)S(1)} %copy-done.14), kind=kLoop, calls=%fused_computation.73 | loop fusion | flops 1114112 | bytes 524800 | tf_op jit(solution)/shard_map/mul | solution.py:29
  110.6 28.0 %all-to-all-done.2 = f32[64,1,4236]{2,1,0:T(1,128)S(1)} async-done(((f32[64,1,4236]{2,1,0:T(1,128)}), f32[64,1,4236]{2,1,0:T(1,128)S(1)}, u32[]{:S(2)}, u32[]{:S(2)}) %all-to-all-start.2) | async-done | bytes 1084448 | tf_op jit(solution)/shard_map/all_to_all | solution.py:206
  139.3 0.9 broadcast_in_dim.15
  140.2 6.2 %all-to-all-start.3 = ((f32[64,1,1164]{2,1,0:T(1,128)}), f32[64,1,1164]{2,1,0:T(1,128)S(1)}, u32[]{:S(2)}, u32[]{:S(2)}) async-start(f32[64,1,1164]{2,1,0:T(1,128)} %broadcast_in_dim.15), calls=%async_computation.3 | async-start | bytes 655360 | tf_op jit(solution)/shard_map/all_to_all | solution.py:210
  146.4 2.0 %fusion.1 = f32[2,96,4,512,1,1]{3,1,5,4,2,0:T(8,128)S(1)} fusion(f32[64,2,2,96,4,2]{0,5,4,3,2,1:T(2,128)S(1)} %bitcast.134, f32[1,512,64,2]{1,2,0,3:T(8,128)} %get-tuple-element.60, f32[1,512,64,2]{1,2,0,3:T(8,128)S(1)} %get-tuple-element.59), kind=kOutput, calls=%fused_computation.3 | convolution fusion | flops 604110848 | bytes 2883584 | tf_op jit(solution)/shard_map/dpiblj,pndj->ibln/dot_general | solution.py:83
  148.5 1.6 fusion.6
  150.1 1.5 copy.154
  151.5 8.1 %all-to-all-done.3 = f32[64,1,1164]{2,1,0:T(1,128)S(1)} async-done(((f32[64,1,1164]{2,1,0:T(1,128)}), f32[64,1,1164]{2,1,0:T(1,128)S(1)}, u32[]{:S(2)}, u32[]{:S(2)}) %all-to-all-start.3) | async-done | bytes 298016 | tf_op jit(solution)/shard_map/all_to_all | solution.py:210
  159.7 0.9 multiply_reduce_fusion
  161.4 0.8 broadcast_in_dim_reshape.8
  162.2 0.8 broadcast_in_dim_reshape.9
  (81 shorter events, 8.4 us)
Async XLA Ops:
  0.6 4.2 %copy-start = (bf16[1,2,96,4,512]{4,3,2,1,0:T(4,128)(2,1)S(1)}, bf16[1,2,96,4,512]{4,3,2,1,0:T(4,128)(2,1)}, u32[]{:S(2)}) copy-start(bf16[1,2,96,4,512]{4,3,2,1,0:T(4,128)(2,1)} %param.6) | copy-start | bytes 2359300
  0.7 1.1 copy-start.13
  1.8 1.1 copy-start.1
  3.6 25.0 %collective-permute-start = (f32[2,96,4,256]{3,1,2,0:T(8,128)S(1)}, f32[2,96,4,256]{3,1,2,0:T(8,128)}, u32[]{:S(2)}, u32[]{:S(2)}) collective-permute-start(f32[2,96,4,256]{3,1,2,0:T(8,128)S(1)} %convolution_bitcast_fusion.1), channel_id=1, source_target_pairs={{64,0},{128,64},{192,128},{256,192},{320,256},{384,320},{448,384},... | collective-permute-start | bytes 2359304 | tf_op jit(solution)/shard_map/ppermute | solution.py:20
  8.8 14.1 %copy-start.16 = (s32[1,2]{1,0:T(1,128)S(1)}, s32[1,2]{1,0:T(1,128)}, u32[]{:S(2)}) copy-start(s32[1,2]{1,0:T(1,128)} %param.8) | copy-start | bytes 28
  8.8 40.3 %all-to-all-start = ((f32[2,96,4,256]{1,2,0,3:T(4,128)}), f32[2,96,4,256]{1,2,0,3:T(4,128)S(1)}, u32[]{:S(2)}, u32[]{:S(2)}) async-start(f32[2,96,4,256]{1,2,0,3:T(4,128)} %copy.125), calls=%async_computation | async-start | bytes 2097152 | tf_op jit(solution)/shard_map/all_to_all | solution.py:152
  20.6 2.3 %copy-start.12 = (f32[1,2,2,96,96]{4,3,2,1,0:T(8,128)S(1)}, f32[1,2,2,96,96]{4,3,2,1,0:T(8,128)}, u32[]{:S(2)}) copy-start(f32[1,2,2,96,96]{4,3,2,1,0:T(8,128)} %param.11) | copy-start | bytes 442372
  20.6 6.4 %copy-start.15 = (f32[1,2,2,96]{3,2,1,0:T(2,128)S(1)}, f32[1,2,2,96]{3,2,1,0:T(2,128)}, u32[]{:S(2)}) copy-start(f32[1,2,2,96]{3,2,1,0:T(2,128)} %param.10) | copy-start | bytes 4612
  21.6 78.1 %collective-permute-start.1 = (bf16[2,96,4,512]{3,1,2,0:T(8,128)(2,1)}, bf16[2,96,4,512]{3,1,2,0:T(8,128)(2,1)}, u32[]{:S(2)}, u32[]{:S(2)}) collective-permute-start(bf16[2,96,4,512]{3,1,2,0:T(8,128)(2,1)} %bitcast.131), channel_id=1, source_target_pairs={{64,0},{128,64},{192,128},{256,192},{320,256},{384,320},{448,384},... | collective-permute-start | bytes 2359304 | tf_op jit(solution)/shard_map/ppermute | solution.py:20
  51.4 11.9 %copy-start.3 = (f32[1,128,2,256]{3,1,2,0:T(8,128)S(1)}, f32[1,128,2,256]{3,1,2,0:T(8,128)}, u32[]{:S(2)}) copy-start(f32[1,128,2,256]{3,1,2,0:T(8,128)} %get-tuple-element.52) | copy-start | bytes 786436
  51.4 11.9 %copy-start.5 = (f32[1,128,2,256]{3,1,2,0:T(8,128)S(1)}, f32[1,128,2,256]{3,1,2,0:T(8,128)}, u32[]{:S(2)}) copy-start(f32[1,128,2,256]{3,1,2,0:T(8,128)} %get-tuple-element.53) | copy-start | bytes 786436
  51.4 34.9 %all-to-all-start.1 = ((f32[2,96,4,256]{1,2,0,3:T(4,128)}), f32[2,96,4,256]{1,2,0,3:T(4,128)S(1)}, u32[]{:S(2)}, u32[]{:S(2)}) async-start(f32[2,96,4,256]{1,2,0,3:T(4,128)} %copy.129), calls=%async_computation.1 | async-start | bytes 2097152 | tf_op jit(solution)/shard_map/all_to_all | solution.py:152
  65.0 1.7 %copy-start.7 = (f32[2,96,96]{2,1,0:T(8,128)S(1)}, f32[2,96,96]{2,1,0:T(8,128)}, u32[]{:S(2)}) copy-start(f32[2,96,96]{2,1,0:T(8,128)} %get-tuple-element.50) | copy-start | bytes 221188
  65.0 1.7 %copy-start.8 = (f32[2,96,96]{2,1,0:T(8,128)S(1)}, f32[2,96,96]{2,1,0:T(8,128)}, u32[]{:S(2)}) copy-start(f32[2,96,96]{2,1,0:T(8,128)} %get-tuple-element.51) | copy-start | bytes 221188
  86.5 1.0 copy-start.4
  86.5 1.0 copy-start.6
  94.4 1.0 copy-start.9
  94.4 1.0 copy-start.10
  94.4 1.0 copy-start.11
  102.4 6.3 %copy-start.14 = (s32[64,2]{0,1:T(2,128)S(1)}, s32[64,2]{0,1:T(2,128)}, u32[]{:S(2)}) copy-start(s32[64,2]{0,1:T(2,128)} %copy-done.13) | copy-start | bytes 1540
  102.4 36.3 %all-to-all-start.2 = ((f32[64,1,4236]{2,1,0:T(1,128)}), f32[64,1,4236]{2,1,0:T(1,128)S(1)}, u32[]{:S(2)}, u32[]{:S(2)}) async-start(f32[64,1,4236]{2,1,0:T(1,128)} %copy.151), calls=%async_computation.2 | async-start | bytes 2228224 | tf_op jit(solution)/shard_map/all_to_all | solution.py:206
  140.2 19.5 %all-to-all-start.3 = ((f32[64,1,1164]{2,1,0:T(1,128)}), f32[64,1,1164]{2,1,0:T(1,128)S(1)}, u32[]{:S(2)}, u32[]{:S(2)}) async-start(f32[64,1,1164]{2,1,0:T(1,128)} %broadcast_in_dim.15), calls=%async_computation.3 | async-start | bytes 655360 | tf_op jit(solution)/shard_map/all_to_all | solution.py:210
  146.4 2.0 %copy-start.2 = (bf16[1,2,96,4,512]{4,3,2,1,0:T(4,128)(2,1)S(1)}, bf16[1,2,96,4,512]{4,3,2,1,0:T(4,128)(2,1)}, u32[]{:S(2)}) copy-start(bf16[1,2,96,4,512]{4,3,2,1,0:T(4,128)(2,1)} %param.7) | copy-start | bytes 2359300

commit v12 on v11

--- a/solution.py
+++ b/solution.py
@@ -171,15 +171,16 @@
     nblocks = field.shape[0]
     width = field.shape[1]
     ndev = lax.axis_size("space")
-    received = from_behind(own_grad, "pipe", -1)
     section_index = lax.axis_index("pipe")
     last_section = lax.axis_size("pipe") - 1
     lon_cos, lon_sin = lon_tables(LON, KEEP_LON)
     lat_cos, lat_sin = lat_tables(LAT, KEEP_LAT)
     table = lon_forward_table(lon_cos, lon_sin, ndev)
+    field_lon, own_grad = lax.optimization_barrier((lon_forward(field, table), own_grad))
+    col_field = to_columns(field_lon, ndev)
     own_lon = lon_forward(own_grad, table)
     received_lon = from_behind(own_lon, "pipe", -1)
-    col_field = to_columns(lon_forward(field, table), ndev)
+    received = from_behind(own_grad, "pipe", -1)
     upstream_lon = jnp.where(section_index == last_section, own_lon, received_lon)
     col_field, upstream_lon = lax.optimization_barrier((col_field, upstream_lon))
     spectrum = lat_forward(col_field, lat_cos, lat_sin)

time: 166 us -> 178 us (1.072)
  waiting for transfers between devices: 74.6 us -> 80.5 us
  starting transfers between devices: 33.2 us -> 37.9 us
    ppermute x2, waiting for transfers between devices: 0.01 us -> 25.5 us  [from_behind(): return lax.ppermute(block, axis, route)]
    all_to_all x2, waiting for transfers between devices: 38.4 us -> 19.3 us  [to_columns(): lax.all_to_all(spectrum, 'space', split_axis=3, concat_axis=2, tiled=True)]
    all_to_all x2, starting transfers between devices: 18.1 us -> 22.7 us  [to_columns(): lax.all_to_all(spectrum, 'space', split_axis=3, concat_axis=2, tiled=True)]
    dot_general x1 -> x0, local copies, waits for them, and re-layouts: 2.45 us -> none  [lon_forward(): return jnp.einsum('ibln,nc->iblc', values, table, precision=HIGHEST)]
    unnamed x39 -> x55, local copies, waits for them, and re-layouts: 4.83 us -> 6.39 us
  transfers between devices with their start and end apart: 6 -> 6, of which waited for: 4 -> 4; matrix products, arithmetic and copies ran while one was open for 26% -> 24% of each run, Pallas kernels for 0% -> 0%
where the time goes in v12:
time: 178 us; the launch traced here: 177 us
  waiting for transfers between devices  80.5 us (45%)
  starting transfers between devices  37.9 us (21%)
  local copies, waits for them, and re-layouts  27.8 us (16%)
  other arithmetic  16.8 us (9%)
  matrix products  11.7 us (7%)
  between operations  1.9 us (1%)
    all_to_all x1, waiting for transfers between devices, shards(): lax.all_to_all(joined, 'space', split_axis=0, concat_axis=0, tiled=True)  28 us
    ppermute x2, waiting for transfers between devices, from_behind(): return lax.ppermute(block, axis, route)  25.5 us
    all_to_all x2, starting transfers between devices, to_columns(): lax.all_to_all(spectrum, 'space', split_axis=3, concat_axis=2, tiled=True)  22.7 us
    all_to_all x2, waiting for transfers between devices, to_columns(): lax.all_to_all(spectrum, 'space', split_axis=3, concat_axis=2, tiled=True)  19.3 us
    all_to_all x1, waiting for transfers between devices, shards(): lax.all_to_all(spread, 'space', split_axis=0, concat_axis=0, tiled=True)  7.69 us
    unnamed x55, local copies, waits for them, and re-layouts  6.39 us
    all_to_all x1, starting transfers between devices, shards(): lax.all_to_all(joined, 'space', split_axis=0, concat_axis=0, tiled=True)  6.33 us
    all_to_all x1, starting transfers between devices, shards(): lax.all_to_all(spread, 'space', split_axis=0, concat_axis=0, tiled=True)  6.19 us
  transfers between devices with their start and end apart: 6, of which 4 were waited for; matrix products, arithmetic and copies ran while one was open for 24% of the time, Pallas kernels for 0%

profile of v12, /device:TPU:1, one launch (start us, length us, event | category | flops | bytes accessed | tf_op | source)
XLA Modules:
  0.0 176.7 jit_solution(14434276482743832187)
XLA Ops:
  0.7 1.1 cosine_multiply_fusion.1
  2.9 1.0 copy.203
  4.0 0.6 convolution_bitcast_fusion.1
  4.6 1.3 copy.125
  5.9 11.6 %all-to-all-start = ((f32[2,96,4,256]{1,2,0,3:T(4,128)}), f32[2,96,4,256]{1,2,0,3:T(4,128)S(1)}, u32[]{:S(2)}, u32[]{:S(2)}) async-start(f32[2,96,4,256]{1,2,0,3:T(4,128)} %copy.125), calls=%async_computation | async-start | bytes 2097152 | tf_op jit(solution)/shard_map/all_to_all | solution.py:152
  17.6 1.4 collective-permute-start.1
  19.0 1.7 fusion.17
  20.8 1.3 collective-permute-start
  22.1 0.7 fusion.82
  24.0 1.6 copy.183
  25.6 0.7 copy.182
  26.9 1.2 fusion.65
  28.0 1.2 compare_and_fusion
  29.3 0.6 sine_multiply_fusion.1
  29.9 0.8 maximum_bitcast_fusion.7
  30.7 25.5 %collective-permute-done = f32[2,96,4,256]{3,1,2,0:T(8,128)S(1)} collective-permute-done((f32[2,96,4,256]{3,1,2,0:T(8,128)S(1)}, f32[2,96,4,256]{3,1,2,0:T(8,128)S(1)}, u32[]{:S(2)}, u32[]{:S(2)}) %collective-permute-start) | collective-permute-done | bytes 786464 | tf_op jit(solution)/shard_map/ppermute | solution.py:20
  56.3 1.0 broadcast_select_fusion
  57.5 0.7 copy.127
  58.6 1.3 copy.129
  60.0 11.1 %all-to-all-start.1 = ((f32[2,96,4,256]{1,2,0,3:T(4,128)}), f32[2,96,4,256]{1,2,0,3:T(4,128)S(1)}, u32[]{:S(2)}, u32[]{:S(2)}) async-start(f32[2,96,4,256]{1,2,0,3:T(4,128)} %copy.129), calls=%async_computation.1 | async-start | bytes 2097152 | tf_op jit(solution)/shard_map/all_to_all | solution.py:152
  71.2 1.5 fusion.77
  72.7 0.6 bitcast_negate_fusion
  73.4 1.6 slice_bitcast_fusion
  75.0 1.4 fusion.64
  76.4 1.8 %convolution_bitcast_fusion.2 = f32[2,2,96,128,2]{3,2,1,4,0:T(8,128)} fusion(f32[1,128,2,256]{3,1,2,0:T(8,128)S(1)} %copy-done.4, f32[1,128,2,256]{3,1,2,0:T(8,128)S(1)} %copy-done.2, f32[2,96,256,2,2]{1,2,4,3,0:T(8,128)S(1)} %bitcast.137), kind=kOutput, calls=%fused_computation.7 | convolution fusion | flops 302120960 | bytes 1703936 | tf_op jit(solution)/shard_map/ofpl,iblpj->iobfj/dot_general | solution.py:57
  78.1 1.4 copy.136
  80.3 19.3 %all-to-all-done.1 = f32[2,96,4,256]{1,2,0,3:T(4,128)S(1)} async-done(((f32[2,96,4,256]{1,2,0,3:T(4,128)}), f32[2,96,4,256]{1,2,0,3:T(4,128)S(1)}, u32[]{:S(2)}, u32[]{:S(2)}) %all-to-all-start.1) | async-done | bytes 786464 | tf_op jit(solution)/shard_map/all_to_all | solution.py:152
  99.8 0.7 copy.131
  100.9 1.1 fusion.84
  102.7 0.6 fusion.32
  103.3 1.7 fusion.85
  107.3 0.8 fusion.37
  109.1 0.6 convolution_bitcast_fusion
  109.7 2.1 %copy.141 = f32[64,2,2,96,4,2]{0,5,4,3,2,1:T(2,128)} copy(f32[64,2,2,96,4,2]{3,0,4,1,5,2:T(8,128)S(1)} %convolution_bitcast_fusion) | data formatting | bytes 1572864 | tf_op jit(solution)/shard_map/opfdr,ipbfj->doibrj/transpose | solution.py:77
  111.8 1.6 pad_maximum_fusion
  113.4 2.6 %copy.151 = f32[64,1,4236]{2,1,0:T(1,128)} copy(f32[64,1,4236]{0,2,1:T(8,128)S(1)} %bitcast.129) | data formatting | bytes 2168832 | tf_op jit(solution)/shard_map/all_to_all | solution.py:207
  116.0 6.3 %all-to-all-start.2 = ((f32[64,1,4236]{2,1,0:T(1,128)}), f32[64,1,4236]{2,1,0:T(1,128)S(1)}, u32[]{:S(2)}, u32[]{:S(2)}) async-start(f32[64,1,4236]{2,1,0:T(1,128)} %copy.151), calls=%async_computation.2 | async-start | bytes 2228224 | tf_op jit(solution)/shard_map/all_to_all | solution.py:207
  122.3 2.0 %cosine_multiply_fusion = (f32[1,512,64,2]{1,2,0,3:T(8,128)}, f32[1,512,64,2]{1,2,0,3:T(8,128)}) fusion(s32[64,2]{0,1:T(2,128)S(1)} %copy-done.19), kind=kLoop, calls=%fused_computation.73 | loop fusion | flops 1114112 | bytes 524800 | tf_op jit(solution)/shard_map/mul | solution.py:29
  124.3 28.0 %all-to-all-done.2 = f32[64,1,4236]{2,1,0:T(1,128)S(1)} async-done(((f32[64,1,4236]{2,1,0:T(1,128)}), f32[64,1,4236]{2,1,0:T(1,128)S(1)}, u32[]{:S(2)}, u32[]{:S(2)}) %all-to-all-start.2) | async-done | bytes 1084448 | tf_op jit(solution)/shard_map/all_to_all | solution.py:207
  152.4 0.9 broadcast_in_dim.15
  153.3 6.2 %all-to-all-start.3 = ((f32[64,1,1164]{2,1,0:T(1,128)}), f32[64,1,1164]{2,1,0:T(1,128)S(1)}, u32[]{:S(2)}, u32[]{:S(2)}) async-start(f32[64,1,1164]{2,1,0:T(1,128)} %broadcast_in_dim.15), calls=%async_computation.3 | async-start | bytes 655360 | tf_op jit(solution)/shard_map/all_to_all | solution.py:211
  160.0 2.0 %fusion.1 = f32[2,96,4,512,1,1]{3,1,5,4,2,0:T(8,128)S(1)} fusion(f32[64,2,2,96,4,2]{0,5,4,3,2,1:T(2,128)S(1)} %bitcast.130, f32[1,512,64,2]{1,2,0,3:T(8,128)} %get-tuple-element.64, f32[1,512,64,2]{1,2,0,3:T(8,128)} %get-tuple-element.63), kind=kOutput, calls=%fused_computation.3 | convolution fusion | flops 604110848 | bytes 2883584 | tf_op jit(solution)/shard_map/dpiblj,pndj->ibln/dot_general | solution.py:83
  162.0 1.6 fusion.6
  163.6 1.5 copy.154
  165.1 7.7 %all-to-all-done.3 = f32[64,1,1164]{2,1,0:T(1,128)S(1)} async-done(((f32[64,1,1164]{2,1,0:T(1,128)}), f32[64,1,1164]{2,1,0:T(1,128)S(1)}, u32[]{:S(2)}, u32[]{:S(2)}) %all-to-all-start.3) | async-done | bytes 298016 | tf_op jit(solution)/shard_map/all_to_all | solution.py:211
  172.8 0.9 multiply_reduce_fusion
  174.5 0.8 broadcast_in_dim_reshape.9
  175.9 0.8 broadcast_in_dim_reshape.8
  (97 shorter events, 10.2 us)
Async XLA Ops:
  0.6 3.3 %copy-start = (bf16[1,2,96,4,512]{4,3,2,1,0:T(4,128)(2,1)S(1)}, bf16[1,2,96,4,512]{4,3,2,1,0:T(4,128)(2,1)}, u32[]{:S(2)}) copy-start(bf16[1,2,96,4,512]{4,3,2,1,0:T(4,128)(2,1)} %param.6) | copy-start | bytes 2359300
  0.7 1.1 copy-start.18
  1.8 1.1 copy-start.12
  5.9 51.4 %all-to-all-start = ((f32[2,96,4,256]{1,2,0,3:T(4,128)}), f32[2,96,4,256]{1,2,0,3:T(4,128)S(1)}, u32[]{:S(2)}, u32[]{:S(2)}) async-start(f32[2,96,4,256]{1,2,0,3:T(4,128)} %copy.125), calls=%async_computation | async-start | bytes 2097152 | tf_op jit(solution)/shard_map/all_to_all | solution.py:152
  17.5 4.5 %copy-start.17 = (f32[1,2,2,96,96]{4,3,2,1,0:T(8,128)S(1)}, f32[1,2,2,96,96]{4,3,2,1,0:T(8,128)}, u32[]{:S(2)}) copy-start(f32[1,2,2,96,96]{4,3,2,1,0:T(8,128)} %param.11) | copy-start | bytes 442372
  17.5 5.2 %copy-start.21 = (s32[1,2]{1,0:T(1,128)S(1)}, s32[1,2]{1,0:T(1,128)}, u32[]{:S(2)}) copy-start(s32[1,2]{1,0:T(1,128)} %param.8) | copy-start | bytes 28
  17.6 11.7 %copy-start.20 = (f32[1,2,2,96]{3,2,1,0:T(2,128)S(1)}, f32[1,2,2,96]{3,2,1,0:T(2,128)}, u32[]{:S(2)}) copy-start(f32[1,2,2,96]{3,2,1,0:T(2,128)} %param.10) | copy-start | bytes 4612
  17.6 95.8 %collective-permute-start.1 = (bf16[2,96,4,512]{3,1,2,0:T(8,128)(2,1)}, bf16[2,96,4,512]{3,1,2,0:T(8,128)(2,1)}, u32[]{:S(2)}, u32[]{:S(2)}) collective-permute-start(bf16[2,96,4,512]{3,1,2,0:T(8,128)(2,1)} %bitcast.127), channel_id=1, source_target_pairs={{64,0},{128,64},{192,128},{256,192},{320,256},{384,320},{448,384},... | collective-permute-start | bytes 2359304 | tf_op jit(solution)/shard_map/ppermute | solution.py:20
  20.8 35.5 %collective-permute-start = (f32[2,96,4,256]{3,1,2,0:T(8,128)S(1)}, f32[2,96,4,256]{3,1,2,0:T(8,128)S(1)}, u32[]{:S(2)}, u32[]{:S(2)}) collective-permute-start(f32[2,96,4,256]{3,1,2,0:T(8,128)S(1)} %fusion.17), channel_id=1, source_target_pairs={{64,0},{128,64},{192,128},{256,192},{320,256},{384,320},{448,384},... | collective-permute-start | bytes 2359304 | tf_op jit(solution)/shard_map/ppermute | solution.py:20
  57.5 1.1 copy-start.1
  59.9 11.1 %copy-start.22 = (f32[2]{0:T(128)S(1)}, f32[2]{0:T(128)}, u32[]{:S(2)}) copy-start(f32[2]{0:T(128)} %compare_select_fusion) | copy-start | bytes 28
  59.9 11.1 %copy-start.23 = (pred[2]{0:T(512)(128)(4,1)S(1)}, pred[2]{0:T(512)(128)(4,1)}, u32[]{:S(2)}) copy-start(pred[2]{0:T(512)(128)(4,1)} %fusion.65) | copy-start | bytes 10
  60.0 11.1 %copy-start.24 = (pred[128]{0:T(512)(128)(4,1)S(1)}, pred[128]{0:T(512)(128)(4,1)}, u32[]{:S(2)}) copy-start(pred[128]{0:T(512)(128)(4,1)} %compare_and_fusion) | copy-start | bytes 388
  60.0 12.8 %copy-start.16 = (f32[1,1,2,96,96]{3,4,2,1,0:T(8,128)S(1)}, f32[1,1,2,96,96]{3,4,2,1,0:T(8,128)}, u32[]{:S(2)}) copy-start(f32[1,1,2,96,96]{3,4,2,1,0:T(8,128)} %copy.183) | copy-start | bytes 221188
  60.0 16.4 %copy-start.2 = (f32[1,128,2,256]{3,1,2,0:T(8,128)S(1)}, f32[1,128,2,256]{3,1,2,0:T(8,128)}, u32[]{:S(2)}) copy-start(f32[1,128,2,256]{3,1,2,0:T(8,128)} %get-tuple-element.56) | copy-start | bytes 786436
  60.0 16.4 %copy-start.4 = (f32[1,128,2,256]{3,1,2,0:T(8,128)S(1)}, f32[1,128,2,256]{3,1,2,0:T(8,128)}, u32[]{:S(2)}) copy-start(f32[1,128,2,256]{3,1,2,0:T(8,128)} %get-tuple-element.57) | copy-start | bytes 786436
  60.0 39.6 %all-to-all-start.1 = ((f32[2,96,4,256]{1,2,0,3:T(4,128)}), f32[2,96,4,256]{1,2,0,3:T(4,128)S(1)}, u32[]{:S(2)}, u32[]{:S(2)}) async-start(f32[2,96,4,256]{1,2,0,3:T(4,128)} %copy.129), calls=%async_computation.1 | async-start | bytes 2097152 | tf_op jit(solution)/shard_map/all_to_all | solution.py:152
  78.1 1.7 copy-start.6
  78.1 1.7 copy-start.8
  78.1 1.7 copy-start.10
  99.8 1.0 copy-start.3
  99.8 1.0 copy-start.5
  106.3 0.9 copy-start.7
  106.3 0.9 copy-start.9
  106.3 1.0 copy-start.11
  108.0 0.9 copy-start.13
  108.0 1.0 copy-start.14
  108.1 1.0 copy-start.15
  116.0 6.3 %copy-start.19 = (s32[64,2]{0,1:T(2,128)S(1)}, s32[64,2]{0,1:T(2,128)}, u32[]{:S(2)}) copy-start(s32[64,2]{0,1:T(2,128)} %copy-done.18) | copy-start | bytes 1540
  116.0 36.3 %all-to-all-start.2 = ((f32[64,1,4236]{2,1,0:T(1,128)}), f32[64,1,4236]{2,1,0:T(1,128)S(1)}, u32[]{:S(2)}, u32[]{:S(2)}) async-start(f32[64,1,4236]{2,1,0:T(1,128)} %copy.151), calls=%async_computation.2 | async-start | bytes 2228224 | tf_op jit(solution)/shard_map/all_to_all | solution.py:207
  153.3 19.5 %all-to-all-start.3 = ((f32[64,1,1164]{2,1,0:T(1,128)}), f32[64,1,1164]{2,1,0:T(1,128)S(1)}, u32[]{:S(2)}, u32[]{:S(2)}) async-start(f32[64,1,1164]{2,1,0:T(1,128)} %broadcast_in_dim.15), calls=%async_computation.3 | async-start | bytes 655360 | tf_op jit(solution)/shard_map/all_to_all | solution.py:211

commit v13 on v8

--- a/solution.py
+++ b/solution.py
@@ -1,6 +1,7 @@
 import math
 
 import jax
+import numpy as np
 import jax.numpy as jnp
 from jax import lax
 from jax.sharding import PartitionSpec as P
@@ -36,6 +37,18 @@
     angle = phase.astype(jnp.float32) * (2.0 * math.pi / length)
     factor = 1.0 / math.sqrt(length)
     return (jnp.cos(angle) * factor, jnp.sin(angle) * factor)
+
+
+def lon_forward_constant(length, count, ndev):
+    column = np.arange(length, dtype=np.int64)
+    number = np.arange(count, dtype=np.int64)
+    angle = (column[:, None] * number[None, :] % length).astype(np.float64) * (2.0 * math.pi / length)
+    factor = 1.0 / math.sqrt(length)
+    share = count // ndev
+    cos_g = (np.cos(angle) * factor).reshape(length, ndev, 1, share)
+    sin_g = -(np.sin(angle) * factor).reshape(length, ndev, 1, share)
+    table = np.concatenate([cos_g, sin_g], axis=2).reshape(length, -1)
+    return jnp.asarray(table.astype(np.float32))
 
 
 def lon_forward_table(cos_table, sin_table, ndev):
@@ -176,7 +189,7 @@
     last_section = lax.axis_size("pipe") - 1
     lon_cos, lon_sin = lon_tables(LON, KEEP_LON)
     lat_cos, lat_sin = lat_tables(LAT, KEEP_LAT)
-    table = lon_forward_table(lon_cos, lon_sin, ndev)
+    table = lon_forward_constant(LON, KEEP_LON, ndev)
     col_field = to_columns(lon_forward(field, table), ndev)
     col_field, received = lax.optimization_barrier((col_field, received))
     spectrum = lat_forward(col_field, lat_cos, lat_sin)

time: 162 us -> 161 us (level)
    unnamed x45 -> x43, local copies, waits for them, and re-layouts: 4.53 us -> 5.98 us
where the time goes in v13:
time: 161 us; the launch traced here: 160 us
  waiting for transfers between devices  44.4 us (28%)
  blocking collectives  36.2 us (22%)
  local copies, waits for them, and re-layouts  28.2 us (18%)
  starting transfers between devices  25.8 us (16%)
  matrix products  12.1 us (8%)
  other arithmetic  11.7 us (7%)
  between operations  1.82 us (1%)
    all_to_all x2, waiting for transfers between devices, to_columns(): lax.all_to_all(spectrum, 'space', split_axis=3, concat_axis=2, tiled=True)  39.7 us
    all_to_all x1, blocking collectives, shards(): lax.all_to_all(jnp.concatenate([back, pieces], axis=1), 'space', split_ax...  36.2 us
    all_to_all x2, starting transfers between devices, to_columns(): lax.all_to_all(spectrum, 'space', split_axis=3, concat_axis=2, tiled=True)  18.1 us
    all_to_all x1, starting transfers between devices, shards(): lax.all_to_all(spread, 'space', split_axis=0, concat_axis=0, tiled=True)  6.41 us
    unnamed x43, local copies, waits for them, and re-layouts  5.98 us
    all_to_all x1, waiting for transfers between devices, shards(): lax.all_to_all(spread, 'space', split_axis=0, concat_axis=0, tiled=True)  4.65 us
    dot_general x2, matrix products, lon_forward(): return jnp.einsum('ibln,nc->iblc', values, table, precision=HIGHEST)  3.33 us
  transfers between devices with their start and end apart: 4, of which 3 were waited for; matrix products, arithmetic and copies ran while one was open for 15% of the time, Pallas kernels for 0%

profile of v13, /device:TPU:1, one launch (start us, length us, event | category | flops | bytes accessed | tf_op | source)
XLA Modules:
  0.0 160.2 jit_solution(15293141007568774713)
XLA Ops:
  0.6 1.1 copy-done
  1.8 1.6 %convolution_bitcast_fusion.1 = f32[2,96,4,256]{3,1,2,0:T(8,128)S(1)} fusion(f32[512,256,1,1]{1,0,3,2:T(8,128)} %constant.91, bf16[2,96,4,512]{3,2,1,0:T(4,128)(2,1)S(1)} %bitcast.132), kind=kOutput, calls=%fused_computation.6 | convolution fusion | flops 603979776 | bytes 2097152 | tf_op jit(solution)/shard_map/ibln,nc->iblc/dot_general | solution.py:63
  3.4 1.4 copy.79
  4.8 11.7 %all-to-all-start = ((f32[2,96,4,256]{1,2,0,3:T(4,128)}), f32[2,96,4,256]{1,2,0,3:T(4,128)S(1)}, u32[]{:S(2)}, u32[]{:S(2)}) async-start(f32[2,96,4,256]{1,2,0,3:T(4,128)} %copy.79), calls=%async_computation | async-start | bytes 2097152 | tf_op jit(solution)/shard_map/all_to_all | solution.py:165
  16.6 1.0 copy.162
  17.6 1.3 collective-permute-start
  18.9 0.6 fusion.77
  20.2 0.7 copy.135
  20.9 0.7 copy.134
  21.6 0.7 compare_and_fusion
  22.3 0.7 fusion.59
  23.1 0.6 sine_multiply_fusion.1
  23.7 0.8 maximum_bitcast_fusion.10
  24.5 20.6 %all-to-all-done = f32[2,96,4,256]{1,2,0,3:T(4,128)S(1)} async-done(((f32[2,96,4,256]{1,2,0,3:T(4,128)}), f32[2,96,4,256]{1,2,0,3:T(4,128)S(1)}, u32[]{:S(2)}, u32[]{:S(2)}) %all-to-all-start) | async-done | bytes 786464 | tf_op jit(solution)/shard_map/all_to_all | solution.py:165
  45.3 0.7 copy.81
  46.3 1.7 %fusion.36 = f32[2,96,4,256]{3,1,2,0:T(8,128)S(1)} fusion(f32[512,256,1,1]{1,0,3,2:T(8,128)S(1)} %copy-done.7, bf16[2,96,4,512]{3,1,2,0:T(8,128)(2,1)} %collective-permute-done, pred[]{:T(512)S(6)} %eq.14, bf16[1,2,96,4,512]{4,3,2,1,0:T(4,128)(2,1)S(1)} %copy-done.1), kind=kOutput, calls=%fused_computation.55 | convolution fusion | flops 604372992 | bytes 2883585 | tf_op jit(solution)/shard_map/ibln,nc->iblc/dot_general | solution.py:63
  48.1 1.4 copy.84
  49.4 6.3 %all-to-all-start.1 = ((f32[2,96,4,256]{1,2,0,3:T(4,128)}), f32[2,96,4,256]{1,2,0,3:T(4,128)S(1)}, u32[]{:S(2)}, u32[]{:S(2)}) async-start(f32[2,96,4,256]{1,2,0,3:T(4,128)} %copy.84), calls=%async_computation.1 | async-start | bytes 2097152 | tf_op jit(solution)/shard_map/all_to_all | solution.py:165
  55.8 0.9 fusion.71
  56.7 1.5 bitcast_negate_fusion
  58.3 1.6 %slice_bitcast_fusion = (f32[2,96,96]{2,1,0:T(8,128)}, f32[2,96,96]{2,1,0:T(8,128)}) fusion(f32[1,2,2,96,96]{4,3,2,1,0:T(8,128)} %param.10), kind=kLoop, calls=%fused_computation.99 | loop fusion | bytes 294912 | tf_op jit(solution)/shard_map/squeeze | solution.py:107
  59.9 1.3 fusion.58
  61.2 1.8 %convolution_bitcast_fusion.2 = f32[2,2,96,128,2]{3,2,1,4,0:T(8,128)} fusion(f32[1,128,2,256]{3,1,2,0:T(8,128)S(1)} %copy-done.5, f32[1,128,2,256]{3,1,2,0:T(8,128)S(1)} %copy-done.3, f32[2,96,256,2,2]{1,2,4,3,0:T(8,128)S(1)} %bitcast.140), kind=kOutput, calls=%fused_computation.7 | convolution fusion | flops 302120960 | bytes 1703936 | tf_op jit(solution)/shard_map/ofpl,iblpj->iobfj/dot_general | solution.py:70
  63.0 1.4 copy.91
  65.1 19.2 %all-to-all-done.1 = f32[2,96,4,256]{1,2,0,3:T(4,128)S(1)} async-done(((f32[2,96,4,256]{1,2,0,3:T(4,128)}), f32[2,96,4,256]{1,2,0,3:T(4,128)S(1)}, u32[]{:S(2)}, u32[]{:S(2)}) %all-to-all-start.1) | async-done | bytes 786464 | tf_op jit(solution)/shard_map/all_to_all | solution.py:165
  84.5 0.7 copy.86
  85.6 1.1 fusion.78
  87.3 0.6 fusion.31
  87.9 0.7 fusion.79
  89.0 0.8 fusion.37
  92.5 0.6 convolution_bitcast_fusion
  93.1 2.1 %copy.96 = f32[64,2,2,96,4,2]{0,5,4,3,2,1:T(2,128)} copy(f32[64,2,2,96,4,2]{3,0,4,1,5,2:T(8,128)S(1)} %convolution_bitcast_fusion) | data formatting | bytes 1572864 | tf_op jit(solution)/shard_map/opfdr,ipbfj->doibrj/transpose | solution.py:90
  95.2 1.6 maximum_bitcast_fusion
  96.8 2.7 %copy.106 = f32[64,1,4236]{2,1,0:T(1,128)} copy(f32[64,1,4236]{0,2,1:T(8,128)S(1)} %maximum_bitcast_fusion) | data formatting | bytes 2168832 | tf_op jit(solution)/shard_map/all_to_all | solution.py:216
  99.5 36.2 %all_to_all.48 = f32[64,1,4236]{2,1,0:T(1,128)S(1)} all-to-all(f32[64,1,4236]{2,1,0:T(1,128)} %copy.106), channel_id=1, replica_groups=mesh['pipe'=8,'space'=64] {'space'}, dimensions={0} | all-to-all | bytes 2168832 | tf_op jit(solution)/shard_map/all_to_all | solution.py:216
  135.7 0.9 broadcast_in_dim.15
  136.6 6.4 %all-to-all-start.3 = ((f32[64,1,1164]{2,1,0:T(1,128)}), f32[64,1,1164]{2,1,0:T(1,128)S(1)}, u32[]{:S(2)}, u32[]{:S(2)}) async-start(f32[64,1,1164]{2,1,0:T(1,128)} %broadcast_in_dim.15), calls=%async_computation.3 | async-start | bytes 655360 | tf_op jit(solution)/shard_map/all_to_all | solution.py:222
  143.1 2.0 %cosine_multiply_fusion = (f32[1,512,64,2]{1,2,0,3:T(8,128)}, f32[1,512,64,2]{1,2,0,3:T(8,128)}) fusion(s32[64,2]{0,1:T(2,128)S(1)} %multiply_add_fusion.2), kind=kLoop, calls=%fused_computation.64 | loop fusion | flops 1114112 | bytes 524800 | tf_op jit(solution)/shard_map/mul | solution.py:30
  145.0 0.9 slice.104
  146.0 1.7 %copy.107 = f32[64,3072]{0,1:T(8,128)S(1)} copy(f32[64,3072]{1,0:T(8,128)} %slice.104) | data formatting | bytes 1572864 | tf_op jit(solution)/shard_map/slice | solution.py:219
  147.7 2.5 %fusion.6 = bf16[1,2,96,4,512]{4,2,3,1,0:T(8,128)(2,1)S(1)} fusion(f32[64,2,2,96,4,2]{0,5,4,3,2,1:T(2,128)S(1)} %bitcast.133, f32[1,512,64,2]{1,2,0,3:T(8,128)} %get-tuple-element.51, f32[1,512,64,2]{1,2,0,3:T(8,128)} %get-tuple-element.50, bf16[2,96,4,512]{3,1,2,0:T(8,128)(2,1)} %collective-permute-done, pred[]{:T(512)S(6)} %eq.14, ...), kind=kOutput, calls=%fused_computation.15 | convolution fusion | flops 605683712 | bytes 3670017 | tf_op jit(solution)/shard_map/dpiblj,pndj->ibln/dot_general | solution.py:96
  150.2 1.5 copy.109
  151.7 4.6 %all-to-all-done.3 = f32[64,1,1164]{2,1,0:T(1,128)S(1)} async-done(((f32[64,1,1164]{2,1,0:T(1,128)}), f32[64,1,1164]{2,1,0:T(1,128)S(1)}, u32[]{:S(2)}, u32[]{:S(2)}) %all-to-all-start.3) | async-done | bytes 298016 | tf_op jit(solution)/shard_map/all_to_all | solution.py:222
  156.3 0.9 multiply_reduce_fusion
  157.4 0.6 mul.457
  158.0 0.8 broadcast_in_dim_reshape.8
  158.8 0.8 broadcast_in_dim_reshape.9
  159.6 0.6 fusion.72
  (76 shorter events, 6.0 us)
Async XLA Ops:
  0.6 1.1 copy-start
  3.4 13.1 %copy-start.1 = (bf16[1,2,96,4,512]{4,3,2,1,0:T(4,128)(2,1)S(1)}, bf16[1,2,96,4,512]{4,3,2,1,0:T(4,128)(2,1)}, u32[]{:S(2)}) copy-start(bf16[1,2,96,4,512]{4,3,2,1,0:T(4,128)(2,1)} %param.8) | copy-start | bytes 2359300
  4.8 14.1 %copy-start.18 = (s32[1,2]{1,0:T(1,128)S(1)}, s32[1,2]{1,0:T(1,128)}, u32[]{:S(2)}) copy-start(s32[1,2]{1,0:T(1,128)} %param.9) | copy-start | bytes 28
  4.8 15.3 %copy-start.14 = (f32[1,2,2,96,96]{4,3,2,1,0:T(8,128)S(1)}, f32[1,2,2,96,96]{4,3,2,1,0:T(8,128)}, u32[]{:S(2)}) copy-start(f32[1,2,2,96,96]{4,3,2,1,0:T(8,128)} %param.12) | copy-start | bytes 442372
  4.8 40.3 %all-to-all-start = ((f32[2,96,4,256]{1,2,0,3:T(4,128)}), f32[2,96,4,256]{1,2,0,3:T(4,128)S(1)}, u32[]{:S(2)}, u32[]{:S(2)}) async-start(f32[2,96,4,256]{1,2,0,3:T(4,128)} %copy.79), calls=%async_computation | async-start | bytes 2097152 | tf_op jit(solution)/shard_map/all_to_all | solution.py:165
  16.5 6.4 %copy-start.17 = (f32[1,2,2,96]{3,2,1,0:T(2,128)S(1)}, f32[1,2,2,96]{3,2,1,0:T(2,128)}, u32[]{:S(2)}) copy-start(f32[1,2,2,96]{3,2,1,0:T(2,128)} %param.11) | copy-start | bytes 4612
  17.6 28.4 %collective-permute-start = (bf16[2,96,4,512]{3,1,2,0:T(8,128)(2,1)}, bf16[2,96,4,512]{3,1,2,0:T(8,128)(2,1)}, u32[]{:S(2)}, u32[]{:S(2)}) collective-permute-start(bf16[2,96,4,512]{3,1,2,0:T(8,128)(2,1)} %bitcast.131), channel_id=1, source_target_pairs={{64,0},{128,64},{192,128},{256,192},{320,256},{384,320},{448,384},... | collective-permute-start | bytes 2359304 | tf_op jit(solution)/shard_map/ppermute | solution.py:21
  45.3 1.0 copy-start.7
  49.4 11.8 %copy-start.3 = (f32[1,128,2,256]{3,1,2,0:T(8,128)S(1)}, f32[1,128,2,256]{3,1,2,0:T(8,128)}, u32[]{:S(2)}) copy-start(f32[1,128,2,256]{3,1,2,0:T(8,128)} %get-tuple-element.43) | copy-start | bytes 786436
  49.4 11.8 %copy-start.5 = (f32[1,128,2,256]{3,1,2,0:T(8,128)S(1)}, f32[1,128,2,256]{3,1,2,0:T(8,128)}, u32[]{:S(2)}) copy-start(f32[1,128,2,256]{3,1,2,0:T(8,128)} %get-tuple-element.44) | copy-start | bytes 786436
  49.4 34.9 %all-to-all-start.1 = ((f32[2,96,4,256]{1,2,0,3:T(4,128)}), f32[2,96,4,256]{1,2,0,3:T(4,128)S(1)}, u32[]{:S(2)}, u32[]{:S(2)}) async-start(f32[2,96,4,256]{1,2,0,3:T(4,128)} %copy.84), calls=%async_computation.1 | async-start | bytes 2097152 | tf_op jit(solution)/shard_map/all_to_all | solution.py:165
  63.0 1.7 %copy-start.8 = (f32[2,96,96]{2,1,0:T(8,128)S(1)}, f32[2,96,96]{2,1,0:T(8,128)}, u32[]{:S(2)}) copy-start(f32[2,96,96]{2,1,0:T(8,128)} %get-tuple-element.41) | copy-start | bytes 221188
  63.0 1.7 %copy-start.9 = (f32[2,96,96]{2,1,0:T(8,128)S(1)}, f32[2,96,96]{2,1,0:T(8,128)}, u32[]{:S(2)}) copy-start(f32[2,96,96]{2,1,0:T(8,128)} %get-tuple-element.42) | copy-start | bytes 221188
  84.5 1.0 copy-start.4
  84.5 1.0 copy-start.6
  86.6 1.3 copy-start.13
  86.7 1.3 copy-start.15
  86.7 1.3 copy-start.16
  91.5 1.0 copy-start.10
  91.5 1.0 copy-start.11
  91.5 1.0 copy-start.12
  136.6 19.7 %all-to-all-start.3 = ((f32[64,1,1164]{2,1,0:T(1,128)}), f32[64,1,1164]{2,1,0:T(1,128)S(1)}, u32[]{:S(2)}, u32[]{:S(2)}) async-start(f32[64,1,1164]{2,1,0:T(1,128)} %broadcast_in_dim.15), calls=%async_computation.3 | async-start | bytes 655360 | tf_op jit(solution)/shard_map/all_to_all | solution.py:222
  146.0 1.7 %copy-start.2 = (bf16[1,2,96,4,512]{4,3,2,1,0:T(4,128)(2,1)S(1)}, bf16[1,2,96,4,512]{4,3,2,1,0:T(4,128)(2,1)}, u32[]{:S(2)}) copy-start(bf16[1,2,96,4,512]{4,3,2,1,0:T(4,128)(2,1)} %param.8) | copy-start | bytes 2359300

commit v14 on v13

--- a/solution.py
+++ b/solution.py
@@ -191,10 +191,10 @@
     lat_cos, lat_sin = lat_tables(LAT, KEEP_LAT)
     table = lon_forward_constant(LON, KEEP_LON, ndev)
     col_field = to_columns(lon_forward(field, table), ndev)
-    col_field, received = lax.optimization_barrier((col_field, received))
+    upstream = jnp.where(section_index == last_section, own_grad, received)
+    col_field, lon_grad = lax.optimization_barrier((col_field, lon_forward(upstream, table)))
     spectrum = lat_forward(col_field, lat_cos, lat_sin)
-    upstream = jnp.where(section_index == last_section, own_grad, received)
-    col_grad = to_columns(lon_forward(upstream, table), ndev)
+    col_grad = to_columns(lon_grad, ndev)
     grad_spec = lat_forward(col_grad, lat_cos, lat_sin)
     share = KEEP_LON // ndev
     signed = jnp.arange(2 * KEEP_LAT, dtype=jnp.int32) - KEEP_LAT

time: 161 us -> 161 us (level)
  local copies, waits for them, and re-layouts: 28.2 us -> 30.8 us
  waiting for transfers between devices: 44.4 us -> 42.7 us
    all_to_all x2, waiting for transfers between devices: 39.7 us -> 38 us  [to_columns(): lax.all_to_all(spectrum, 'space', split_axis=3, concat_axis=2, tiled=True)]
    unnamed x43 -> x47, local copies, waits for them, and re-layouts: 5.98 us -> 7.09 us
  transfers between devices with their start and end apart: 4 -> 4, of which waited for: 3 -> 3; matrix products, arithmetic and copies ran while one was open for 15% -> 18% of each run, Pallas kernels for 0% -> 0%
where the time goes in v14:
time: 161 us; the launch traced here: 160 us
  waiting for transfers between devices  42.7 us (27%)
  blocking collectives  36.2 us (22%)
  local copies, waits for them, and re-layouts  30.8 us (19%)
  starting transfers between devices  25.8 us (16%)
  other arithmetic  11.8 us (7%)
  matrix products  10.8 us (7%)
  between operations  1.83 us (1%)
    all_to_all x2, waiting for transfers between devices, to_columns(): lax.all_to_all(spectrum, 'space', split_axis=3, concat_axis=2, tiled=True)  38 us
    all_to_all x1, blocking collectives, shards(): lax.all_to_all(jnp.concatenate([back, pieces], axis=1), 'space', split_ax...  36.2 us
    all_to_all x2, starting transfers between devices, to_columns(): lax.all_to_all(spectrum, 'space', split_axis=3, concat_axis=2, tiled=True)  18.1 us
    unnamed x47, local copies, waits for them, and re-layouts  7.09 us
    all_to_all x1, starting transfers between devices, shards(): lax.all_to_all(spread, 'space', split_axis=0, concat_axis=0, tiled=True)  6.41 us
    all_to_all x1, waiting for transfers between devices, shards(): lax.all_to_all(spread, 'space', split_axis=0, concat_axis=0, tiled=True)  4.62 us
  transfers between devices with their start and end apart: 4, of which 3 were waited for; matrix products, arithmetic and copies ran while one was open for 18% of the time, Pallas kernels for 0%

profile of v14, /device:TPU:1, one launch (start us, length us, event | category | flops | bytes accessed | tf_op | source)
XLA Modules:
  0.0 159.9 jit_solution(14810619311846240968)
XLA Ops:
  0.7 2.3 %copy.162 = bf16[1,2,96,4,512]{4,2,3,1,0:T(8,128)(2,1)} copy(bf16[1,2,96,4,512]{4,3,2,1,0:T(4,128)(2,1)} %param.8) | data formatting | bytes 1572864 | tf_op args[1]
  2.9 1.3 collective-permute-start
  4.2 0.6 convolution_bitcast_fusion.1
  4.8 1.3 copy.81
  6.2 11.7 %all-to-all-start = ((f32[2,96,4,256]{1,2,0,3:T(4,128)}), f32[2,96,4,256]{1,2,0,3:T(4,128)S(1)}, u32[]{:S(2)}, u32[]{:S(2)}) async-start(f32[2,96,4,256]{1,2,0,3:T(4,128)} %copy.81), calls=%async_computation | async-start | bytes 2097152 | tf_op jit(solution)/shard_map/all_to_all | solution.py:165
  17.9 0.6 fusion.77
  19.2 1.6 fusion.76
  20.8 1.6 %copy.135 = f32[1,1,2,96,96]{3,4,2,1,0:T(8,128)} copy(f32[1,1,2,96,96]{4,3,2,1,0:T(8,128)} %get-tuple-element.39) | data formatting | bytes 147456
  22.4 0.7 copy.134
  23.1 0.7 compare_and_fusion
  23.9 0.7 fusion.59
  24.6 0.6 sine_multiply_fusion.1
  25.3 0.9 maximum_bitcast_fusion.10
  26.1 1.5 fusion.36
  27.6 18.9 %all-to-all-done = f32[2,96,4,256]{1,2,0,3:T(4,128)S(1)} async-done(((f32[2,96,4,256]{1,2,0,3:T(4,128)}), f32[2,96,4,256]{1,2,0,3:T(4,128)S(1)}, u32[]{:S(2)}, u32[]{:S(2)}) %all-to-all-start) | async-done | bytes 786464 | tf_op jit(solution)/shard_map/all_to_all | solution.py:165
  46.7 0.7 copy.83
  47.8 1.3 copy.84
  49.2 6.3 %all-to-all-start.1 = ((f32[2,96,4,256]{1,2,0,3:T(4,128)}), f32[2,96,4,256]{1,2,0,3:T(4,128)S(1)}, u32[]{:S(2)}, u32[]{:S(2)}) async-start(f32[2,96,4,256]{1,2,0,3:T(4,128)} %copy.84), calls=%async_computation.1 | async-start | bytes 2097152 | tf_op jit(solution)/shard_map/all_to_all | solution.py:165
  55.6 0.9 fusion.71
  56.5 1.5 bitcast_negate_fusion
  58.0 1.6 %slice_bitcast_fusion = (f32[2,96,96]{2,1,0:T(8,128)}, f32[2,96,96]{2,1,0:T(8,128)}) fusion(f32[1,2,2,96,96]{4,3,2,1,0:T(8,128)} %param.10), kind=kLoop, calls=%fused_computation.99 | loop fusion | bytes 294912 | tf_op jit(solution)/shard_map/squeeze | solution.py:107
  59.7 1.3 fusion.58
  61.0 1.8 %convolution_bitcast_fusion.2 = f32[2,2,96,128,2]{3,2,1,4,0:T(8,128)} fusion(f32[1,128,2,256]{3,1,2,0:T(8,128)S(1)} %copy-done.7, f32[1,128,2,256]{3,1,2,0:T(8,128)S(1)} %copy-done.5, f32[2,96,256,2,2]{1,2,4,3,0:T(8,128)S(1)} %bitcast.140), kind=kOutput, calls=%fused_computation.7 | convolution fusion | flops 302120960 | bytes 1703936 | tf_op jit(solution)/shard_map/ofpl,iblpj->iobfj/dot_general | solution.py:70
  62.8 1.4 copy.91
  64.9 19.2 %all-to-all-done.1 = f32[2,96,4,256]{1,2,0,3:T(4,128)S(1)} async-done(((f32[2,96,4,256]{1,2,0,3:T(4,128)}), f32[2,96,4,256]{1,2,0,3:T(4,128)S(1)}, u32[]{:S(2)}, u32[]{:S(2)}) %all-to-all-start.1) | async-done | bytes 786464 | tf_op jit(solution)/shard_map/all_to_all | solution.py:165
  84.3 0.7 copy.86
  85.3 1.1 fusion.78
  87.1 0.6 fusion.31
  87.7 0.7 fusion.79
  88.8 0.8 fusion.37
  92.2 0.6 convolution_bitcast_fusion
  92.8 2.1 %copy.96 = f32[64,2,2,96,4,2]{0,5,4,3,2,1:T(2,128)} copy(f32[64,2,2,96,4,2]{3,0,4,1,5,2:T(8,128)S(1)} %convolution_bitcast_fusion) | data formatting | bytes 1572864 | tf_op jit(solution)/shard_map/opfdr,ipbfj->doibrj/transpose | solution.py:90
  95.0 1.6 maximum_bitcast_fusion
  96.5 2.7 %copy.106 = f32[64,1,4236]{2,1,0:T(1,128)} copy(f32[64,1,4236]{0,2,1:T(8,128)S(1)} %maximum_bitcast_fusion) | data formatting | bytes 2168832 | tf_op jit(solution)/shard_map/all_to_all | solution.py:216
  99.2 36.2 %all_to_all.48 = f32[64,1,4236]{2,1,0:T(1,128)S(1)} all-to-all(f32[64,1,4236]{2,1,0:T(1,128)} %copy.106), channel_id=1, replica_groups=mesh['pipe'=8,'space'=64] {'space'}, dimensions={0} | all-to-all | bytes 2168832 | tf_op jit(solution)/shard_map/all_to_all | solution.py:216
  135.5 0.9 broadcast_in_dim.15
  136.4 6.4 %all-to-all-start.3 = ((f32[64,1,1164]{2,1,0:T(1,128)}), f32[64,1,1164]{2,1,0:T(1,128)S(1)}, u32[]{:S(2)}, u32[]{:S(2)}) async-start(f32[64,1,1164]{2,1,0:T(1,128)} %broadcast_in_dim.15), calls=%async_computation.3 | async-start | bytes 655360 | tf_op jit(solution)/shard_map/all_to_all | solution.py:222
  142.8 2.0 %cosine_multiply_fusion = (f32[1,512,64,2]{1,2,0,3:T(8,128)}, f32[1,512,64,2]{1,2,0,3:T(8,128)}) fusion(s32[64,2]{0,1:T(2,128)S(1)} %multiply_add_fusion.2), kind=kLoop, calls=%fused_computation.64 | loop fusion | flops 1114112 | bytes 524800 | tf_op jit(solution)/shard_map/mul | solution.py:30
  144.8 0.9 slice.104
  145.7 1.7 %copy.107 = f32[64,3072]{0,1:T(8,128)S(1)} copy(f32[64,3072]{1,0:T(8,128)} %slice.104) | data formatting | bytes 1572864 | tf_op jit(solution)/shard_map/slice | solution.py:219
  147.4 2.5 %fusion.6 = bf16[1,2,96,4,512]{4,2,3,1,0:T(8,128)(2,1)S(1)} fusion(f32[64,2,2,96,4,2]{0,5,4,3,2,1:T(2,128)S(1)} %bitcast.133, f32[1,512,64,2]{1,2,0,3:T(8,128)} %get-tuple-element.51, f32[1,512,64,2]{1,2,0,3:T(8,128)} %get-tuple-element.50, bf16[2,96,4,512]{3,1,2,0:T(8,128)(2,1)} %copy-done.3, pred[]{:T(512)S(6)} %eq.14, ...), kind=kOutput, calls=%fused_computation.15 | convolution fusion | flops 605683712 | bytes 3670017 | tf_op jit(solution)/shard_map/dpiblj,pndj->ibln/dot_general | solution.py:96
  149.9 1.5 copy.109
  151.4 4.6 %all-to-all-done.3 = f32[64,1,1164]{2,1,0:T(1,128)S(1)} async-done(((f32[64,1,1164]{2,1,0:T(1,128)}), f32[64,1,1164]{2,1,0:T(1,128)S(1)}, u32[]{:S(2)}, u32[]{:S(2)}) %all-to-all-start.3) | async-done | bytes 298016 | tf_op jit(solution)/shard_map/all_to_all | solution.py:222
  156.0 0.9 multiply_reduce_fusion
  157.2 0.6 mul.457
  157.8 0.8 broadcast_in_dim_reshape.8
  158.5 0.8 broadcast_in_dim_reshape.9
  159.3 0.6 fusion.72
  (80 shorter events, 6.1 us)
Async XLA Ops:
  0.6 3.6 %copy-start = (bf16[1,2,96,4,512]{4,3,2,1,0:T(4,128)(2,1)S(1)}, bf16[1,2,96,4,512]{4,3,2,1,0:T(4,128)(2,1)}, u32[]{:S(2)}) copy-start(bf16[1,2,96,4,512]{4,3,2,1,0:T(4,128)(2,1)} %param.7) | copy-start | bytes 2359300
  0.6 3.6 %copy-start.9 = (f32[512,256,1,1]{1,0,3,2:T(8,128)S(1)}, f32[512,256,1,1]{1,0,3,2:T(8,128)}, u32[]{:S(2)}) copy-start(f32[512,256,1,1]{1,0,3,2:T(8,128)} %constant.91) | copy-start | bytes 1572868
  2.9 23.2 %collective-permute-start = (bf16[2,96,4,512]{3,1,2,0:T(8,128)(2,1)}, bf16[2,96,4,512]{3,1,2,0:T(8,128)(2,1)S(1)}, u32[]{:S(2)}, u32[]{:S(2)}) collective-permute-start(bf16[2,96,4,512]{3,1,2,0:T(8,128)(2,1)} %bitcast.131), channel_id=1, source_target_pairs={{64,0},{128,64},{192,128},{256,192},{320,256},{384,320},{448,384},... | collective-permute-start | bytes 2359304 | tf_op jit(solution)/shard_map/ppermute | solution.py:21
  4.8 13.1 %copy-start.20 = (s32[1,2]{1,0:T(1,128)S(1)}, s32[1,2]{1,0:T(1,128)}, u32[]{:S(2)}) copy-start(s32[1,2]{1,0:T(1,128)} %param.9) | copy-start | bytes 28
  6.2 18.4 %copy-start.19 = (f32[1,2,2,96]{3,2,1,0:T(2,128)S(1)}, f32[1,2,2,96]{3,2,1,0:T(2,128)}, u32[]{:S(2)}) copy-start(f32[1,2,2,96]{3,2,1,0:T(2,128)} %param.11) | copy-start | bytes 4612
  6.2 40.3 %all-to-all-start = ((f32[2,96,4,256]{1,2,0,3:T(4,128)}), f32[2,96,4,256]{1,2,0,3:T(4,128)S(1)}, u32[]{:S(2)}, u32[]{:S(2)}) async-start(f32[2,96,4,256]{1,2,0,3:T(4,128)} %copy.81), calls=%async_computation | async-start | bytes 2097152 | tf_op jit(solution)/shard_map/all_to_all | solution.py:165
  17.9 8.2 %copy-start.1 = (bf16[1,2,96,4,512]{4,3,2,1,0:T(4,128)(2,1)S(1)}, bf16[1,2,96,4,512]{4,3,2,1,0:T(4,128)(2,1)}, u32[]{:S(2)}) copy-start(bf16[1,2,96,4,512]{4,3,2,1,0:T(4,128)(2,1)} %param.8) | copy-start | bytes 2359300
  23.1 3.0 %copy-start.10 = (f32[512,256,1,1]{1,0,3,2:T(8,128)S(1)}, f32[512,256,1,1]{1,0,3,2:T(8,128)}, u32[]{:S(2)}) copy-start(f32[512,256,1,1]{1,0,3,2:T(8,128)} %constant.91) | copy-start | bytes 1572868
  26.1 20.6 %copy-start.3 = (bf16[2,96,4,512]{3,1,2,0:T(8,128)(2,1)}, bf16[2,96,4,512]{3,1,2,0:T(8,128)(2,1)S(1)}, u32[]{:S(2)}) copy-start(bf16[2,96,4,512]{3,1,2,0:T(8,128)(2,1)S(1)} %collective-permute-done) | copy-start | bytes 2359300
  46.7 1.1 copy-start.4
  49.2 11.8 %copy-start.5 = (f32[1,128,2,256]{3,1,2,0:T(8,128)S(1)}, f32[1,128,2,256]{3,1,2,0:T(8,128)}, u32[]{:S(2)}) copy-start(f32[1,128,2,256]{3,1,2,0:T(8,128)} %get-tuple-element.43) | copy-start | bytes 786436
  49.2 11.8 %copy-start.7 = (f32[1,128,2,256]{3,1,2,0:T(8,128)S(1)}, f32[1,128,2,256]{3,1,2,0:T(8,128)}, u32[]{:S(2)}) copy-start(f32[1,128,2,256]{3,1,2,0:T(8,128)} %get-tuple-element.44) | copy-start | bytes 786436
  49.2 34.9 %all-to-all-start.1 = ((f32[2,96,4,256]{1,2,0,3:T(4,128)}), f32[2,96,4,256]{1,2,0,3:T(4,128)S(1)}, u32[]{:S(2)}, u32[]{:S(2)}) async-start(f32[2,96,4,256]{1,2,0,3:T(4,128)} %copy.84), calls=%async_computation.1 | async-start | bytes 2097152 | tf_op jit(solution)/shard_map/all_to_all | solution.py:165
  62.8 1.7 %copy-start.11 = (f32[2,96,96]{2,1,0:T(8,128)S(1)}, f32[2,96,96]{2,1,0:T(8,128)}, u32[]{:S(2)}) copy-start(f32[2,96,96]{2,1,0:T(8,128)} %get-tuple-element.41) | copy-start | bytes 221188
  62.8 1.7 %copy-start.12 = (f32[2,96,96]{2,1,0:T(8,128)S(1)}, f32[2,96,96]{2,1,0:T(8,128)}, u32[]{:S(2)}) copy-start(f32[2,96,96]{2,1,0:T(8,128)} %get-tuple-element.42) | copy-start | bytes 221188
  84.3 1.0 copy-start.6
  84.3 1.0 copy-start.8
  86.4 1.3 copy-start.16
  86.4 1.3 copy-start.17
  86.4 1.3 copy-start.18
  91.2 1.0 copy-start.13
  91.2 1.0 copy-start.14
  91.2 1.0 copy-start.15
  136.4 19.7 %all-to-all-start.3 = ((f32[64,1,1164]{2,1,0:T(1,128)}), f32[64,1,1164]{2,1,0:T(1,128)S(1)}, u32[]{:S(2)}, u32[]{:S(2)}) async-start(f32[64,1,1164]{2,1,0:T(1,128)} %broadcast_in_dim.15), calls=%async_computation.3 | async-start | bytes 655360 | tf_op jit(solution)/shard_map/all_to_all | solution.py:222
  145.7 1.7 %copy-start.2 = (bf16[1,2,96,4,512]{4,3,2,1,0:T(4,128)(2,1)S(1)}, bf16[1,2,96,4,512]{4,3,2,1,0:T(4,128)(2,1)}, u32[]{:S(2)}) copy-start(bf16[1,2,96,4,512]{4,3,2,1,0:T(4,128)(2,1)} %param.8) | copy-start | bytes 2359300

commit v15 on v14

--- a/solution.py
+++ b/solution.py
@@ -184,13 +184,14 @@
     nblocks = field.shape[0]
     width = field.shape[1]
     ndev = lax.axis_size("space")
-    received = from_behind(own_grad, "pipe", -1)
     section_index = lax.axis_index("pipe")
     last_section = lax.axis_size("pipe") - 1
     lon_cos, lon_sin = lon_tables(LON, KEEP_LON)
     lat_cos, lat_sin = lat_tables(LAT, KEEP_LAT)
     table = lon_forward_constant(LON, KEEP_LON, ndev)
-    col_field = to_columns(lon_forward(field, table), ndev)
+    field_lon, own_grad = lax.optimization_barrier((lon_forward(field, table), own_grad))
+    received = from_behind(own_grad, "pipe", -1)
+    col_field = to_columns(field_lon, ndev)
     upstream = jnp.where(section_index == last_section, own_grad, received)
     col_field, lon_grad = lax.optimization_barrier((col_field, lon_forward(upstream, table)))
     spectrum = lat_forward(col_field, lat_cos, lat_sin)

time: 161 us -> 160 us (level)
  no operation moved by 1% of the time
where the time goes in v15:
time: 160 us; the launch traced here: 159 us
  waiting for transfers between devices  42.8 us (27%)
  blocking collectives  36.1 us (23%)
  local copies, waits for them, and re-layouts  30 us (19%)
  starting transfers between devices  25.8 us (16%)
  other arithmetic  11.8 us (7%)
  matrix products  10.7 us (7%)
  between operations  1.83 us (1%)
    all_to_all x2, waiting for transfers between devices, to_columns(): lax.all_to_all(spectrum, 'space', split_axis=3, concat_axis=2, tiled=True)  38.1 us
    all_to_all x1, blocking collectives, shards(): lax.all_to_all(jnp.concatenate([back, pieces], axis=1), 'space', split_ax...  36.1 us
    all_to_all x2, starting transfers between devices, to_columns(): lax.all_to_all(spectrum, 'space', split_axis=3, concat_axis=2, tiled=True)  18.1 us
    all_to_all x1, starting transfers between devices, shards(): lax.all_to_all(spread, 'space', split_axis=0, concat_axis=0, tiled=True)  6.41 us
    unnamed x47, local copies, waits for them, and re-layouts  6.3 us
    all_to_all x1, waiting for transfers between devices, shards(): lax.all_to_all(spread, 'space', split_axis=0, concat_axis=0, tiled=True)  4.73 us
  transfers between devices with their start and end apart: 4, of which 3 were waited for; matrix products, arithmetic and copies ran while one was open for 18% of the time, Pallas kernels for 0%

profile of v15, /device:TPU:1, one launch (start us, length us, event | category | flops | bytes accessed | tf_op | source)
XLA Modules:
  0.0 159.1 jit_solution(8380241282502908147)
XLA Ops:
  0.7 1.4 copy.157
  2.2 0.6 convolution_bitcast_fusion.1
  2.8 1.3 collective-permute-start
  4.0 1.3 copy.81
  5.4 11.7 %all-to-all-start = ((f32[2,96,4,256]{1,2,0,3:T(4,128)}), f32[2,96,4,256]{1,2,0,3:T(4,128)S(1)}, u32[]{:S(2)}, u32[]{:S(2)}) async-start(f32[2,96,4,256]{1,2,0,3:T(4,128)} %copy.81), calls=%async_computation | async-start | bytes 2097152 | tf_op jit(solution)/shard_map/all_to_all | solution.py:165
  17.2 0.6 fusion.77
  18.4 1.6 %fusion.76 = (f32[1,1,2,96,96]{4,3,2,1,0:T(8,128)}, f32[1,1,2,96,96]{4,3,2,1,0:T(8,128)S(1)}) fusion(f32[1,2,2,96,96]{4,3,2,1,0:T(8,128)} %param.12), kind=kLoop, calls=%fused_computation.131 | loop fusion | bytes 294912 | tf_op jit(solution)/shard_map/slice | solution.py:107
  20.0 1.6 %copy.135 = f32[1,1,2,96,96]{3,4,2,1,0:T(8,128)} copy(f32[1,1,2,96,96]{4,3,2,1,0:T(8,128)} %get-tuple-element.43) | data formatting | bytes 147456
  21.6 0.7 copy.134
  22.4 0.7 compare_and_fusion
  23.1 0.7 fusion.59
  23.9 0.6 sine_multiply_fusion.1
  24.5 0.9 maximum_bitcast_fusion.10
  25.4 1.5 fusion.36
  26.8 18.9 %all-to-all-done = f32[2,96,4,256]{1,2,0,3:T(4,128)S(1)} async-done(((f32[2,96,4,256]{1,2,0,3:T(4,128)}), f32[2,96,4,256]{1,2,0,3:T(4,128)S(1)}, u32[]{:S(2)}, u32[]{:S(2)}) %all-to-all-start) | async-done | bytes 786464 | tf_op jit(solution)/shard_map/all_to_all | solution.py:165
  45.9 0.7 copy.83
  47.1 1.3 copy.84
  48.4 6.3 %all-to-all-start.1 = ((f32[2,96,4,256]{1,2,0,3:T(4,128)}), f32[2,96,4,256]{1,2,0,3:T(4,128)S(1)}, u32[]{:S(2)}, u32[]{:S(2)}) async-start(f32[2,96,4,256]{1,2,0,3:T(4,128)} %copy.84), calls=%async_computation.1 | async-start | bytes 2097152 | tf_op jit(solution)/shard_map/all_to_all | solution.py:165
  54.8 0.9 fusion.71
  55.7 1.5 bitcast_negate_fusion
  57.2 1.6 %slice_bitcast_fusion = (f32[2,96,96]{2,1,0:T(8,128)}, f32[2,96,96]{2,1,0:T(8,128)}) fusion(f32[1,2,2,96,96]{4,3,2,1,0:T(8,128)} %param.10), kind=kLoop, calls=%fused_computation.99 | loop fusion | bytes 294912 | tf_op jit(solution)/shard_map/squeeze | solution.py:107
  58.9 1.3 fusion.58
  60.2 1.8 %convolution_bitcast_fusion.2 = f32[2,2,96,128,2]{3,2,1,4,0:T(8,128)} fusion(f32[1,128,2,256]{3,1,2,0:T(8,128)S(1)} %copy-done.7, f32[1,128,2,256]{3,1,2,0:T(8,128)S(1)} %copy-done.5, f32[2,96,256,2,2]{1,2,4,3,0:T(8,128)S(1)} %bitcast.138), kind=kOutput, calls=%fused_computation.7 | convolution fusion | flops 302120960 | bytes 1703936 | tf_op jit(solution)/shard_map/ofpl,iblpj->iobfj/dot_general | solution.py:70
  62.0 1.4 copy.91
  64.1 19.2 %all-to-all-done.1 = f32[2,96,4,256]{1,2,0,3:T(4,128)S(1)} async-done(((f32[2,96,4,256]{1,2,0,3:T(4,128)}), f32[2,96,4,256]{1,2,0,3:T(4,128)S(1)}, u32[]{:S(2)}, u32[]{:S(2)}) %all-to-all-start.1) | async-done | bytes 786464 | tf_op jit(solution)/shard_map/all_to_all | solution.py:165
  83.5 0.7 copy.86
  84.5 1.1 fusion.78
  86.3 0.6 fusion.31
  86.9 0.7 fusion.79
  88.0 0.8 fusion.37
  91.5 0.6 convolution_bitcast_fusion
  92.1 2.1 %copy.96 = f32[64,2,2,96,4,2]{0,5,4,3,2,1:T(2,128)} copy(f32[64,2,2,96,4,2]{3,0,4,1,5,2:T(8,128)S(1)} %convolution_bitcast_fusion) | data formatting | bytes 1572864 | tf_op jit(solution)/shard_map/opfdr,ipbfj->doibrj/transpose | solution.py:90
  94.2 1.6 maximum_bitcast_fusion
  95.8 2.7 %copy.106 = f32[64,1,4236]{2,1,0:T(1,128)} copy(f32[64,1,4236]{0,2,1:T(8,128)S(1)} %maximum_bitcast_fusion) | data formatting | bytes 2168832 | tf_op jit(solution)/shard_map/all_to_all | solution.py:217
  98.4 36.1 %all_to_all.48 = f32[64,1,4236]{2,1,0:T(1,128)S(1)} all-to-all(f32[64,1,4236]{2,1,0:T(1,128)} %copy.106), channel_id=1, replica_groups=mesh['pipe'=8,'space'=64] {'space'}, dimensions={0} | all-to-all | bytes 2168832 | tf_op jit(solution)/shard_map/all_to_all | solution.py:217
  134.7 0.9 broadcast_in_dim.15
  135.6 6.4 %all-to-all-start.3 = ((f32[64,1,1164]{2,1,0:T(1,128)}), f32[64,1,1164]{2,1,0:T(1,128)S(1)}, u32[]{:S(2)}, u32[]{:S(2)}) async-start(f32[64,1,1164]{2,1,0:T(1,128)} %broadcast_in_dim.15), calls=%async_computation.3 | async-start | bytes 655360 | tf_op jit(solution)/shard_map/all_to_all | solution.py:223
  142.0 2.0 %cosine_multiply_fusion = (f32[1,512,64,2]{1,2,0,3:T(8,128)}, f32[1,512,64,2]{1,2,0,3:T(8,128)}) fusion(s32[64,2]{0,1:T(2,128)S(1)} %multiply_add_fusion.2), kind=kLoop, calls=%fused_computation.64 | loop fusion | flops 1114112 | bytes 524800 | tf_op jit(solution)/shard_map/mul | solution.py:30
  144.0 0.9 slice.104
  144.9 1.7 %copy.107 = f32[64,3072]{0,1:T(8,128)S(1)} copy(f32[64,3072]{1,0:T(8,128)} %slice.104) | data formatting | bytes 1572864 | tf_op jit(solution)/shard_map/slice | solution.py:220
  146.6 2.4 %fusion.6 = bf16[1,2,96,4,512]{4,2,3,1,0:T(8,128)(2,1)S(1)} fusion(f32[64,2,2,96,4,2]{0,5,4,3,2,1:T(2,128)S(1)} %bitcast.131, f32[1,512,64,2]{1,2,0,3:T(8,128)} %get-tuple-element.55, f32[1,512,64,2]{1,2,0,3:T(8,128)} %get-tuple-element.54, bf16[2,96,4,512]{3,1,2,0:T(8,128)(2,1)S(1)} %bitcast.130, bf16[2,96,4,512]{3,1,2,0:T(8,128)(2,1)} %copy-done.3, ...), kind=kOutput, calls=%fused_computation.15 | convolution fusion | flops 605683712 | bytes 3670017 | tf_op jit(solution)/shard_map/dpiblj,pndj->ibln/dot_general | solution.py:96
  149.0 1.5 copy.109
  150.5 4.7 %all-to-all-done.3 = f32[64,1,1164]{2,1,0:T(1,128)S(1)} async-done(((f32[64,1,1164]{2,1,0:T(1,128)}), f32[64,1,1164]{2,1,0:T(1,128)S(1)}, u32[]{:S(2)}, u32[]{:S(2)}) %all-to-all-start.3) | async-done | bytes 298016 | tf_op jit(solution)/shard_map/all_to_all | solution.py:223
  155.3 0.9 multiply_reduce_fusion
  156.4 0.6 mul.457
  157.0 0.8 broadcast_in_dim_reshape.8
  157.8 0.8 broadcast_in_dim_reshape.9
  158.5 0.6 fusion.72
  (80 shorter events, 6.2 us)
Async XLA Ops:
  0.6 1.4 copy-start
  0.6 1.5 copy-start.9
  2.1 23.3 %copy-start.1 = (bf16[1,2,96,4,512]{4,2,3,1,0:T(8,128)(2,1)}, bf16[1,2,96,4,512]{4,2,3,1,0:T(8,128)(2,1)S(1)}, u32[]{:S(2)}) copy-start(bf16[1,2,96,4,512]{4,2,3,1,0:T(8,128)(2,1)S(1)} %copy.157) | copy-start | bytes 2359300
  2.7 14.4 %copy-start.20 = (s32[1,2]{1,0:T(1,128)S(1)}, s32[1,2]{1,0:T(1,128)}, u32[]{:S(2)}) copy-start(s32[1,2]{1,0:T(1,128)} %param.9) | copy-start | bytes 28
  2.8 22.6 %collective-permute-start = (bf16[2,96,4,512]{3,1,2,0:T(8,128)(2,1)S(1)}, bf16[2,96,4,512]{3,1,2,0:T(8,128)(2,1)S(1)}, u32[]{:S(2)}, u32[]{:S(2)}) collective-permute-start(bf16[2,96,4,512]{3,1,2,0:T(8,128)(2,1)S(1)} %bitcast.128), channel_id=1, source_target_pairs={{64,0},{128,64},{192,128},{256,192},{320,256},{384,320},{448,384},... | collective-permute-start | bytes 2359304 | tf_op jit(solution)/shard_map/ppermute | solution.py:21
  5.4 18.4 %copy-start.19 = (f32[1,2,2,96]{3,2,1,0:T(2,128)S(1)}, f32[1,2,2,96]{3,2,1,0:T(2,128)}, u32[]{:S(2)}) copy-start(f32[1,2,2,96]{3,2,1,0:T(2,128)} %param.11) | copy-start | bytes 4612
  5.4 40.3 %all-to-all-start = ((f32[2,96,4,256]{1,2,0,3:T(4,128)}), f32[2,96,4,256]{1,2,0,3:T(4,128)S(1)}, u32[]{:S(2)}, u32[]{:S(2)}) async-start(f32[2,96,4,256]{1,2,0,3:T(4,128)} %copy.81), calls=%async_computation | async-start | bytes 2097152 | tf_op jit(solution)/shard_map/all_to_all | solution.py:165
  22.4 3.0 %copy-start.10 = (f32[512,256,1,1]{1,0,3,2:T(8,128)S(1)}, f32[512,256,1,1]{1,0,3,2:T(8,128)}, u32[]{:S(2)}) copy-start(f32[512,256,1,1]{1,0,3,2:T(8,128)} %constant.91) | copy-start | bytes 1572868
  25.3 20.6 %copy-start.3 = (bf16[2,96,4,512]{3,1,2,0:T(8,128)(2,1)}, bf16[2,96,4,512]{3,1,2,0:T(8,128)(2,1)S(1)}, u32[]{:S(2)}) copy-start(bf16[2,96,4,512]{3,1,2,0:T(8,128)(2,1)S(1)} %collective-permute-done) | copy-start | bytes 2359300
  45.9 1.1 copy-start.4
  48.4 11.8 %copy-start.5 = (f32[1,128,2,256]{3,1,2,0:T(8,128)S(1)}, f32[1,128,2,256]{3,1,2,0:T(8,128)}, u32[]{:S(2)}) copy-start(f32[1,128,2,256]{3,1,2,0:T(8,128)} %get-tuple-element.47) | copy-start | bytes 786436
  48.4 11.8 %copy-start.7 = (f32[1,128,2,256]{3,1,2,0:T(8,128)S(1)}, f32[1,128,2,256]{3,1,2,0:T(8,128)}, u32[]{:S(2)}) copy-start(f32[1,128,2,256]{3,1,2,0:T(8,128)} %get-tuple-element.48) | copy-start | bytes 786436
  48.4 34.9 %all-to-all-start.1 = ((f32[2,96,4,256]{1,2,0,3:T(4,128)}), f32[2,96,4,256]{1,2,0,3:T(4,128)S(1)}, u32[]{:S(2)}, u32[]{:S(2)}) async-start(f32[2,96,4,256]{1,2,0,3:T(4,128)} %copy.84), calls=%async_computation.1 | async-start | bytes 2097152 | tf_op jit(solution)/shard_map/all_to_all | solution.py:165
  62.0 1.7 %copy-start.11 = (f32[2,96,96]{2,1,0:T(8,128)S(1)}, f32[2,96,96]{2,1,0:T(8,128)}, u32[]{:S(2)}) copy-start(f32[2,96,96]{2,1,0:T(8,128)} %get-tuple-element.45) | copy-start | bytes 221188
  62.0 1.7 %copy-start.12 = (f32[2,96,96]{2,1,0:T(8,128)S(1)}, f32[2,96,96]{2,1,0:T(8,128)}, u32[]{:S(2)}) copy-start(f32[2,96,96]{2,1,0:T(8,128)} %get-tuple-element.46) | copy-start | bytes 221188
  83.5 1.0 copy-start.6
  83.5 1.0 copy-start.8
  85.6 1.3 copy-start.16
  85.6 1.3 copy-start.17
  85.6 1.3 copy-start.18
  90.4 1.0 copy-start.13
  90.4 1.0 copy-start.14
  90.4 1.0 copy-start.15
  135.6 19.7 %all-to-all-start.3 = ((f32[64,1,1164]{2,1,0:T(1,128)}), f32[64,1,1164]{2,1,0:T(1,128)S(1)}, u32[]{:S(2)}, u32[]{:S(2)}) async-start(f32[64,1,1164]{2,1,0:T(1,128)} %broadcast_in_dim.15), calls=%async_computation.3 | async-start | bytes 655360 | tf_op jit(solution)/shard_map/all_to_all | solution.py:223
  144.9 1.7 %copy-start.2 = (bf16[1,2,96,4,512]{4,2,3,1,0:T(8,128)(2,1)S(1)}, bf16[1,2,96,4,512]{4,2,3,1,0:T(8,128)(2,1)}, u32[]{:S(2)}) copy-start(bf16[1,2,96,4,512]{4,2,3,1,0:T(8,128)(2,1)} %copy-done.1) | copy-start | bytes 2359300
